TPU v7x, 128 devices: a whole 4x4x4 slice. The times are simulated.
128 devices in a mesh: seq: 16 (over z, x), heads: 8 (over y, core).
Axes of the slice: x: 4, y: 4, z: 4, core: 2. Of those that a mesh axis runs over, the one named last changes fastest.
Arguments:
- audio: bfloat16 [4096, 1280], P('seq'), may hold values from -6 to 6
- ln_gain: float32 [1280], replicated, may hold values from 0.25 to 1.75
- ln_shift: float32 [1280], replicated, may hold values from -3 to 3
- enc_wq: bfloat16 [1280, 1024], P(None, 'heads'), may hold values from -0.15625 to 0.15625
- enc_bq: float32 [1024], P('heads'), may hold values from -3 to 3
- enc_wk: bfloat16 [1280, 1024], P(None, 'heads'), may hold values from -4 to 4
- enc_wv: bfloat16 [1280, 1024], P(None, 'heads'), may hold values from -0.15625 to 0.15625
- enc_bv: float32 [1024], P('heads'), may hold values from -3 to 3
- enc_wo: bfloat16 [1024, 1280], P('heads'), may hold values from -0.1875 to 0.1875
- enc_bo: float32 [1280], replicated, may hold values from -3 to 3
- windows: int32 [16], P('heads'), may hold values from 1 to 128, as said below
- dec_wkv: bfloat16 [1280, 8, 256], replicated, may hold values from -4 to 4
- dec_bv: float32 [8, 128], replicated, may hold values from -3 to 3
- text: bfloat16 [8192, 8192], P('seq'), may hold values from -6 to 6
- norm_gain: float32 [8192], replicated, may hold values from 0.25 to 1.75
- dec_wq: bfloat16 [8192, 4096], P('seq', 'heads'), may hold values from -0.0625 to 0.0625
- dec_bq: float32 [4096], P('heads'), may hold values from -3 to 3
- dec_wo: bfloat16 [4096, 8192], P('heads', 'seq'), may hold values from -0.125 to 0.125
- span_start: int32 [8192], P('seq'), may hold values from 0 to 3840, as said below
- span_len: int32 [8192], P('seq'), may hold values from 1 to 256, as said below
Outputs:
- enc_out: bfloat16 [4096, 1280], P(('seq', 'heads'))
- dec_out: bfloat16 [8192, 8192], P('seq', 'heads')
Inputs may be any that keep to these rules, and one draw needn't show every extreme that they name: `windows`: every head's window is 1 to 128; some head has exactly 128 and some head exactly 1. `span_start`: row r's band begins between r * 256 // 512 - 255 and r * 256 // 512, and never before frame 0 or after 4096 - 256; row 0 begins at 0 and the last row at 3840; the last row of every aligned block of 512 rows but the final one begins exactly at r * 256 // 512. `span_len`: row 0 has 256 valid frames and row 1 has one; the last row of every aligned block of 512 rows has 256, unless it is row 1.
All inputs are finite; a program needn't handle non-finite values.
Results may differ from a plain program's by a relative error of at most 0.025.
Values may be sent and summed in bfloat16 or wider, within the bound.
No kernel may reach another device: no remote copies, remote signals or barrier semaphores. Data moves between devices by JAX's collectives and lax.ppermute only.
A program may use at most 128 MiB of HBM per device.

v0:
```python
import jax
import jax.numpy as jnp
from jax import lax
from jax.sharding import PartitionSpec as P

EWIN = 128
BAND = 256


def with_halo(block, sides, width):
    for axis, dim in sides:
        count = lax.axis_size(axis)
        forward = [(i, i + 1) for i in range(count - 1)]
        backward = [(target, source) for source, target in forward]
        low = lax.ppermute(
            lax.slice_in_dim(block, block.shape[dim] - width, None, axis=dim), axis, forward
        )
        high = lax.ppermute(lax.slice_in_dim(block, 0, width, axis=dim), axis, backward)
        block = jnp.concatenate([low, block, high], axis=dim)
    return block


def layer_norm(values, gain, shift):
    values = values.astype(jnp.float32)
    centre = values - jnp.mean(values, axis=-1, keepdims=True)
    spread = jnp.mean(centre * centre, axis=-1, keepdims=True)
    return centre * lax.rsqrt(spread + 1e-05) * gain + shift


def rms_norm(values, gain):
    values = values.astype(jnp.float32)
    return values * lax.rsqrt(jnp.mean(values * values, axis=-1, keepdims=True) + 1e-06) * gain


def masked_softmax(scores, valid):
    highest = jnp.max(jnp.where(valid, scores, -jnp.inf), axis=-1, keepdims=True)
    raised = jnp.where(valid, jnp.exp(scores - highest), jnp.zeros_like(scores))
    return (raised / jnp.sum(raised, axis=-1, keepdims=True)).astype(jnp.bfloat16)


def shards(
    audio,
    ln_gain,
    ln_shift,
    enc_wq,
    enc_bq,
    enc_wk,
    enc_wv,
    enc_bv,
    enc_wo,
    enc_bo,
    windows,
    dec_wkv,
    dec_bv,
    text,
    norm_gain,
    dec_wq,
    dec_bq,
    dec_wo,
    span_start,
    span_len,
):
    seq_count = lax.axis_size("seq")
    head_count = lax.axis_size("heads")
    seq_index = lax.axis_index("seq")
    head_index = lax.axis_index("heads")
    frames_dev = audio.shape[0]
    enc_width = audio.shape[1]
    heads_dev = windows.shape[0]
    head_size = enc_wq.shape[1] // heads_dev
    all_frames = frames_dev * seq_count
    hidden = layer_norm(audio, ln_gain, ln_shift).astype(jnp.bfloat16)
    enc_query = (jnp.dot(hidden, enc_wq, preferred_element_type=jnp.float32) + enc_bq).astype(
        jnp.bfloat16
    )
    enc_keys = jnp.dot(hidden, enc_wk, preferred_element_type=jnp.float32).astype(jnp.bfloat16)
    enc_values = (jnp.dot(hidden, enc_wv, preferred_element_type=jnp.float32) + enc_bv).astype(
        jnp.bfloat16
    )
    enc_pairs = jnp.stack([enc_keys, enc_values], axis=1)
    widened = with_halo(enc_pairs, (("seq", 0),), EWIN)
    extent = frames_dev + 2 * EWIN
    key_block = widened[:, 0, :].reshape(extent, heads_dev, head_size)
    value_block = widened[:, 1, :].reshape(extent, heads_dev, head_size)
    query_block = enc_query.reshape(frames_dev, heads_dev, head_size)
    scores = jnp.einsum(
        "qhd,khd->hqk", query_block, key_block, preferred_element_type=jnp.float32
    ) * head_size ** (-0.5)
    row_frames = seq_index * frames_dev + jnp.arange(frames_dev, dtype=jnp.int32)
    col_frames = seq_index * frames_dev - EWIN + jnp.arange(extent, dtype=jnp.int32)
    distance = jnp.abs(row_frames[:, None] - col_frames[None, :])
    inside = (col_frames >= 0) & (col_frames < all_frames)
    valid = (distance[None, :, :] <= windows[:, None, None]) & inside[None, None, :]
    enc_weights = masked_softmax(scores, valid)
    enc_context = jnp.einsum(
        "hqk,khd->qhd", enc_weights, value_block, preferred_element_type=jnp.float32
    )
    enc_context = enc_context.astype(jnp.bfloat16).reshape(frames_dev, heads_dev * head_size)
    enc_term = jnp.dot(enc_context, enc_wo, preferred_element_type=jnp.float32)
    mixed = lax.psum_scatter(
        enc_term.astype(jnp.bfloat16), "heads", scatter_dimension=0, tiled=True
    ).astype(jnp.float32)
    share = frames_dev // head_count
    own_audio = lax.dynamic_slice_in_dim(audio, head_index * share, share, 0)
    enc_out = (own_audio.astype(jnp.float32) + mixed + enc_bo).astype(jnp.bfloat16)
    groups_dev = dec_wkv.shape[1] // head_count
    pair_width = dec_wkv.shape[2]
    dec_head = pair_width // 2
    band_bias = jnp.concatenate([jnp.zeros_like(dec_bv), dec_bv], axis=1)
    frames_all = lax.all_gather(enc_out, "heads", axis=0, tiled=True)
    weight_group = lax.dynamic_slice_in_dim(
        dec_wkv, head_index * groups_dev, groups_dev, 1
    ).reshape(enc_width, groups_dev * pair_width)
    bias_group = lax.dynamic_slice_in_dim(
        band_bias, head_index * groups_dev, groups_dev, 0
    ).reshape(groups_dev * pair_width)
    band_pairs = (
        jnp.dot(frames_all, weight_group, preferred_element_type=jnp.float32) + bias_group
    ).astype(jnp.bfloat16)
    band_pairs = band_pairs.reshape(frames_dev, groups_dev, pair_width)
    band_wide = with_halo(band_pairs, (("seq", 0),), BAND)
    rows_dev = text.shape[0]
    model_width = text.shape[1]
    query_width = dec_wq.shape[1]
    query_heads = query_width // (groups_dev * dec_head)
    normed = rms_norm(text, norm_gain).astype(jnp.bfloat16)
    query_sum = jnp.dot(
        normed,
        lax.all_gather(dec_wq, "seq", axis=0, tiled=True),
        preferred_element_type=jnp.float32,
    )
    dec_query = (
        (query_sum + dec_bq)
        .astype(jnp.bfloat16)
        .reshape(rows_dev, groups_dev, query_heads, dec_head)
    )
    band_extent = band_wide.shape[0]
    band_keys = band_wide[:, :, :dec_head]
    band_values = band_wide[:, :, dec_head:]
    dec_scores = jnp.einsum(
        "rgqd,kgd->rgqk", dec_query, band_keys, preferred_element_type=jnp.float32
    ) * dec_head ** (-0.5)
    band_frames = seq_index * frames_dev - BAND + jnp.arange(band_extent, dtype=jnp.int32)
    in_band = (band_frames[None, :] >= span_start[:, None]) & (
        band_frames[None, :] < (span_start + span_len)[:, None]
    )
    dec_weights = masked_softmax(dec_scores, in_band[:, None, None, :])
    dec_context = jnp.einsum(
        "rgqk,kgd->rgqd", dec_weights, band_values, preferred_element_type=jnp.float32
    )
    dec_context = dec_context.astype(jnp.bfloat16).reshape(rows_dev, query_width)
    dec_term = jnp.dot(
        dec_context,
        lax.all_gather(dec_wo, "seq", axis=1, tiled=True),
        preferred_element_type=jnp.float32,
    )
    summed = lax.psum_scatter(
        dec_term.astype(jnp.bfloat16), "heads", scatter_dimension=1, tiled=True
    ).astype(jnp.float32)
    col_share = model_width // head_count
    own_text = lax.dynamic_slice_in_dim(text, head_index * col_share, col_share, 1)
    dec_out = (own_text.astype(jnp.float32) + summed).astype(jnp.bfloat16)
    return (enc_out, dec_out)


def solution(mesh):
    return jax.shard_map(
        shards,
        mesh=mesh,
        in_specs=(
            P("seq", None),
            P(),
            P(),
            P(None, "heads"),
            P("heads"),
            P(None, "heads"),
            P(None, "heads"),
            P("heads"),
            P("heads", None),
            P(),
            P("heads"),
            P(),
            P(),
            P("seq", None),
            P(),
            P("seq", "heads"),
            P("heads"),
            P("heads", "seq"),
            P("seq"),
            P("seq"),
        ),
        out_specs=(P(("seq", "heads"), None), P("seq", "heads")),
        check_vma=False,
    )
```

profile of v0, /device:TPU:96, one launch (start us, length us, event | category | flops | bytes accessed | tf_op | source)
XLA Modules:
  0.0 258.5 jit_solution(15080871466820976474)
XLA Ops:
  8.1 1.3 convert_reduce_fusion
  9.4 1.4 fusion.24
  10.8 1.4 fusion.27
  12.2 1.3 fusion.41
  13.5 1.3 fusion.42
  14.8 3.4 %collective-permute-start = (bf16[128,2,128]{2,0,1:T(8,128)(2,1)S(1)}, bf16[128,2,128]{2,0,1:T(8,128)(2,1)S(1)}, u32[]{:S(2)}, u32[]{:S(2)}) collective-permute-start(bf16[128,2,128]{2,0,1:T(8,128)(2,1)S(1)} %get-tuple-element.4), channel_id=1, source_target_pairs={{0,8},{8,16},{16,24},{24,32},{32,40},{40,48},{48,56},{56,64},{64,7... | collective-permute-start | bytes 196616 | tf_op jit(solution)/shard_map/ppermute | solution.py:15
  18.2 4.6 %collective-permute-start.1 = (bf16[128,2,128]{2,0,1:T(8,128)(2,1)S(1)}, bf16[128,2,128]{2,0,1:T(8,128)(2,1)S(1)}, u32[]{:S(2)}, u32[]{:S(2)}) collective-permute-start(bf16[128,2,128]{2,0,1:T(8,128)(2,1)S(1)} %get-tuple-element.5), channel_id=1, source_target_pairs={{8,0},{16,8},{24,16},{32,24},{40,32},{48,40},{56,48},{64,56},{72,6... | collective-permute-start | bytes 196616 | tf_op jit(solution)/shard_map/ppermute | solution.py:18
  23.0 1.4 fusion.40
  25.4 0.7 fusion.60
  26.0 1.2 convolution_convert_fusion.2
  27.2 1.2 convolution_convert_fusion.1
  28.5 0.5 all-gather.3.cloned.1.call-update
  29.1 0.5 all-gather.5.cloned.1.call-update
  29.8 3.2 %constant_dynamic-slice_fusion = bf16[1280,1,256]{2,1,0:T(2,128)(2,1)S(1)} fusion(bf16[1280,8,256]{2,1,0:T(8,128)(2,1)} %param.31, s32[]{:T(128)S(6)} %select_n.30), kind=kLoop, calls=%fused_computation.75 | loop fusion | bytes 1310724 | tf_op jit(solution)/shard_map/dynamic_slice | solution.py:111
  33.0 0.4 compare_and_fusion
  33.4 5.1 %fusion.1 = f32[512]{0:T(512)S(1)} fusion(bf16[512,8192]{1,0:T(8,128)(2,1)} %param.33), kind=kLoop, calls=%fused_computation.3 | loop fusion | flops 12582400 | bytes 8390656 | tf_op jit(solution)/shard_map/reduce_sum | solution.py:32
  38.5 25.3 %reduce-scatter.3.cloned.1.call-done = bf16[32,1280]{1,0:T(8,128)(2,1)} async-done(((bf16[256,1280]{1,0:T(8,128)(2,1)}), bf16[32,1280]{1,0:T(8,128)(2,1)}) %reduce-scatter.3.cloned.1.call-update) | async-done | bytes 81936 | tf_op jit(solution)/shard_map/reduce_scatter | solution.py:100
  63.8 1.0 add_convert_fusion.1
  64.8 13.2 %all_gather.9 = bf16[256,1280]{1,0:T(8,128)(2,1)S(1)} all-gather(bf16[32,1280]{1,0:T(8,128)(2,1)S(1)} %add_convert_fusion.1), channel_id=1, replica_groups=mesh['seq'=16,'heads'=8] {'heads'}, dimensions={0}, use_global_device_ids=true | all-gather | bytes 737280 | tf_op jit(solution)/shard_map/all_gather | solution.py:110
  78.4 4.4 %collective-permute-start.3 = (bf16[256,1,256]{2,0,1:T(8,128)(2,1)S(1)}, bf16[256,1,256]{2,0,1:T(8,128)(2,1)S(1)}, u32[]{:S(2)}, u32[]{:S(2)}) collective-permute-start(bf16[256,1,256]{2,0,1:T(8,128)(2,1)S(1)} %fusion.38), channel_id=1, source_target_pairs={{8,0},{16,8},{24,16},{32,24},{40,32},{48,40},{56,48},{64,56},{72,6... | collective-permute-start | bytes 393224 | tf_op jit(solution)/shard_map/ppermute | solution.py:18
  82.8 2.1 collective-permute-start.2
  85.0 4.4 %collective-permute-done.3 = bf16[256,1,256]{2,0,1:T(8,128)(2,1)S(1)} collective-permute-done((bf16[256,1,256]{2,0,1:T(8,128)(2,1)S(1)}, bf16[256,1,256]{2,0,1:T(8,128)(2,1)S(1)}, u32[]{:S(2)}, u32[]{:S(2)}) %collective-permute-start.3) | collective-permute-done | bytes 131104 | tf_op jit(solution)/shard_map/ppermute | solution.py:18
  89.3 6.4 %collective-permute-done.2 = bf16[256,1,256]{2,0,1:T(8,128)(2,1)S(1)} collective-permute-done((bf16[256,1,256]{2,0,1:T(8,128)(2,1)S(1)}, bf16[256,1,256]{2,0,1:T(8,128)(2,1)S(1)}, u32[]{:S(2)}, u32[]{:S(2)}) %collective-permute-start.2) | collective-permute-done | bytes 131104 | tf_op jit(solution)/shard_map/ppermute | solution.py:15
  95.8 10.3 %all-gather.3.cloned.1.call-done = bf16[8192,512]{1,0:T(8,128)(2,1)} async-done(((bf16[512,512]{1,0:T(8,128)(2,1)}), bf16[8192,512]{1,0:T(8,128)(2,1)}) %all-gather.3.cloned.1.call-update) | async-done | bytes 8388624 | tf_op jit(solution)/shard_map/all_gather | solution.py:129
  106.1 10.4 %fusion.34 = bf16[512,512]{0,1:T(8,128)(2,1)S(1)} fusion(bf16[8192,512]{1,0:T(8,128)(2,1)} %all-gather.3.cloned.1.call-done, bf16[512,8192]{1,0:T(8,128)(2,1)} %param.33, f32[8192]{0:T(1024)S(1)} %copy-done.6, f32[512]{0:T(512)S(1)} %add_rsqrt_fusion, f32[512]{0:T(512)S(1)} %copy-done.7), kind=kOutput, calls=%fused_computation.38 | convolution fusion | flops 4312268800 | bytes 17338368 | tf_op jit(solution)/shard_map/dot_general | solution.py:127
  116.5 1.2 fusion.8
  117.7 1.4 fusion.11
  119.0 2.1 fusion.31
  121.1 64.5 %all-gather.5.cloned.1.call-done = bf16[512,8192]{1,0:T(8,128)(2,1)} async-done(((bf16[512,512]{1,0:T(8,128)(2,1)}), bf16[512,8192]{1,0:T(8,128)(2,1)}) %all-gather.5.cloned.1.call-update) | async-done | bytes 8388624 | tf_op jit(solution)/shard_map/all_gather | solution.py:154
  185.6 10.1 %convolution_convert_fusion = bf16[512,8192]{1,0:T(8,128)(2,1)} fusion(bf16[512,512]{0,1:T(8,128)(2,1)S(1)} %bitcast.74, bf16[512,8192]{1,0:T(8,128)(2,1)} %all-gather.5.cloned.1.call-done), kind=kOutput, calls=%fused_computation.6 | convolution fusion | flops 4299161600 | bytes 17301504 | tf_op jit(solution)/shard_map/dot_general | solution.py:152
  195.7 52.4 %reduce-scatter.5.cloned.1.call-done = bf16[512,1024]{1,0:T(8,128)(2,1)} async-done(((bf16[512,8192]{1,0:T(8,128)(2,1)}), bf16[512,1024]{1,0:T(8,128)(2,1)}) %reduce-scatter.5.cloned.1.call-update) | async-done | bytes 1048592 | tf_op jit(solution)/shard_map/reduce_scatter | solution.py:157
  248.2 2.9 %add_convert_fusion = bf16[512,1024]{1,0:T(8,128)(2,1)} fusion(bf16[512,1024]{1,0:T(8,128)(2,1)} %reduce-scatter.5.cloned.1.call-done, bf16[512,8192]{1,0:T(8,128)(2,1)} %param.33, s32[]{:T(128)S(6)} %select_n.29), kind=kLoop, calls=%fused_computation.20 | loop fusion | flops 2097152 | bytes 3145732 | tf_op jit(solution)/shard_map/convert_element_type | solution.py:162
  (44 shorter events, 1.8 us)
Async XLA Ops:
  8.0 19.2 %copy-start = (bf16[128,1280]{1,0:T(8,128)(2,1)S(1)}, bf16[128,1280]{1,0:T(8,128)(2,1)}, u32[]{:S(2)}) copy-start(bf16[128,1280]{1,0:T(8,128)(2,1)} %param.28) | copy-start | bytes 983044
  8.0 17.3 %copy-start.8 = (s32[2]{0:T(128)S(1)}, s32[2]{0:T(128)}, u32[]{:S(2)}) copy-start(s32[2]{0:T(128)} %param.30) | copy-start | bytes 28
  8.0 55.8 %reduce-scatter.3.cloned.1.call-start = ((), (), s32[]{:S(2)}) async-start(), calls=%async_computation.2 | async-start | bytes 737280 | tf_op jit(solution)/shard_map/reduce_scatter | solution.py:100
  14.8 9.5 %collective-permute-start = (bf16[128,2,128]{2,0,1:T(8,128)(2,1)S(1)}, bf16[128,2,128]{2,0,1:T(8,128)(2,1)S(1)}, u32[]{:S(2)}, u32[]{:S(2)}) collective-permute-start(bf16[128,2,128]{2,0,1:T(8,128)(2,1)S(1)} %get-tuple-element.4), channel_id=1, source_target_pairs={{0,8},{8,16},{16,24},{24,32},{32,40},{40,48},{48,56},{56,64},{64,7... | collective-permute-start | bytes 196616 | tf_op jit(solution)/shard_map/ppermute | solution.py:15
  18.2 6.4 %collective-permute-start.1 = (bf16[128,2,128]{2,0,1:T(8,128)(2,1)S(1)}, bf16[128,2,128]{2,0,1:T(8,128)(2,1)S(1)}, u32[]{:S(2)}, u32[]{:S(2)}) collective-permute-start(bf16[128,2,128]{2,0,1:T(8,128)(2,1)S(1)} %get-tuple-element.5), channel_id=1, source_target_pairs={{8,0},{16,8},{24,16},{32,24},{40,32},{48,40},{56,48},{64,56},{72,6... | collective-permute-start | bytes 196616 | tf_op jit(solution)/shard_map/ppermute | solution.py:18
  24.9 4.8 %copy-start.2 = (s32[512]{0:T(512)S(1)}, s32[512]{0:T(512)}, u32[]{:S(2)}) copy-start(s32[512]{0:T(512)} %param.38) | copy-start | bytes 6148
  24.9 4.8 %copy-start.5 = (s32[512]{0:T(512)S(1)}, s32[512]{0:T(512)}, u32[]{:S(2)}) copy-start(s32[512]{0:T(512)} %param.39) | copy-start | bytes 6148
  24.9 4.8 %copy-start.4 = (f32[8,128]{1,0:T(8,128)S(1)}, f32[8,128]{1,0:T(8,128)}, u32[]{:S(2)}) copy-start(f32[8,128]{1,0:T(8,128)} %param.32) | copy-start | bytes 12292
  28.5 35.4 %copy-start.3 = (f32[1280]{0:T(1024)S(1)}, f32[1280]{0:T(1024)}, u32[]{:S(2)}) copy-start(f32[1280]{0:T(1024)} %param.29) | copy-start | bytes 15364
  28.5 77.6 %all-gather.3.cloned.1.call-start = ((), (), s32[]{:S(2)}) async-start(), calls=%async_computation.3 | async-start | bytes 8912896 | tf_op jit(solution)/shard_map/all_gather | solution.py:129
  29.0 156.6 %all-gather.5.cloned.1.call-start = ((), (), s32[]{:S(2)}) async-start(), calls=%async_computation.4 | async-start | bytes 8912896 | tf_op jit(solution)/shard_map/all_gather | solution.py:154
  29.6 218.5 %reduce-scatter.5.cloned.1.call-start = ((), (), s32[]{:S(2)}) async-start(), calls=%async_computation.5 | async-start | bytes 9437184 | tf_op jit(solution)/shard_map/reduce_scatter | solution.py:157
  33.0 73.1 %copy-start.6 = (f32[8192]{0:T(1024)S(1)}, f32[8192]{0:T(1024)}, u32[]{:S(2)}) copy-start(f32[8192]{0:T(1024)} %param.34) | copy-start | bytes 98308
  33.0 73.1 %copy-start.7 = (f32[512]{0:T(512)S(1)}, f32[512]{0:T(512)}, u32[]{:S(2)}) copy-start(f32[512]{0:T(512)} %param.36) | copy-start | bytes 6148
  64.8 51.7 %copy-start.1 = (bf16[32,1280]{1,0:T(8,128)(2,1)}, bf16[32,1280]{1,0:T(8,128)(2,1)S(1)}, u32[]{:S(2)}) copy-start(bf16[32,1280]{1,0:T(8,128)(2,1)S(1)} %add_convert_fusion.1) | copy-start | bytes 245764
  78.4 11.0 %collective-permute-start.3 = (bf16[256,1,256]{2,0,1:T(8,128)(2,1)S(1)}, bf16[256,1,256]{2,0,1:T(8,128)(2,1)S(1)}, u32[]{:S(2)}, u32[]{:S(2)}) collective-permute-start(bf16[256,1,256]{2,0,1:T(8,128)(2,1)S(1)} %fusion.38), channel_id=1, source_target_pairs={{8,0},{16,8},{24,16},{32,24},{40,32},{48,40},{56,48},{64,56},{72,6... | collective-permute-start | bytes 393224 | tf_op jit(solution)/shard_map/ppermute | solution.py:18
  82.8 12.9 %collective-permute-start.2 = (bf16[256,1,256]{2,0,1:T(8,128)(2,1)S(1)}, bf16[256,1,256]{2,0,1:T(8,128)(2,1)S(1)}, u32[]{:S(2)}, u32[]{:S(2)}) collective-permute-start(bf16[256,1,256]{2,0,1:T(8,128)(2,1)S(1)} %fusion.38), channel_id=1, source_target_pairs={{0,8},{8,16},{16,24},{24,32},{32,40},{40,48},{48,56},{56,64},{64,7... | collective-permute-start | bytes 393224 | tf_op jit(solution)/shard_map/ppermute | solution.py:15
Sparse Core Ops, SparseCore 0:
  28.6 35.2 reduce-scatter.2
  195.9 52.2 reduce-scatter.4
Sparse Core Ops, SparseCore 1:
  31.1 75.0 all-gather.2
  108.1 77.5 all-gather.4
where the time goes:
time: 260 us; the launch traced here: 259 us
  waiting for transfers between devices  165 us (63%)
  matrix products  30.7 us (12%)
  between operations  15.9 us (6%)
  other arithmetic  15.7 us (6%)
  starting transfers between devices  14.7 us (6%)
  blocking collectives  13.2 us (5%)
  local copies, waits for them, and re-layouts  3.56 us (1%)
    all_gather x1, waiting for transfers between devices, shards(): lax.all_gather(dec_wo, 'seq', axis=1, tiled=True)  64.5 us
    reduce_scatter x1, waiting for transfers between devices, shards(): lax.psum_scatter(dec_term.astype(jnp.bfloat16), 'heads', scatter_dimensio...  52.4 us
    reduce_scatter x1, waiting for transfers between devices, shards(): lax.psum_scatter(enc_term.astype(jnp.bfloat16), 'heads', scatter_dimensio...  25.3 us
    all_gather x1, blocking collectives, shards(): frames_all = lax.all_gather(enc_out, 'heads', axis=0, tiled=True)  13.2 us
    dot_general x1, matrix products, shards(): jnp.dot(normed, lax.all_gather(dec_wq, 'seq', axis=0, tiled=True), prefer...  10.4 us
    all_gather x1, waiting for transfers between devices, shards(): lax.all_gather(dec_wq, 'seq', axis=0, tiled=True)  10.3 us
    dot_general x1, matrix products, shards(): jnp.dot(dec_context, lax.all_gather(dec_wo, 'seq', axis=1, tiled=True), p...  10.1 us
    ppermute x2, starting transfers between devices, with_halo(): lax.ppermute(lax.slice_in_dim(block, 0, width, axis=dim), axis, backward)  9 us
  transfers between devices with their start and end apart: 8, of which 7 were waited for; matrix products, arithmetic and copies ran while one was open for 10% of the time, Pallas kernels for 0%

commit v1 on v0

--- a/solution.py
+++ b/solution.py
@@ -38,7 +38,7 @@
     return (raised / jnp.sum(raised, axis=-1, keepdims=True)).astype(jnp.bfloat16)
 
 
-def shards(
+def layer_body(
     audio,
     ln_gain,
     ln_shift,
@@ -69,6 +69,8 @@
     heads_dev = windows.shape[0]
     head_size = enc_wq.shape[1] // heads_dev
     all_frames = frames_dev * seq_count
+    query_weight = lax.all_gather(dec_wq, "seq", axis=0, tiled=True)
+    output_weight = lax.all_gather(dec_wo, "seq", axis=1, tiled=True)
     hidden = layer_norm(audio, ln_gain, ln_shift).astype(jnp.bfloat16)
     enc_query = (jnp.dot(hidden, enc_wq, preferred_element_type=jnp.float32) + enc_bq).astype(
         jnp.bfloat16
@@ -126,7 +128,7 @@
     normed = rms_norm(text, norm_gain).astype(jnp.bfloat16)
     query_sum = jnp.dot(
         normed,
-        lax.all_gather(dec_wq, "seq", axis=0, tiled=True),
+        query_weight,
         preferred_element_type=jnp.float32,
     )
     dec_query = (
@@ -151,7 +153,7 @@
     dec_context = dec_context.astype(jnp.bfloat16).reshape(rows_dev, query_width)
     dec_term = jnp.dot(
         dec_context,
-        lax.all_gather(dec_wo, "seq", axis=1, tiled=True),
+        output_weight,
         preferred_element_type=jnp.float32,
     )
     summed = lax.psum_scatter(
@@ -165,7 +167,7 @@
 
 def solution(mesh):
     return jax.shard_map(
-        shards,
+        layer_body,
         mesh=mesh,
         in_specs=(
             P("seq", None),

time: 260 us -> 260 us (level)
  no operation moved by 1% of the time
where the time goes in v1:
time: 260 us; the launch traced here: 259 us
  waiting for transfers between devices  165 us (63%)
  matrix products  30.7 us (12%)
  between operations  15.9 us (6%)
  other arithmetic  15.7 us (6%)
  starting transfers between devices  14.7 us (6%)
  blocking collectives  13.2 us (5%)
  local copies, waits for them, and re-layouts  3.56 us (1%)
    all_gather x1, waiting for transfers between devices, layer_body(): output_weight = lax.all_gather(dec_wo, 'seq', axis=1, tiled=True)  64.5 us
    reduce_scatter x1, waiting for transfers between devices, layer_body(): lax.psum_scatter(dec_term.astype(jnp.bfloat16), 'heads', scatter_dimensio...  52.4 us
    reduce_scatter x1, waiting for transfers between devices, layer_body(): lax.psum_scatter(enc_term.astype(jnp.bfloat16), 'heads', scatter_dimensio...  25.3 us
    all_gather x1, blocking collectives, layer_body(): frames_all = lax.all_gather(enc_out, 'heads', axis=0, tiled=True)  13.2 us
    dot_general x1, matrix products, layer_body(): jnp.dot(normed, query_weight, preferred_element_type=jnp.float32)  10.4 us
    all_gather x1, waiting for transfers between devices, layer_body(): query_weight = lax.all_gather(dec_wq, 'seq', axis=0, tiled=True)  10.3 us
    dot_general x1, matrix products, layer_body(): jnp.dot(dec_context, output_weight, preferred_element_type=jnp.float32)  10.1 us
    ppermute x2, starting transfers between devices, with_halo(): lax.ppermute(lax.slice_in_dim(block, 0, width, axis=dim), axis, backward)  9 us
  transfers between devices with their start and end apart: 8, of which 7 were waited for; matrix products, arithmetic and copies ran while one was open for 10% of the time, Pallas kernels for 0%

profile of v1, /device:TPU:96, one launch (start us, length us, event | category | flops | bytes accessed | tf_op | source)
XLA Modules:
  0.0 258.5 jit_solution(15080871466820976474)
XLA Ops:
  8.1 1.3 convert_reduce_fusion
  9.4 1.4 fusion.24
  10.8 1.4 fusion.27
  12.2 1.3 fusion.41
  13.5 1.3 fusion.42
  14.8 3.4 %collective-permute-start = (bf16[128,2,128]{2,0,1:T(8,128)(2,1)S(1)}, bf16[128,2,128]{2,0,1:T(8,128)(2,1)S(1)}, u32[]{:S(2)}, u32[]{:S(2)}) collective-permute-start(bf16[128,2,128]{2,0,1:T(8,128)(2,1)S(1)} %get-tuple-element.4), channel_id=1, source_target_pairs={{0,8},{8,16},{16,24},{24,32},{32,40},{40,48},{48,56},{56,64},{64,7... | collective-permute-start | bytes 196616 | tf_op jit(solution)/shard_map/ppermute | solution.py:15
  18.2 4.6 %collective-permute-start.1 = (bf16[128,2,128]{2,0,1:T(8,128)(2,1)S(1)}, bf16[128,2,128]{2,0,1:T(8,128)(2,1)S(1)}, u32[]{:S(2)}, u32[]{:S(2)}) collective-permute-start(bf16[128,2,128]{2,0,1:T(8,128)(2,1)S(1)} %get-tuple-element.5), channel_id=1, source_target_pairs={{8,0},{16,8},{24,16},{32,24},{40,32},{48,40},{56,48},{64,56},{72,6... | collective-permute-start | bytes 196616 | tf_op jit(solution)/shard_map/ppermute | solution.py:18
  23.0 1.4 fusion.40
  25.4 0.7 fusion.60
  26.0 1.2 convolution_convert_fusion.2
  27.2 1.2 convolution_convert_fusion.1
  28.5 0.5 all-gather.3.cloned.1.call-update
  29.1 0.5 all-gather.5.cloned.1.call-update
  29.8 3.2 %constant_dynamic-slice_fusion = bf16[1280,1,256]{2,1,0:T(2,128)(2,1)S(1)} fusion(bf16[1280,8,256]{2,1,0:T(8,128)(2,1)} %param.31, s32[]{:T(128)S(6)} %select_n.30), kind=kLoop, calls=%fused_computation.75 | loop fusion | bytes 1310724 | tf_op jit(solution)/shard_map/dynamic_slice | solution.py:113
  33.0 0.4 compare_and_fusion
  33.4 5.1 %fusion.1 = f32[512]{0:T(512)S(1)} fusion(bf16[512,8192]{1,0:T(8,128)(2,1)} %param.33), kind=kLoop, calls=%fused_computation.3 | loop fusion | flops 12582400 | bytes 8390656 | tf_op jit(solution)/shard_map/reduce_sum | solution.py:32
  38.5 25.3 %reduce-scatter.3.cloned.1.call-done = bf16[32,1280]{1,0:T(8,128)(2,1)} async-done(((bf16[256,1280]{1,0:T(8,128)(2,1)}), bf16[32,1280]{1,0:T(8,128)(2,1)}) %reduce-scatter.3.cloned.1.call-update) | async-done | bytes 81936 | tf_op jit(solution)/shard_map/reduce_scatter | solution.py:102
  63.8 1.0 add_convert_fusion.1
  64.8 13.2 %all_gather.9 = bf16[256,1280]{1,0:T(8,128)(2,1)S(1)} all-gather(bf16[32,1280]{1,0:T(8,128)(2,1)S(1)} %add_convert_fusion.1), channel_id=1, replica_groups=mesh['seq'=16,'heads'=8] {'heads'}, dimensions={0}, use_global_device_ids=true | all-gather | bytes 737280 | tf_op jit(solution)/shard_map/all_gather | solution.py:112
  78.4 4.4 %collective-permute-start.3 = (bf16[256,1,256]{2,0,1:T(8,128)(2,1)S(1)}, bf16[256,1,256]{2,0,1:T(8,128)(2,1)S(1)}, u32[]{:S(2)}, u32[]{:S(2)}) collective-permute-start(bf16[256,1,256]{2,0,1:T(8,128)(2,1)S(1)} %fusion.38), channel_id=1, source_target_pairs={{8,0},{16,8},{24,16},{32,24},{40,32},{48,40},{56,48},{64,56},{72,6... | collective-permute-start | bytes 393224 | tf_op jit(solution)/shard_map/ppermute | solution.py:18
  82.8 2.1 collective-permute-start.2
  85.0 4.4 %collective-permute-done.3 = bf16[256,1,256]{2,0,1:T(8,128)(2,1)S(1)} collective-permute-done((bf16[256,1,256]{2,0,1:T(8,128)(2,1)S(1)}, bf16[256,1,256]{2,0,1:T(8,128)(2,1)S(1)}, u32[]{:S(2)}, u32[]{:S(2)}) %collective-permute-start.3) | collective-permute-done | bytes 131104 | tf_op jit(solution)/shard_map/ppermute | solution.py:18
  89.3 6.4 %collective-permute-done.2 = bf16[256,1,256]{2,0,1:T(8,128)(2,1)S(1)} collective-permute-done((bf16[256,1,256]{2,0,1:T(8,128)(2,1)S(1)}, bf16[256,1,256]{2,0,1:T(8,128)(2,1)S(1)}, u32[]{:S(2)}, u32[]{:S(2)}) %collective-permute-start.2) | collective-permute-done | bytes 131104 | tf_op jit(solution)/shard_map/ppermute | solution.py:15
  95.8 10.3 %all-gather.3.cloned.1.call-done = bf16[8192,512]{1,0:T(8,128)(2,1)} async-done(((bf16[512,512]{1,0:T(8,128)(2,1)}), bf16[8192,512]{1,0:T(8,128)(2,1)}) %all-gather.3.cloned.1.call-update) | async-done | bytes 8388624 | tf_op jit(solution)/shard_map/all_gather | solution.py:72
  106.1 10.4 %fusion.34 = bf16[512,512]{0,1:T(8,128)(2,1)S(1)} fusion(bf16[8192,512]{1,0:T(8,128)(2,1)} %all-gather.3.cloned.1.call-done, bf16[512,8192]{1,0:T(8,128)(2,1)} %param.33, f32[8192]{0:T(1024)S(1)} %copy-done.6, f32[512]{0:T(512)S(1)} %add_rsqrt_fusion, f32[512]{0:T(512)S(1)} %copy-done.7), kind=kOutput, calls=%fused_computation.38 | convolution fusion | flops 4312268800 | bytes 17338368 | tf_op jit(solution)/shard_map/dot_general | solution.py:129
  116.5 1.2 fusion.8
  117.7 1.4 fusion.11
  119.0 2.1 fusion.31
  121.1 64.5 %all-gather.5.cloned.1.call-done = bf16[512,8192]{1,0:T(8,128)(2,1)} async-done(((bf16[512,512]{1,0:T(8,128)(2,1)}), bf16[512,8192]{1,0:T(8,128)(2,1)}) %all-gather.5.cloned.1.call-update) | async-done | bytes 8388624 | tf_op jit(solution)/shard_map/all_gather | solution.py:73
  185.6 10.1 %convolution_convert_fusion = bf16[512,8192]{1,0:T(8,128)(2,1)} fusion(bf16[512,512]{0,1:T(8,128)(2,1)S(1)} %bitcast.74, bf16[512,8192]{1,0:T(8,128)(2,1)} %all-gather.5.cloned.1.call-done), kind=kOutput, calls=%fused_computation.6 | convolution fusion | flops 4299161600 | bytes 17301504 | tf_op jit(solution)/shard_map/dot_general | solution.py:154
  195.7 52.4 %reduce-scatter.5.cloned.1.call-done = bf16[512,1024]{1,0:T(8,128)(2,1)} async-done(((bf16[512,8192]{1,0:T(8,128)(2,1)}), bf16[512,1024]{1,0:T(8,128)(2,1)}) %reduce-scatter.5.cloned.1.call-update) | async-done | bytes 1048592 | tf_op jit(solution)/shard_map/reduce_scatter | solution.py:159
  248.2 2.9 %add_convert_fusion = bf16[512,1024]{1,0:T(8,128)(2,1)} fusion(bf16[512,1024]{1,0:T(8,128)(2,1)} %reduce-scatter.5.cloned.1.call-done, bf16[512,8192]{1,0:T(8,128)(2,1)} %param.33, s32[]{:T(128)S(6)} %select_n.29), kind=kLoop, calls=%fused_computation.20 | loop fusion | flops 2097152 | bytes 3145732 | tf_op jit(solution)/shard_map/convert_element_type | solution.py:164
  (44 shorter events, 1.8 us)
Async XLA Ops:
  8.0 19.2 %copy-start = (bf16[128,1280]{1,0:T(8,128)(2,1)S(1)}, bf16[128,1280]{1,0:T(8,128)(2,1)}, u32[]{:S(2)}) copy-start(bf16[128,1280]{1,0:T(8,128)(2,1)} %param.28) | copy-start | bytes 983044
  8.0 17.3 %copy-start.8 = (s32[2]{0:T(128)S(1)}, s32[2]{0:T(128)}, u32[]{:S(2)}) copy-start(s32[2]{0:T(128)} %param.30) | copy-start | bytes 28
  8.0 55.8 %reduce-scatter.3.cloned.1.call-start = ((), (), s32[]{:S(2)}) async-start(), calls=%async_computation.2 | async-start | bytes 737280 | tf_op jit(solution)/shard_map/reduce_scatter | solution.py:102
  14.8 9.5 %collective-permute-start = (bf16[128,2,128]{2,0,1:T(8,128)(2,1)S(1)}, bf16[128,2,128]{2,0,1:T(8,128)(2,1)S(1)}, u32[]{:S(2)}, u32[]{:S(2)}) collective-permute-start(bf16[128,2,128]{2,0,1:T(8,128)(2,1)S(1)} %get-tuple-element.4), channel_id=1, source_target_pairs={{0,8},{8,16},{16,24},{24,32},{32,40},{40,48},{48,56},{56,64},{64,7... | collective-permute-start | bytes 196616 | tf_op jit(solution)/shard_map/ppermute | solution.py:15
  18.2 6.4 %collective-permute-start.1 = (bf16[128,2,128]{2,0,1:T(8,128)(2,1)S(1)}, bf16[128,2,128]{2,0,1:T(8,128)(2,1)S(1)}, u32[]{:S(2)}, u32[]{:S(2)}) collective-permute-start(bf16[128,2,128]{2,0,1:T(8,128)(2,1)S(1)} %get-tuple-element.5), channel_id=1, source_target_pairs={{8,0},{16,8},{24,16},{32,24},{40,32},{48,40},{56,48},{64,56},{72,6... | collective-permute-start | bytes 196616 | tf_op jit(solution)/shard_map/ppermute | solution.py:18
  24.9 4.8 %copy-start.2 = (s32[512]{0:T(512)S(1)}, s32[512]{0:T(512)}, u32[]{:S(2)}) copy-start(s32[512]{0:T(512)} %param.38) | copy-start | bytes 6148
  24.9 4.8 %copy-start.5 = (s32[512]{0:T(512)S(1)}, s32[512]{0:T(512)}, u32[]{:S(2)}) copy-start(s32[512]{0:T(512)} %param.39) | copy-start | bytes 6148
  24.9 4.8 %copy-start.4 = (f32[8,128]{1,0:T(8,128)S(1)}, f32[8,128]{1,0:T(8,128)}, u32[]{:S(2)}) copy-start(f32[8,128]{1,0:T(8,128)} %param.32) | copy-start | bytes 12292
  28.5 35.4 %copy-start.3 = (f32[1280]{0:T(1024)S(1)}, f32[1280]{0:T(1024)}, u32[]{:S(2)}) copy-start(f32[1280]{0:T(1024)} %param.29) | copy-start | bytes 15364
  28.5 77.6 %all-gather.3.cloned.1.call-start = ((), (), s32[]{:S(2)}) async-start(), calls=%async_computation.3 | async-start | bytes 8912896 | tf_op jit(solution)/shard_map/all_gather | solution.py:72
  29.0 156.6 %all-gather.5.cloned.1.call-start = ((), (), s32[]{:S(2)}) async-start(), calls=%async_computation.4 | async-start | bytes 8912896 | tf_op jit(solution)/shard_map/all_gather | solution.py:73
  29.6 218.5 %reduce-scatter.5.cloned.1.call-start = ((), (), s32[]{:S(2)}) async-start(), calls=%async_computation.5 | async-start | bytes 9437184 | tf_op jit(solution)/shard_map/reduce_scatter | solution.py:159
  33.0 73.1 %copy-start.6 = (f32[8192]{0:T(1024)S(1)}, f32[8192]{0:T(1024)}, u32[]{:S(2)}) copy-start(f32[8192]{0:T(1024)} %param.34) | copy-start | bytes 98308
  33.0 73.1 %copy-start.7 = (f32[512]{0:T(512)S(1)}, f32[512]{0:T(512)}, u32[]{:S(2)}) copy-start(f32[512]{0:T(512)} %param.36) | copy-start | bytes 6148
  64.8 51.7 %copy-start.1 = (bf16[32,1280]{1,0:T(8,128)(2,1)}, bf16[32,1280]{1,0:T(8,128)(2,1)S(1)}, u32[]{:S(2)}) copy-start(bf16[32,1280]{1,0:T(8,128)(2,1)S(1)} %add_convert_fusion.1) | copy-start | bytes 245764
  78.4 11.0 %collective-permute-start.3 = (bf16[256,1,256]{2,0,1:T(8,128)(2,1)S(1)}, bf16[256,1,256]{2,0,1:T(8,128)(2,1)S(1)}, u32[]{:S(2)}, u32[]{:S(2)}) collective-permute-start(bf16[256,1,256]{2,0,1:T(8,128)(2,1)S(1)} %fusion.38), channel_id=1, source_target_pairs={{8,0},{16,8},{24,16},{32,24},{40,32},{48,40},{56,48},{64,56},{72,6... | collective-permute-start | bytes 393224 | tf_op jit(solution)/shard_map/ppermute | solution.py:18
  82.8 12.9 %collective-permute-start.2 = (bf16[256,1,256]{2,0,1:T(8,128)(2,1)S(1)}, bf16[256,1,256]{2,0,1:T(8,128)(2,1)S(1)}, u32[]{:S(2)}, u32[]{:S(2)}) collective-permute-start(bf16[256,1,256]{2,0,1:T(8,128)(2,1)S(1)} %fusion.38), channel_id=1, source_target_pairs={{0,8},{8,16},{16,24},{24,32},{32,40},{40,48},{48,56},{56,64},{64,7... | collective-permute-start | bytes 393224 | tf_op jit(solution)/shard_map/ppermute | solution.py:15
Sparse Core Ops, SparseCore 0:
  28.6 35.2 reduce-scatter.2
  195.9 52.2 reduce-scatter.4
Sparse Core Ops, SparseCore 1:
  31.1 75.0 all-gather.2
  108.1 77.5 all-gather.4

commit v2 on v0

--- a/solution.py
+++ b/solution.py
@@ -18,6 +18,23 @@
         high = lax.ppermute(lax.slice_in_dim(block, 0, width, axis=dim), axis, backward)
         block = jnp.concatenate([low, block, high], axis=dim)
     return block
+
+
+def heads_gather(block, axis):
+    count = lax.axis_size(axis)
+    index = lax.axis_index(axis)
+    gathered = block[None]
+    bit = 1
+    while bit < count:
+        other = lax.ppermute(gathered, axis, [(i, i ^ bit) for i in range(count)])
+        upper = (index & bit) != 0
+        gathered = jnp.where(
+            upper,
+            jnp.concatenate([other, gathered], axis=0),
+            jnp.concatenate([gathered, other], axis=0),
+        )
+        bit *= 2
+    return gathered
 
 
 def layer_norm(values, gain, shift):
@@ -96,27 +113,26 @@
         "hqk,khd->qhd", enc_weights, value_block, preferred_element_type=jnp.float32
     )
     enc_context = enc_context.astype(jnp.bfloat16).reshape(frames_dev, heads_dev * head_size)
-    enc_term = jnp.dot(enc_context, enc_wo, preferred_element_type=jnp.float32)
-    mixed = lax.psum_scatter(
-        enc_term.astype(jnp.bfloat16), "heads", scatter_dimension=0, tiled=True
-    ).astype(jnp.float32)
     share = frames_dev // head_count
+    full_wo = heads_gather(enc_wo, "heads").reshape(head_count * enc_wo.shape[0], enc_width)
+    context_share = lax.all_to_all(enc_context, "heads", 0, 1, tiled=True)
+    mixed = jnp.dot(context_share, full_wo, preferred_element_type=jnp.float32)
     own_audio = lax.dynamic_slice_in_dim(audio, head_index * share, share, 0)
     enc_out = (own_audio.astype(jnp.float32) + mixed + enc_bo).astype(jnp.bfloat16)
-    groups_dev = dec_wkv.shape[1] // head_count
+    groups = dec_wkv.shape[1]
+    groups_dev = groups // head_count
     pair_width = dec_wkv.shape[2]
     dec_head = pair_width // 2
     band_bias = jnp.concatenate([jnp.zeros_like(dec_bv), dec_bv], axis=1)
-    frames_all = lax.all_gather(enc_out, "heads", axis=0, tiled=True)
-    weight_group = lax.dynamic_slice_in_dim(
-        dec_wkv, head_index * groups_dev, groups_dev, 1
-    ).reshape(enc_width, groups_dev * pair_width)
-    bias_group = lax.dynamic_slice_in_dim(
-        band_bias, head_index * groups_dev, groups_dev, 0
-    ).reshape(groups_dev * pair_width)
-    band_pairs = (
-        jnp.dot(frames_all, weight_group, preferred_element_type=jnp.float32) + bias_group
+    share_pairs = (
+        jnp.dot(
+            enc_out,
+            dec_wkv.reshape(enc_width, groups * pair_width),
+            preferred_element_type=jnp.float32,
+        )
+        + band_bias.reshape(groups * pair_width)
     ).astype(jnp.bfloat16)
+    band_pairs = lax.all_to_all(share_pairs, "heads", 1, 0, tiled=True)
     band_pairs = band_pairs.reshape(frames_dev, groups_dev, pair_width)
     band_wide = with_halo(band_pairs, (("seq", 0),), BAND)
     rows_dev = text.shape[0]

time: 260 us -> 236 us (0.908)
  waiting for transfers between devices: 165 us -> 132 us
  blocking collectives: 13.2 us -> 0 us
  starting transfers between devices: 14.7 us -> 26.7 us
  local copies, waits for them, and re-layouts: 3.56 us -> 9.01 us
  matrix products: 30.7 us -> 34.1 us
    reduce_scatter x1 -> x0, waiting for transfers between devices: 25.3 us -> none  [shards(): lax.psum_scatter(enc_term.astype(jnp.bfloat16), 'heads', scatter_dimensio...]
    all_gather x1, waiting for transfers between devices: 64.5 us -> 43.1 us  [shards(): lax.all_gather(dec_wo, 'seq', axis=1, tiled=True)]
    all_to_all x0 -> x2, waiting for transfers between devices: none -> 18.7 us  [the longest x1 13 us: shards(): context_share = lax.all_to_all(enc_context, 'heads', 0, 1, tiled=True)]
    all_gather x1 -> x0, blocking collectives: 13.2 us -> none  [shards(): frames_all = lax.all_gather(enc_out, 'heads', axis=0, tiled=True)]
    all_gather x1, waiting for transfers between devices: 10.3 us -> 0.02 us  [shards(): lax.all_gather(dec_wq, 'seq', axis=0, tiled=True)]
    ppermute x0 -> x3, waiting for transfers between devices: none -> 8.28 us  [heads_gather(): other = lax.ppermute(gathered, axis, [(i, i ^ bit) for i in range(count)])]
    all_to_all x0 -> x2, starting transfers between devices: none -> 7.65 us  [the longest x1 4.3 us: shards(): band_pairs = lax.all_to_all(share_pairs, 'heads', 1, 0, tiled=True)]
    unnamed x18 -> x27, local copies, waits for them, and re-layouts: 0.06 us -> 7.23 us
  transfers between devices with their start and end apart: 8 -> 12, of which waited for: 7 -> 7; matrix products, arithmetic and copies ran while one was open for 10% -> 20% of each run, Pallas kernels for 0% -> 0%
where the time goes in v2:
time: 236 us; the launch traced here: 234 us
  waiting for transfers between devices  132 us (56%)
  matrix products  34.1 us (14%)
  starting transfers between devices  26.7 us (11%)
  other arithmetic  17.7 us (8%)
  between operations  14.2 us (6%)
  local copies, waits for them, and re-layouts  9.01 us (4%)
    reduce_scatter x1, waiting for transfers between devices, shards(): lax.psum_scatter(dec_term.astype(jnp.bfloat16), 'heads', scatter_dimensio...  52.4 us
    all_gather x1, waiting for transfers between devices, shards(): lax.all_gather(dec_wo, 'seq', axis=1, tiled=True)  43.1 us
    all_to_all x1, waiting for transfers between devices, shards(): context_share = lax.all_to_all(enc_context, 'heads', 0, 1, tiled=True)  13 us
    dot_general x1, matrix products, shards(): jnp.dot(normed, lax.all_gather(dec_wq, 'seq', axis=0, tiled=True), prefer...  10.6 us
    dot_general x1, matrix products, shards(): jnp.dot(dec_context, lax.all_gather(dec_wo, 'seq', axis=1, tiled=True), p...  10.1 us
    ppermute x3, waiting for transfers between devices, heads_gather(): other = lax.ppermute(gathered, axis, [(i, i ^ bit) for i in range(count)])  8.28 us
    unnamed x27, local copies, waits for them, and re-layouts  7.23 us
    ppermute x2, waiting for transfers between devices, with_halo(): lax.ppermute(lax.slice_in_dim(block, block.shape[dim] - width, None, axis...  7.04 us
  transfers between devices with their start and end apart: 12, of which 7 were waited for; matrix products, arithmetic and copies ran while one was open for 20% of the time, Pallas kernels for 0%

profile of v2, /device:TPU:96, one launch (start us, length us, event | category | flops | bytes accessed | tf_op | source)
XLA Modules:
  0.0 233.5 jit_solution(11193668153644258772)
XLA Ops:
  8.8 1.3 convert_reduce_fusion
  10.1 1.4 fusion.36
  11.5 1.4 fusion.39
  13.2 1.3 fusion.53
  14.5 3.4 %collective-permute-start = (bf16[128,2,128]{2,0,1:T(8,128)(2,1)S(1)}, bf16[128,2,128]{2,0,1:T(8,128)(2,1)S(1)}, u32[]{:S(2)}, u32[]{:S(2)}) collective-permute-start(bf16[128,2,128]{2,0,1:T(8,128)(2,1)S(1)} %get-tuple-element.4), channel_id=1, source_target_pairs={{0,8},{8,16},{16,24},{24,32},{32,40},{40,48},{48,56},{56,64},{64,7... | collective-permute-start | bytes 196616 | tf_op jit(solution)/shard_map/ppermute | solution.py:15
  18.0 4.5 %collective-permute-start.1 = (bf16[128,2,128]{2,0,1:T(8,128)(2,1)S(1)}, bf16[128,2,128]{2,0,1:T(8,128)(2,1)S(1)}, u32[]{:S(2)}, u32[]{:S(2)}) collective-permute-start(bf16[128,2,128]{2,0,1:T(8,128)(2,1)S(1)} %get-tuple-element.5), channel_id=1, source_target_pairs={{8,0},{16,8},{24,16},{32,24},{40,32},{48,40},{56,48},{64,56},{72,6... | collective-permute-start | bytes 196616 | tf_op jit(solution)/shard_map/ppermute | solution.py:18
  23.1 1.7 collective-permute-start.3
  24.7 0.9 subtract_abs_fusion
  25.7 5.8 %fusion.1 = f32[512]{0:T(512)} fusion(bf16[512,8192]{1,0:T(8,128)(2,1)} %param.33), kind=kLoop, calls=%fused_computation.3 | loop fusion | flops 12582400 | bytes 8390656 | tf_op jit(solution)/shard_map/reduce_sum | solution.py:49
  31.5 8.3 %collective-permute-done.3 = bf16[2,128,1280]{2,1,0:T(8,128)(2,1)S(1)} collective-permute-done((bf16[2,128,1280]{2,1,0:T(8,128)(2,1)S(1)}, bf16[2,128,1280]{2,1,0:T(8,128)(2,1)S(1)}, u32[]{:S(2)}, u32[]{:S(2)}) %collective-permute-start.3) | collective-permute-done | bytes 655392 | tf_op jit(solution)/shard_map/ppermute | solution.py:29
  39.9 3.3 %collective-permute-start.4 = (bf16[4,128,1280]{2,1,0:T(8,128)(2,1)S(1)}, bf16[4,128,1280]{2,1,0:T(8,128)(2,1)}, u32[]{:S(2)}, u32[]{:S(2)}) collective-permute-start(bf16[4,128,1280]{2,1,0:T(8,128)(2,1)S(1)} %maximum_select_fusion.10), channel_id=1, source_target_pairs={{0,4},{1,5},{2,6},{3,7},{4,0},{5,1},{6,2},{7,3},{8,12},{9,13},{10,... | collective-permute-start | bytes 3932168 | tf_op jit(solution)/shard_map/ppermute | solution.py:29
  43.3 7.2 %copy.48 = bf16[160,8,8,256]{3,1,2,0:T(8,128)(2,1)} copy(bf16[160,8,8,256]{3,2,1,0:T(8,128)(2,1)} %bitcast.91) | data formatting | bytes 10485760
  51.6 1.4 fusion.73
  53.0 1.9 fusion.52
  55.8 3.4 %all-to-all-start = ((bf16[8,32,128]{2,1,0:T(8,128)(2,1)}), bf16[8,32,128]{2,1,0:T(8,128)(2,1)S(1)}, u32[]{:S(2)}, u32[]{:S(2)}) async-start(bf16[8,32,128]{2,1,0:T(8,128)(2,1)} %all_to_all.24), calls=%async_computation | async-start | bytes 131072 | tf_op jit(solution)/shard_map/all_to_all | solution.py:118
  59.2 13.0 %all-to-all-done = bf16[8,32,128]{2,1,0:T(8,128)(2,1)S(1)} async-done(((bf16[8,32,128]{2,1,0:T(8,128)(2,1)}), bf16[8,32,128]{2,1,0:T(8,128)(2,1)S(1)}, u32[]{:S(2)}, u32[]{:S(2)}) %all-to-all-start) | async-done | bytes 65568 | tf_op jit(solution)/shard_map/all_to_all | solution.py:118
  72.2 2.4 %fusion.25 = bf16[32,1280]{1,0:T(8,128)(2,1)S(1)} fusion(bf16[4,128,1280]{2,1,0:T(8,128)(2,1)S(1)} %maximum_select_fusion.10, bf16[4,128,1280]{2,1,0:T(8,128)(2,1)} %collective-permute-done.4, pred[]{:T(512)S(6)} %ne.9, f32[1280]{0:T(1024)} %param.29, bf16[256,1280]{1,0:T(8,128)(2,1)} %param.20, s32[]{:T(128)S(6)} %select_n.46, ...), kind=kOutput, calls=%fused_computation.32 | convolution fusion | flops 87982080 | bytes 2855941 | tf_op jit(solution)/shard_map/dot_general | solution.py:119
  74.7 3.5 %fusion.24 = bf16[32,2048]{1,0:T(8,128)(2,1)S(1)} fusion(bf16[32,1280]{1,0:T(8,128)(2,1)S(1)} %fusion.25, bf16[1280,2048]{1,0:T(8,128)(2,1)} %bitcast.90, f32[2048]{0:T(1024)S(1)} %bitcast.103), kind=kOutput, calls=%fused_computation.31 | convolution fusion | flops 167903232 | bytes 5464064 | tf_op jit(solution)/shard_map/dot_general | solution.py:128
  78.9 4.3 %all-to-all-start.1 = ((bf16[32,8,256]{2,0,1:T(8,128)(2,1)}), bf16[32,8,256]{2,0,1:T(8,128)(2,1)S(1)}, u32[]{:S(2)}, u32[]{:S(2)}) async-start(bf16[32,8,256]{2,0,1:T(8,128)(2,1)} %bitcast.89), calls=%async_computation.1 | async-start | bytes 262144 | tf_op jit(solution)/shard_map/all_to_all | solution.py:135
  83.6 5.7 %all-to-all-done.1 = bf16[32,8,256]{2,0,1:T(8,128)(2,1)S(1)} async-done(((bf16[32,8,256]{2,0,1:T(8,128)(2,1)}), bf16[32,8,256]{2,0,1:T(8,128)(2,1)S(1)}, u32[]{:S(2)}, u32[]{:S(2)}) %all-to-all-start.1) | async-done | bytes 131104 | tf_op jit(solution)/shard_map/all_to_all | solution.py:135
  89.3 2.4 %collective-permute-start.6 = (bf16[256,1,256]{2,0,1:T(8,128)(2,1)S(1)}, bf16[256,1,256]{2,0,1:T(8,128)(2,1)S(1)}, u32[]{:S(2)}, u32[]{:S(2)}) collective-permute-start(bf16[256,1,256]{2,0,1:T(8,128)(2,1)S(1)} %bitcast.96), channel_id=1, source_target_pairs={{8,0},{16,8},{24,16},{32,24},{40,32},{48,40},{56,48},{64,56},{72,6... | collective-permute-start | bytes 393224 | tf_op jit(solution)/shard_map/ppermute | solution.py:18
  91.6 3.6 %collective-permute-start.5 = (bf16[256,1,256]{2,0,1:T(8,128)(2,1)S(1)}, bf16[256,1,256]{2,0,1:T(8,128)(2,1)S(1)}, u32[]{:S(2)}, u32[]{:S(2)}) collective-permute-start(bf16[256,1,256]{2,0,1:T(8,128)(2,1)S(1)} %bitcast.97), channel_id=1, source_target_pairs={{0,8},{8,16},{16,24},{24,32},{32,40},{40,48},{48,56},{56,64},{64,7... | collective-permute-start | bytes 393224 | tf_op jit(solution)/shard_map/ppermute | solution.py:15
  95.3 0.9 collective-permute-done.6
  96.2 7.0 %collective-permute-done.5 = bf16[256,1,256]{2,0,1:T(8,128)(2,1)S(1)} collective-permute-done((bf16[256,1,256]{2,0,1:T(8,128)(2,1)S(1)}, bf16[256,1,256]{2,0,1:T(8,128)(2,1)S(1)}, u32[]{:S(2)}, u32[]{:S(2)}) %collective-permute-start.5) | collective-permute-done | bytes 131104 | tf_op jit(solution)/shard_map/ppermute | solution.py:15
  103.3 10.6 %fusion.46 = bf16[512,512]{0,1:T(8,128)(2,1)S(1)} fusion(bf16[8192,512]{1,0:T(8,128)(2,1)} %all-gather.3.cloned.1.call-done, bf16[512,8192]{1,0:T(8,128)(2,1)} %param.33, f32[8192]{0:T(1024)S(1)} %copy-done.10, f32[512]{0:T(512)S(1)} %add_rsqrt_fusion, f32[512]{0:T(512)S(1)} %copy-done.11), kind=kOutput, calls=%fused_computation.52 | convolution fusion | flops 4312268800 | bytes 17338368 | tf_op jit(solution)/shard_map/dot_general | solution.py:143
  113.9 1.1 fusion.8
  115.0 1.4 fusion.11
  116.4 2.1 fusion.43
  118.5 43.1 %all-gather.5.cloned.1.call-done = bf16[512,8192]{1,0:T(8,128)(2,1)} async-done(((bf16[512,512]{1,0:T(8,128)(2,1)}), bf16[512,8192]{1,0:T(8,128)(2,1)}) %all-gather.5.cloned.1.call-update) | async-done | bytes 8388624 | tf_op jit(solution)/shard_map/all_gather | solution.py:170
  161.5 10.1 %convolution_convert_fusion = bf16[512,8192]{1,0:T(8,128)(2,1)} fusion(bf16[512,512]{0,1:T(8,128)(2,1)S(1)} %bitcast.92, bf16[512,8192]{1,0:T(8,128)(2,1)} %all-gather.5.cloned.1.call-done), kind=kOutput, calls=%fused_computation.6 | convolution fusion | flops 4299161600 | bytes 17301504 | tf_op jit(solution)/shard_map/dot_general | solution.py:168
  171.6 52.4 %reduce-scatter.2.cloned.1.call-done = bf16[512,1024]{1,0:T(8,128)(2,1)} async-done(((bf16[512,8192]{1,0:T(8,128)(2,1)}), bf16[512,1024]{1,0:T(8,128)(2,1)}) %reduce-scatter.2.cloned.1.call-update) | async-done | bytes 1048592 | tf_op jit(solution)/shard_map/reduce_scatter | solution.py:173
  224.1 2.9 %add_convert_fusion = bf16[512,1024]{1,0:T(8,128)(2,1)} fusion(bf16[512,1024]{1,0:T(8,128)(2,1)} %reduce-scatter.2.cloned.1.call-done, bf16[512,8192]{1,0:T(8,128)(2,1)} %param.33, s32[]{:T(128)S(6)} %select_n.55), kind=kLoop, calls=%fused_computation.33 | loop fusion | flops 2097152 | bytes 3145732 | tf_op jit(solution)/shard_map/convert_element_type | solution.py:178
  (61 shorter events, 5.8 us)
Async XLA Ops:
  7.2 5.7 %copy-start = (bf16[1280,128]{1,0:T(8,128)(2,1)S(1)}, bf16[1280,128]{1,0:T(8,128)(2,1)}, u32[]{:S(2)}) copy-start(bf16[1280,128]{1,0:T(8,128)(2,1)} %param.25) | copy-start | bytes 983044
  7.2 15.8 %copy-start.3 = (bf16[128,1280]{1,0:T(8,128)(2,1)S(1)}, bf16[128,1280]{1,0:T(8,128)(2,1)}, u32[]{:S(2)}) copy-start(bf16[128,1280]{1,0:T(8,128)(2,1)} %param.28) | copy-start | bytes 983044
  7.2 15.3 %copy-start.9 = (f32[128]{0:T(128)S(1)}, f32[128]{0:T(128)}, u32[]{:S(2)}) copy-start(f32[128]{0:T(128)} %param.24) | copy-start | bytes 1540
  7.2 15.3 %copy-start.2 = (bf16[1280,128]{1,0:T(8,128)(2,1)S(1)}, bf16[1280,128]{1,0:T(8,128)(2,1)}, u32[]{:S(2)}) copy-start(bf16[1280,128]{1,0:T(8,128)(2,1)} %param.23) | copy-start | bytes 983044
  7.2 96.1 %all-gather.3.cloned.1.call-start = ((), (), s32[]{:S(2)}) async-start(), calls=%async_computation.3 | async-start | bytes 8912896 | tf_op jit(solution)/shard_map/all_gather | solution.py:145
  7.9 153.6 %all-gather.5.cloned.1.call-start = ((), (), s32[]{:S(2)}) async-start(), calls=%async_computation.4 | async-start | bytes 8912896 | tf_op jit(solution)/shard_map/all_gather | solution.py:170
  8.7 14.3 %collective-permute-start.2 = (bf16[1,128,1280]{2,1,0:T(8,128)(2,1)}, bf16[1,128,1280]{2,1,0:T(8,128)(2,1)S(1)}, u32[]{:S(2)}, u32[]{:S(2)}) collective-permute-start(bf16[1,128,1280]{2,1,0:T(8,128)(2,1)} %bitcast.99), channel_id=1, source_target_pairs={{0,1},{1,0},{2,3},{3,2},{4,5},{5,4},{6,7},{7,6},{8,9},{9,8},{10,11... | collective-permute-start | bytes 983048 | tf_op jit(solution)/shard_map/ppermute | solution.py:29
  14.5 36.4 %collective-permute-start = (bf16[128,2,128]{2,0,1:T(8,128)(2,1)S(1)}, bf16[128,2,128]{2,0,1:T(8,128)(2,1)S(1)}, u32[]{:S(2)}, u32[]{:S(2)}) collective-permute-start(bf16[128,2,128]{2,0,1:T(8,128)(2,1)S(1)} %get-tuple-element.4), channel_id=1, source_target_pairs={{0,8},{8,16},{16,24},{24,32},{32,40},{40,48},{48,56},{56,64},{64,7... | collective-permute-start | bytes 196616 | tf_op jit(solution)/shard_map/ppermute | solution.py:15
  18.0 33.0 %collective-permute-start.1 = (bf16[128,2,128]{2,0,1:T(8,128)(2,1)S(1)}, bf16[128,2,128]{2,0,1:T(8,128)(2,1)S(1)}, u32[]{:S(2)}, u32[]{:S(2)}) collective-permute-start(bf16[128,2,128]{2,0,1:T(8,128)(2,1)S(1)} %get-tuple-element.5), channel_id=1, source_target_pairs={{8,0},{16,8},{24,16},{32,24},{40,32},{48,40},{56,48},{64,56},{72,6... | collective-permute-start | bytes 196616 | tf_op jit(solution)/shard_map/ppermute | solution.py:18
  23.1 16.7 %collective-permute-start.3 = (bf16[2,128,1280]{2,1,0:T(8,128)(2,1)S(1)}, bf16[2,128,1280]{2,1,0:T(8,128)(2,1)S(1)}, u32[]{:S(2)}, u32[]{:S(2)}) collective-permute-start(bf16[2,128,1280]{2,1,0:T(8,128)(2,1)S(1)} %maximum_select_fusion.11), channel_id=1, source_target_pairs={{0,2},{1,3},{2,0},{3,1},{4,6},{5,7},{6,4},{7,5},{8,10},{9,11},{10,... | collective-permute-start | bytes 1966088 | tf_op jit(solution)/shard_map/ppermute | solution.py:29
  25.7 17.6 %copy-start.7 = (f32[8,128]{1,0:T(8,128)S(1)}, f32[8,128]{1,0:T(8,128)}, u32[]{:S(2)}) copy-start(f32[8,128]{1,0:T(8,128)} %param.32) | copy-start | bytes 12292
  39.9 32.3 %collective-permute-start.4 = (bf16[4,128,1280]{2,1,0:T(8,128)(2,1)S(1)}, bf16[4,128,1280]{2,1,0:T(8,128)(2,1)}, u32[]{:S(2)}, u32[]{:S(2)}) collective-permute-start(bf16[4,128,1280]{2,1,0:T(8,128)(2,1)S(1)} %maximum_select_fusion.10), channel_id=1, source_target_pairs={{0,4},{1,5},{2,6},{3,7},{4,0},{5,1},{6,2},{7,3},{8,12},{9,13},{10,... | collective-permute-start | bytes 3932168 | tf_op jit(solution)/shard_map/ppermute | solution.py:29
  43.2 7.2 %copy-start.5 = (s32[512]{0:T(512)S(1)}, s32[512]{0:T(512)}, u32[]{:S(2)}) copy-start(s32[512]{0:T(512)} %param.38) | copy-start | bytes 6148
  43.2 7.2 %copy-start.8 = (s32[512]{0:T(512)S(1)}, s32[512]{0:T(512)}, u32[]{:S(2)}) copy-start(s32[512]{0:T(512)} %param.39) | copy-start | bytes 6148
  43.2 8.3 %copy-start.1 = (s32[256,512]{1,0:T(8,128)S(1)}, s32[256,512]{1,0:T(8,128)}, u32[]{:S(2)}) copy-start(s32[256,512]{1,0:T(8,128)} %subtract_abs_fusion) | copy-start | bytes 1572868
  55.8 16.4 %all-to-all-start = ((bf16[8,32,128]{2,1,0:T(8,128)(2,1)}), bf16[8,32,128]{2,1,0:T(8,128)(2,1)S(1)}, u32[]{:S(2)}, u32[]{:S(2)}) async-start(bf16[8,32,128]{2,1,0:T(8,128)(2,1)} %all_to_all.24), calls=%async_computation | async-start | bytes 131072 | tf_op jit(solution)/shard_map/all_to_all | solution.py:118
  74.6 39.3 %copy-start.4 = (bf16[32,1280]{1,0:T(8,128)(2,1)}, bf16[32,1280]{1,0:T(8,128)(2,1)S(1)}, u32[]{:S(2)}) copy-start(bf16[32,1280]{1,0:T(8,128)(2,1)S(1)} %fusion.25) | copy-start | bytes 245764
  74.6 20.7 %copy-start.6 = (f32[512]{0:T(512)S(1)}, f32[512]{0:T(512)}, u32[]{:S(2)}) copy-start(f32[512]{0:T(512)} %fusion.1) | copy-start | bytes 6148
  74.6 28.7 %copy-start.10 = (f32[8192]{0:T(1024)S(1)}, f32[8192]{0:T(1024)}, u32[]{:S(2)}) copy-start(f32[8192]{0:T(1024)} %param.34) | copy-start | bytes 98308
  74.6 28.7 %copy-start.11 = (f32[512]{0:T(512)S(1)}, f32[512]{0:T(512)}, u32[]{:S(2)}) copy-start(f32[512]{0:T(512)} %param.36) | copy-start | bytes 6148
  78.9 10.4 %all-to-all-start.1 = ((bf16[32,8,256]{2,0,1:T(8,128)(2,1)}), bf16[32,8,256]{2,0,1:T(8,128)(2,1)S(1)}, u32[]{:S(2)}, u32[]{:S(2)}) async-start(bf16[32,8,256]{2,0,1:T(8,128)(2,1)} %bitcast.89), calls=%async_computation.1 | async-start | bytes 262144 | tf_op jit(solution)/shard_map/all_to_all | solution.py:135
  83.2 140.9 %reduce-scatter.2.cloned.1.call-start = ((), (), s32[]{:S(2)}) async-start(), calls=%async_computation.5 | async-start | bytes 9437184 | tf_op jit(solution)/shard_map/reduce_scatter | solution.py:173
  89.3 6.9 %collective-permute-start.6 = (bf16[256,1,256]{2,0,1:T(8,128)(2,1)S(1)}, bf16[256,1,256]{2,0,1:T(8,128)(2,1)S(1)}, u32[]{:S(2)}, u32[]{:S(2)}) collective-permute-start(bf16[256,1,256]{2,0,1:T(8,128)(2,1)S(1)} %bitcast.96), channel_id=1, source_target_pairs={{8,0},{16,8},{24,16},{32,24},{40,32},{48,40},{56,48},{64,56},{72,6... | collective-permute-start | bytes 393224 | tf_op jit(solution)/shard_map/ppermute | solution.py:18
  91.6 11.6 %collective-permute-start.5 = (bf16[256,1,256]{2,0,1:T(8,128)(2,1)S(1)}, bf16[256,1,256]{2,0,1:T(8,128)(2,1)S(1)}, u32[]{:S(2)}, u32[]{:S(2)}) collective-permute-start(bf16[256,1,256]{2,0,1:T(8,128)(2,1)S(1)} %bitcast.97), channel_id=1, source_target_pairs={{0,8},{8,16},{16,24},{24,32},{32,40},{40,48},{48,56},{56,64},{64,7... | collective-permute-start | bytes 393224 | tf_op jit(solution)/shard_map/ppermute | solution.py:15
Sparse Core Ops, SparseCore 0:
  10.2 72.5 all-gather.2
  84.8 76.6 all-gather.4
  171.8 52.2 reduce-scatter.1

commit v3 on v2

--- a/solution.py
+++ b/solution.py
@@ -55,7 +55,7 @@
     return (raised / jnp.sum(raised, axis=-1, keepdims=True)).astype(jnp.bfloat16)
 
 
-def shards(
+def layer_body(
     audio,
     ln_gain,
     ln_shift,
@@ -86,6 +86,7 @@
     heads_dev = windows.shape[0]
     head_size = enc_wq.shape[1] // heads_dev
     all_frames = frames_dev * seq_count
+    output_weight = lax.all_to_all(jnp.tile(dec_wo, (1, seq_count)), "seq", 1, 1, tiled=True)
     hidden = layer_norm(audio, ln_gain, ln_shift).astype(jnp.bfloat16)
     enc_query = (jnp.dot(hidden, enc_wq, preferred_element_type=jnp.float32) + enc_bq).astype(
         jnp.bfloat16
@@ -115,7 +116,10 @@
     enc_context = enc_context.astype(jnp.bfloat16).reshape(frames_dev, heads_dev * head_size)
     share = frames_dev // head_count
     full_wo = heads_gather(enc_wo, "heads").reshape(head_count * enc_wo.shape[0], enc_width)
-    context_share = lax.all_to_all(enc_context, "heads", 0, 1, tiled=True)
+    context_all = heads_gather(enc_context.reshape(head_count, share, enc_context.shape[1]), "heads")
+    context_share = lax.dynamic_index_in_dim(
+        jnp.moveaxis(context_all, 0, 2), head_index, 0, keepdims=False
+    ).reshape(share, head_count * enc_context.shape[1])
     mixed = jnp.dot(context_share, full_wo, preferred_element_type=jnp.float32)
     own_audio = lax.dynamic_slice_in_dim(audio, head_index * share, share, 0)
     enc_out = (own_audio.astype(jnp.float32) + mixed + enc_bo).astype(jnp.bfloat16)
@@ -124,15 +128,16 @@
     pair_width = dec_wkv.shape[2]
     dec_head = pair_width // 2
     band_bias = jnp.concatenate([jnp.zeros_like(dec_bv), dec_bv], axis=1)
-    share_pairs = (
-        jnp.dot(
-            enc_out,
-            dec_wkv.reshape(enc_width, groups * pair_width),
-            preferred_element_type=jnp.float32,
-        )
-        + band_bias.reshape(groups * pair_width)
+    frames_all = heads_gather(enc_out, "heads").reshape(frames_dev, enc_width)
+    weight_group = lax.dynamic_slice_in_dim(
+        dec_wkv, head_index * groups_dev, groups_dev, 1
+    ).reshape(enc_width, groups_dev * pair_width)
+    bias_group = lax.dynamic_slice_in_dim(
+        band_bias, head_index * groups_dev, groups_dev, 0
+    ).reshape(groups_dev * pair_width)
+    band_pairs = (
+        jnp.dot(frames_all, weight_group, preferred_element_type=jnp.float32) + bias_group
     ).astype(jnp.bfloat16)
-    band_pairs = lax.all_to_all(share_pairs, "heads", 1, 0, tiled=True)
     band_pairs = band_pairs.reshape(frames_dev, groups_dev, pair_width)
     band_wide = with_halo(band_pairs, (("seq", 0),), BAND)
     rows_dev = text.shape[0]
@@ -167,7 +172,7 @@
     dec_context = dec_context.astype(jnp.bfloat16).reshape(rows_dev, query_width)
     dec_term = jnp.dot(
         dec_context,
-        lax.all_gather(dec_wo, "seq", axis=1, tiled=True),
+        output_weight,
         preferred_element_type=jnp.float32,
     )
     summed = lax.psum_scatter(
@@ -181,7 +186,7 @@
 
 def solution(mesh):
     return jax.shard_map(
-        shards,
+        layer_body,
         mesh=mesh,
         in_specs=(
             P("seq", None),

time: 236 us -> 356 us (1.51)
  waiting for transfers between devices: 132 us -> 225 us
  starting transfers between devices: 26.7 us -> 45.6 us
  local copies, waits for them, and re-layouts: 9.01 us -> 21.2 us
  matrix products: 34.1 us -> 28.6 us
    ppermute x2, waiting for transfers between devices: 7.04 us -> 116 us  [with_halo(): lax.ppermute(lax.slice_in_dim(block, block.shape[dim] - width, None, axis...]
    all_gather x2 -> x1, waiting for transfers between devices: 43.1 us -> 0.01 us  [layer_body(): lax.all_gather(dec_wq, 'seq', axis=0, tiled=True)]
    ppermute x3 -> x9, waiting for transfers between devices: 8.28 us -> 43.7 us  [heads_gather(): other = lax.ppermute(gathered, axis, [(i, i ^ bit) for i in range(count)])]
    all_to_all x2 -> x1, waiting for transfers between devices: 18.7 us -> 0.01 us  [layer_body(): lax.all_to_all(jnp.tile(dec_wo, (1, seq_count)), 'seq', 1, 1, tiled=True)]
    ppermute x2, starting transfers between devices: 6.93 us -> 23.9 us  [with_halo(): lax.ppermute(lax.slice_in_dim(block, 0, width, axis=dim), axis, backward)]
    ppermute x2, waiting for transfers between devices: 0.88 us -> 15.2 us  [with_halo(): lax.ppermute(lax.slice_in_dim(block, 0, width, axis=dim), axis, backward)]
    all_to_all x2 -> x1, local copies, waits for them, and re-layouts: 1.41 us -> 12.3 us  [layer_body(): lax.all_to_all(jnp.tile(dec_wo, (1, seq_count)), 'seq', 1, 1, tiled=True)]
    unnamed x27 -> x36, local copies, waits for them, and re-layouts: 7.23 us -> 0.1 us
  transfers between devices with their start and end apart: 12 -> 16, of which waited for: 7 -> 10; matrix products, arithmetic and copies ran while one was open for 20% -> 11% of each run, Pallas kernels for 0% -> 0%
where the time goes in v3:
time: 356 us; the launch traced here: 354 us
  waiting for transfers between devices  225 us (63%)
  starting transfers between devices  45.6 us (13%)
  matrix products  28.6 us (8%)
  local copies, waits for them, and re-layouts  21.2 us (6%)
  other arithmetic  18.4 us (5%)
  between operations  14.6 us (4%)
    ppermute x2, waiting for transfers between devices, with_halo(): lax.ppermute(lax.slice_in_dim(block, block.shape[dim] - width, None, axis...  116 us
    reduce_scatter x1, waiting for transfers between devices, layer_body(): lax.psum_scatter(dec_term.astype(jnp.bfloat16), 'heads', scatter_dimensio...  49.3 us
    ppermute x9, waiting for transfers between devices, heads_gather(): other = lax.ppermute(gathered, axis, [(i, i ^ bit) for i in range(count)])  43.7 us
    ppermute x2, starting transfers between devices, with_halo(): lax.ppermute(lax.slice_in_dim(block, 0, width, axis=dim), axis, backward)  23.9 us
    ppermute x2, waiting for transfers between devices, with_halo(): lax.ppermute(lax.slice_in_dim(block, 0, width, axis=dim), axis, backward)  15.2 us
    all_to_all x1, local copies, waits for them, and re-layouts, layer_body(): lax.all_to_all(jnp.tile(dec_wo, (1, seq_count)), 'seq', 1, 1, tiled=True)  12.3 us
    dot_general x1, matrix products, layer_body(): jnp.dot(normed, lax.all_gather(dec_wq, 'seq', axis=0, tiled=True), prefer...  10.4 us
    dot_general x1, matrix products, layer_body(): jnp.dot(dec_context, output_weight, preferred_element_type=jnp.float32)  10.2 us
  transfers between devices with their start and end apart: 16, of which 10 were waited for; matrix products, arithmetic and copies ran while one was open for 11% of the time, Pallas kernels for 0%

profile of v3, /device:TPU:96, one launch (start us, length us, event | category | flops | bytes accessed | tf_op | source)
XLA Modules:
  0.0 353.8 jit_solution(15011444666636452761)
XLA Ops:
  8.0 5.1 %tile.2 = bf16[512,16,512]{2,0,1:T(8,128)(2,1)} broadcast(bf16[512,512]{1,0:T(8,128)(2,1)} %param.37), dimensions={0,2} | broadcast | bytes 8912896 | tf_op jit(solution)/shard_map/tile | solution.py:89
  13.1 7.1 %all-to-all-start = ((bf16[512,16,512]{2,0,1:T(8,128)(2,1)}), bf16[512,16,512]{2,0,1:T(8,128)(2,1)}, u32[]{:S(2)}, u32[]{:S(2)}) async-start(bf16[512,16,512]{2,0,1:T(8,128)(2,1)} %tile.2), calls=%async_computation | async-start | bytes 16777216 | tf_op jit(solution)/shard_map/all_to_all | solution.py:89
  21.9 3.4 collective-permute-start
  25.3 4.6 %collective-permute-start.1 = (bf16[128,2,128]{2,0,1:T(8,128)(2,1)S(1)}, bf16[128,2,128]{2,0,1:T(8,128)(2,1)S(1)}, u32[]{:S(2)}, u32[]{:S(2)}) collective-permute-start(bf16[128,2,128]{2,0,1:T(8,128)(2,1)S(1)} %get-tuple-element.5), channel_id=1, source_target_pairs={{8,0},{16,8},{24,16},{32,24},{40,32},{48,40},{56,48},{64,56},{72,6... | collective-permute-start | bytes 196616 | tf_op jit(solution)/shard_map/ppermute | solution.py:18
  30.3 1.2 maximum_select_fusion.2
  31.5 1.7 collective-permute-start.6
  34.1 110.0 %collective-permute-done = bf16[128,2,128]{2,0,1:T(8,128)(2,1)S(1)} collective-permute-done((bf16[128,2,128]{2,0,1:T(8,128)(2,1)S(1)}, bf16[128,2,128]{2,0,1:T(8,128)(2,1)S(1)}, u32[]{:S(2)}, u32[]{:S(2)}) %collective-permute-start) | collective-permute-done | bytes 65568 | tf_op jit(solution)/shard_map/ppermute | solution.py:15
  144.1 14.8 %collective-permute-done.1 = bf16[128,2,128]{2,0,1:T(8,128)(2,1)S(1)} collective-permute-done((bf16[128,2,128]{2,0,1:T(8,128)(2,1)S(1)}, bf16[128,2,128]{2,0,1:T(8,128)(2,1)S(1)}, u32[]{:S(2)}, u32[]{:S(2)}) %collective-permute-start.1) | collective-permute-done | bytes 65568 | tf_op jit(solution)/shard_map/ppermute | solution.py:18
  159.1 1.5 maximum_select_fusion.1
  160.6 3.4 collective-permute-start.7
  164.6 1.9 fusion.67
  166.5 2.4 fusion.44
  169.2 1.2 collective-permute-done.2
  171.3 23.5 %collective-permute-done.3 = bf16[2,8,32,128]{3,2,1,0:T(8,128)(2,1)S(1)} collective-permute-done((bf16[2,8,32,128]{3,2,1,0:T(8,128)(2,1)S(1)}, bf16[2,8,32,128]{3,2,1,0:T(8,128)(2,1)S(1)}, u32[]{:S(2)}, u32[]{:S(2)}) %collective-permute-start.3) | collective-permute-done | bytes 131104 | tf_op jit(solution)/shard_map/ppermute | solution.py:29
  194.9 1.1 collective-permute-start.4
  196.0 6.9 %collective-permute-done.4 = bf16[4,8,32,128]{3,2,1,0:T(8,128)(2,1)S(1)} collective-permute-done((bf16[4,8,32,128]{3,2,1,0:T(8,128)(2,1)S(1)}, bf16[4,8,32,128]{3,2,1,0:T(8,128)(2,1)S(1)}, u32[]{:S(2)}, u32[]{:S(2)}) %collective-permute-start.4) | collective-permute-done | bytes 262176 | tf_op jit(solution)/shard_map/ppermute | solution.py:29
  202.9 2.0 maximum_select_fusion
  205.7 5.1 %fusion.1 = f32[512]{0:T(512)S(1)} fusion(bf16[512,8192]{1,0:T(8,128)(2,1)} %param.33), kind=kLoop, calls=%fused_computation.3 | loop fusion | flops 12582400 | bytes 8390656 | tf_op jit(solution)/shard_map/reduce_sum | solution.py:49
  211.5 3.2 constant_dynamic-slice_fusion
  214.8 2.7 collective-permute-done.9
  219.0 9.4 %collective-permute-done.10 = bf16[4,32,1280]{2,1,0:T(8,128)(2,1)S(1)} collective-permute-done((bf16[4,32,1280]{2,1,0:T(8,128)(2,1)S(1)}, bf16[4,32,1280]{2,1,0:T(8,128)(2,1)S(1)}, u32[]{:S(2)}, u32[]{:S(2)}) %collective-permute-start.10) | collective-permute-done | bytes 327712 | tf_op jit(solution)/shard_map/ppermute | solution.py:29
  228.8 19.3 %collective-permute-start.12 = (bf16[256,1,256]{2,0,1:T(8,128)(2,1)S(1)}, bf16[256,1,256]{2,0,1:T(8,128)(2,1)S(1)}, u32[]{:S(2)}, u32[]{:S(2)}) collective-permute-start(bf16[256,1,256]{2,0,1:T(8,128)(2,1)S(1)} %fusion.40), channel_id=1, source_target_pairs={{8,0},{16,8},{24,16},{32,24},{40,32},{48,40},{56,48},{64,56},{72,6... | collective-permute-start | bytes 393224 | tf_op jit(solution)/shard_map/ppermute | solution.py:18
  248.1 2.1 collective-permute-start.11
  250.6 6.5 %collective-permute-done.11 = bf16[256,1,256]{2,0,1:T(8,128)(2,1)S(1)} collective-permute-done((bf16[256,1,256]{2,0,1:T(8,128)(2,1)S(1)}, bf16[256,1,256]{2,0,1:T(8,128)(2,1)S(1)}, u32[]{:S(2)}, u32[]{:S(2)}) %collective-permute-start.11) | collective-permute-done | bytes 131104 | tf_op jit(solution)/shard_map/ppermute | solution.py:15
  257.1 12.3 %copy.51 = bf16[512,16,512]{0,2,1:T(8,128)(2,1)} copy(bf16[512,16,512]{2,0,1:T(8,128)(2,1)} %all-to-all-done) | data formatting | bytes 16777216 | tf_op jit(solution)/shard_map/all_to_all | solution.py:89
  269.4 10.4 %fusion.36 = bf16[512,512]{0,1:T(8,128)(2,1)S(1)} fusion(bf16[8192,512]{1,0:T(8,128)(2,1)} %all-gather.2.cloned.1.call-done, bf16[512,8192]{1,0:T(8,128)(2,1)} %param.33, f32[8192]{0:T(1024)S(1)} %copy-done.15, f32[512]{0:T(512)S(1)} %add_rsqrt_fusion, f32[512]{0:T(512)S(1)} %copy-done.16), kind=kOutput, calls=%fused_computation.42 | convolution fusion | flops 4312268800 | bytes 17338368 | tf_op jit(solution)/shard_map/dot_general | solution.py:148
  279.9 1.2 fusion.8
  281.0 1.4 fusion.11
  282.4 2.1 fusion.33
  284.5 10.2 %convolution_convert_fusion = bf16[512,8192]{1,0:T(8,128)(2,1)} fusion(bf16[512,512]{0,1:T(8,128)(2,1)S(1)} %bitcast.97, bf16[512,8192]{0,1:T(8,128)(2,1)} %bitcast.85), kind=kOutput, calls=%fused_computation.6 | convolution fusion | flops 4299161600 | bytes 17301504 | tf_op jit(solution)/shard_map/dot_general | solution.py:173
  294.7 49.3 %reduce-scatter.2.cloned.1.call-done = bf16[512,1024]{1,0:T(8,128)(2,1)} async-done(((bf16[512,8192]{1,0:T(8,128)(2,1)}), bf16[512,1024]{1,0:T(8,128)(2,1)}) %reduce-scatter.2.cloned.1.call-update) | async-done | bytes 1048592 | tf_op jit(solution)/shard_map/reduce_scatter | solution.py:178
  344.0 2.9 add_convert_fusion
  (88 shorter events, 9.3 us)
Async XLA Ops:
  7.2 14.0 %copy-start = (bf16[1280,128]{1,0:T(8,128)(2,1)S(1)}, bf16[1280,128]{1,0:T(8,128)(2,1)}, u32[]{:S(2)}) copy-start(bf16[1280,128]{1,0:T(8,128)(2,1)} %param.25) | copy-start | bytes 983044
  7.2 262.3 %all-gather.2.cloned.1.call-start = ((), (), s32[]{:S(2)}) async-start(), calls=%async_computation.2 | async-start | bytes 8912896 | tf_op jit(solution)/shard_map/all_gather | solution.py:150
  7.9 22.4 %collective-permute-start.5 = (bf16[1,128,1280]{2,1,0:T(8,128)(2,1)}, bf16[1,128,1280]{2,1,0:T(8,128)(2,1)}, u32[]{:S(2)}, u32[]{:S(2)}) collective-permute-start(bf16[1,128,1280]{2,1,0:T(8,128)(2,1)} %bitcast.91), channel_id=1, source_target_pairs={{0,1},{1,0},{2,3},{3,2},{4,5},{5,4},{6,7},{7,6},{8,9},{9,8},{10,11... | collective-permute-start | bytes 983048 | tf_op jit(solution)/shard_map/ppermute | solution.py:29
  13.1 7.2 %copy-start.2 = (bf16[256,1280]{1,0:T(8,128)(2,1)S(1)}, bf16[256,1280]{1,0:T(8,128)(2,1)}, u32[]{:S(2)}) copy-start(bf16[256,1280]{1,0:T(8,128)(2,1)} %param.20) | copy-start | bytes 1966084
  13.1 7.8 %copy-start.9 = (f32[1280]{0:T(1024)S(1)}, f32[1280]{0:T(1024)}, u32[]{:S(2)}) copy-start(f32[1280]{0:T(1024)} %param.22) | copy-start | bytes 15364
  13.1 7.8 %copy-start.10 = (f32[1280]{0:T(1024)S(1)}, f32[1280]{0:T(1024)}, u32[]{:S(2)}) copy-start(f32[1280]{0:T(1024)} %param.21) | copy-start | bytes 15364
  13.1 8.5 %copy-start.4 = (bf16[1280,128]{1,0:T(8,128)(2,1)S(1)}, bf16[1280,128]{1,0:T(8,128)(2,1)}, u32[]{:S(2)}) copy-start(bf16[1280,128]{1,0:T(8,128)(2,1)} %param.26) | copy-start | bytes 983044
  13.1 8.5 %copy-start.13 = (f32[128]{0:T(128)S(1)}, f32[128]{0:T(128)}, u32[]{:S(2)}) copy-start(f32[128]{0:T(128)} %param.27) | copy-start | bytes 1540
  13.1 16.8 %copy-start.5 = (bf16[1280,128]{1,0:T(8,128)(2,1)S(1)}, bf16[1280,128]{1,0:T(8,128)(2,1)}, u32[]{:S(2)}) copy-start(bf16[1280,128]{1,0:T(8,128)(2,1)} %param.23) | copy-start | bytes 983044
  13.1 16.8 %copy-start.14 = (f32[128]{0:T(128)S(1)}, f32[128]{0:T(128)}, u32[]{:S(2)}) copy-start(f32[128]{0:T(128)} %param.24) | copy-start | bytes 1540
  13.1 244.0 %all-to-all-start = ((bf16[512,16,512]{2,0,1:T(8,128)(2,1)}), bf16[512,16,512]{2,0,1:T(8,128)(2,1)}, u32[]{:S(2)}, u32[]{:S(2)}) async-start(bf16[512,16,512]{2,0,1:T(8,128)(2,1)} %tile.2), calls=%async_computation | async-start | bytes 16777216 | tf_op jit(solution)/shard_map/all_to_all | solution.py:89
  20.3 10.1 %copy-start.6 = (bf16[128,1280]{1,0:T(8,128)(2,1)S(1)}, bf16[128,1280]{1,0:T(8,128)(2,1)}, u32[]{:S(2)}) copy-start(bf16[128,1280]{1,0:T(8,128)(2,1)} %param.28) | copy-start | bytes 983044
  20.3 323.8 %reduce-scatter.2.cloned.1.call-start = ((), (), s32[]{:S(2)}) async-start(), calls=%async_computation.3 | async-start | bytes 9437184 | tf_op jit(solution)/shard_map/reduce_scatter | solution.py:178
  21.2 143.4 %copy-start.17 = (s32[2]{0:T(128)S(1)}, s32[2]{0:T(128)}, u32[]{:S(2)}) copy-start(s32[2]{0:T(128)} %param.30) | copy-start | bytes 28
  21.9 122.2 %collective-permute-start = (bf16[128,2,128]{2,0,1:T(8,128)(2,1)S(1)}, bf16[128,2,128]{2,0,1:T(8,128)(2,1)S(1)}, u32[]{:S(2)}, u32[]{:S(2)}) collective-permute-start(bf16[128,2,128]{2,0,1:T(8,128)(2,1)S(1)} %get-tuple-element.4), channel_id=1, source_target_pairs={{0,8},{8,16},{16,24},{24,32},{32,40},{40,48},{48,56},{56,64},{64,7... | collective-permute-start | bytes 196616 | tf_op jit(solution)/shard_map/ppermute | solution.py:15
  25.3 133.6 %collective-permute-start.1 = (bf16[128,2,128]{2,0,1:T(8,128)(2,1)S(1)}, bf16[128,2,128]{2,0,1:T(8,128)(2,1)S(1)}, u32[]{:S(2)}, u32[]{:S(2)}) collective-permute-start(bf16[128,2,128]{2,0,1:T(8,128)(2,1)S(1)} %get-tuple-element.5), channel_id=1, source_target_pairs={{8,0},{16,8},{24,16},{32,24},{40,32},{48,40},{56,48},{64,56},{72,6... | collective-permute-start | bytes 196616 | tf_op jit(solution)/shard_map/ppermute | solution.py:18
  31.5 127.6 %collective-permute-start.6 = (bf16[2,128,1280]{2,1,0:T(8,128)(2,1)S(1)}, bf16[2,128,1280]{2,1,0:T(8,128)(2,1)}, u32[]{:S(2)}, u32[]{:S(2)}) collective-permute-start(bf16[2,128,1280]{2,1,0:T(8,128)(2,1)S(1)} %maximum_select_fusion.2), channel_id=1, source_target_pairs={{0,2},{1,3},{2,0},{3,1},{4,6},{5,7},{6,4},{7,5},{8,10},{9,11},{10,... | collective-permute-start | bytes 1966088 | tf_op jit(solution)/shard_map/ppermute | solution.py:29
  160.6 42.3 %collective-permute-start.7 = (bf16[4,128,1280]{2,1,0:T(8,128)(2,1)S(1)}, bf16[4,128,1280]{2,1,0:T(8,128)(2,1)}, u32[]{:S(2)}, u32[]{:S(2)}) collective-permute-start(bf16[4,128,1280]{2,1,0:T(8,128)(2,1)S(1)} %maximum_select_fusion.1), channel_id=1, source_target_pairs={{0,4},{1,5},{2,6},{3,7},{4,0},{5,1},{6,2},{7,3},{8,12},{9,13},{10,... | collective-permute-start | bytes 3932168 | tf_op jit(solution)/shard_map/ppermute | solution.py:29
  166.5 38.5 %copy-start.7 = (f32[1280]{0:T(1024)S(1)}, f32[1280]{0:T(1024)}, u32[]{:S(2)}) copy-start(f32[1280]{0:T(1024)} %param.29) | copy-start | bytes 15364
  169.1 1.3 collective-permute-start.2
  170.5 24.4 %collective-permute-start.3 = (bf16[2,8,32,128]{3,2,1,0:T(8,128)(2,1)S(1)}, bf16[2,8,32,128]{3,2,1,0:T(8,128)(2,1)S(1)}, u32[]{:S(2)}, u32[]{:S(2)}) collective-permute-start(bf16[2,8,32,128]{3,2,1,0:T(8,128)(2,1)S(1)} %maximum_select_fusion.7), channel_id=1, source_target_pairs={{0,2},{1,3},{2,0},{3,1},{4,6},{5,7},{6,4},{7,5},{8,10},{9,11},{10,... | collective-permute-start | bytes 393224 | tf_op jit(solution)/shard_map/ppermute | solution.py:29
  194.9 8.0 %collective-permute-start.4 = (bf16[4,8,32,128]{3,2,1,0:T(8,128)(2,1)S(1)}, bf16[4,8,32,128]{3,2,1,0:T(8,128)(2,1)S(1)}, u32[]{:S(2)}, u32[]{:S(2)}) collective-permute-start(bf16[4,8,32,128]{3,2,1,0:T(8,128)(2,1)S(1)} %maximum_select_fusion.5), channel_id=1, source_target_pairs={{0,4},{1,5},{2,6},{3,7},{4,0},{5,1},{6,2},{7,3},{8,12},{9,13},{10,... | collective-permute-start | bytes 786440 | tf_op jit(solution)/shard_map/ppermute | solution.py:29
  205.6 9.2 %copy-start.3 = (bf16[32,1280]{1,0:T(8,128)(2,1)}, bf16[32,1280]{1,0:T(8,128)(2,1)S(1)}, u32[]{:S(2)}) copy-start(bf16[32,1280]{1,0:T(8,128)(2,1)S(1)} %fusion.15) | copy-start | bytes 245764
  205.6 13.0 %copy-start.11 = (f32[8,128]{1,0:T(8,128)S(1)}, f32[8,128]{1,0:T(8,128)}, u32[]{:S(2)}) copy-start(f32[8,128]{1,0:T(8,128)} %param.32) | copy-start | bytes 12292
  205.6 5.2 %collective-permute-start.8 = (bf16[1,32,1280]{2,1,0:T(8,128)(2,1)S(1)}, bf16[1,32,1280]{2,1,0:T(8,128)(2,1)S(1)}, u32[]{:S(2)}, u32[]{:S(2)}) collective-permute-start(bf16[1,32,1280]{2,1,0:T(8,128)(2,1)S(1)} %bitcast.89), channel_id=1, source_target_pairs={{0,1},{1,0},{2,3},{3,2},{4,5},{5,4},{6,7},{7,6},{8,9},{9,8},{10,11... | collective-permute-start | bytes 245768 | tf_op jit(solution)/shard_map/ppermute | solution.py:29
  210.8 6.7 %collective-permute-start.9 = (bf16[2,32,1280]{2,1,0:T(8,128)(2,1)S(1)}, bf16[2,32,1280]{2,1,0:T(8,128)(2,1)S(1)}, u32[]{:S(2)}, u32[]{:S(2)}) collective-permute-start(bf16[2,32,1280]{2,1,0:T(8,128)(2,1)S(1)} %maximum_select_fusion.6), channel_id=1, source_target_pairs={{0,2},{1,3},{2,0},{3,1},{4,6},{5,7},{6,4},{7,5},{8,10},{9,11},{10,... | collective-permute-start | bytes 491528 | tf_op jit(solution)/shard_map/ppermute | solution.py:29
  217.5 10.8 %collective-permute-start.10 = (bf16[4,32,1280]{2,1,0:T(8,128)(2,1)S(1)}, bf16[4,32,1280]{2,1,0:T(8,128)(2,1)S(1)}, u32[]{:S(2)}, u32[]{:S(2)}) collective-permute-start(bf16[4,32,1280]{2,1,0:T(8,128)(2,1)S(1)} %maximum_select_fusion.4), channel_id=1, source_target_pairs={{0,4},{1,5},{2,6},{3,7},{4,0},{5,1},{6,2},{7,3},{8,12},{9,13},{10,... | collective-permute-start | bytes 983048 | tf_op jit(solution)/shard_map/ppermute | solution.py:29
  228.8 21.8 %collective-permute-start.12 = (bf16[256,1,256]{2,0,1:T(8,128)(2,1)S(1)}, bf16[256,1,256]{2,0,1:T(8,128)(2,1)S(1)}, u32[]{:S(2)}, u32[]{:S(2)}) collective-permute-start(bf16[256,1,256]{2,0,1:T(8,128)(2,1)S(1)} %fusion.40), channel_id=1, source_target_pairs={{8,0},{16,8},{24,16},{32,24},{40,32},{48,40},{56,48},{64,56},{72,6... | collective-permute-start | bytes 393224 | tf_op jit(solution)/shard_map/ppermute | solution.py:18
  248.1 9.0 %collective-permute-start.11 = (bf16[256,1,256]{2,0,1:T(8,128)(2,1)S(1)}, bf16[256,1,256]{2,0,1:T(8,128)(2,1)S(1)}, u32[]{:S(2)}, u32[]{:S(2)}) collective-permute-start(bf16[256,1,256]{2,0,1:T(8,128)(2,1)S(1)} %fusion.40), channel_id=1, source_target_pairs={{0,8},{8,16},{16,24},{24,32},{32,40},{40,48},{48,56},{56,64},{64,7... | collective-permute-start | bytes 393224 | tf_op jit(solution)/shard_map/ppermute | solution.py:15
  257.1 12.3 %copy-start.15 = (f32[8192]{0:T(1024)S(1)}, f32[8192]{0:T(1024)}, u32[]{:S(2)}) copy-start(f32[8192]{0:T(1024)} %param.34) | copy-start | bytes 98308
  257.1 12.3 %copy-start.16 = (f32[512]{0:T(512)S(1)}, f32[512]{0:T(512)}, u32[]{:S(2)}) copy-start(f32[512]{0:T(512)} %param.36) | copy-start | bytes 6148
  294.7 52.2 %copy-start.1 = (bf16[1280,128]{1,0:T(8,128)(2,1)S(1)}, bf16[1280,128]{1,0:T(8,128)(2,1)}, u32[]{:S(2)}) copy-start(bf16[1280,128]{1,0:T(8,128)(2,1)} %param.25) | copy-start | bytes 983044
  (2 other events, 13.1 us)
Sparse Core Ops, SparseCore 0:
  10.1 172.3 all-gather.1
  294.9 49.1 reduce-scatter.1

commit v4 on v2

--- a/solution.py
+++ b/solution.py
@@ -35,6 +35,27 @@
         )
         bit *= 2
     return gathered
+
+
+def heads_ring_gather(block, axis):
+    count = lax.axis_size(axis)
+    ring = count // 2
+    index = lax.axis_index(axis)
+    chip = index // 2
+    core = index % 2
+    swap = [(i, i ^ 1) for i in range(count)]
+    sibling = lax.ppermute(block, axis, swap)
+    own = jnp.where(core == 0, jnp.stack([block, sibling]), jnp.stack([sibling, block]))
+    step = []
+    for i in range(count):
+        direction = 1 if i % 2 == 0 else -1
+        step.append((i, ((i // 2 + direction) % ring) * 2 + i % 2))
+    near = lax.ppermute(own, axis, step)
+    far = lax.ppermute(near, axis, step)
+    other = lax.ppermute(near, axis, swap)
+    sign = 1 - 2 * core
+    owners = [chip, (chip - sign) % ring, (chip + 2) % ring, (chip + sign) % ring]
+    return [own, near, far, other], owners
 
 
 def layer_norm(values, gain, shift):
@@ -165,14 +186,29 @@
         "rgqk,kgd->rgqd", dec_weights, band_values, preferred_element_type=jnp.float32
     )
     dec_context = dec_context.astype(jnp.bfloat16).reshape(rows_dev, query_width)
-    dec_term = jnp.dot(
-        dec_context,
-        lax.all_gather(dec_wo, "seq", axis=1, tiled=True),
-        preferred_element_type=jnp.float32,
-    )
-    summed = lax.psum_scatter(
-        dec_term.astype(jnp.bfloat16), "heads", scatter_dimension=1, tiled=True
-    ).astype(jnp.float32)
+    ratio = seq_count // head_count
+    set_rows = dec_wo.shape[0]
+    block_cols = dec_wo.shape[1]
+    flat = [(c, j) for c in range(seq_count) for j in range(head_count)]
+    regroup = [
+        (c * head_count + j, (ratio * j + c % ratio) * head_count + c // ratio) for c, j in flat
+    ]
+    piece = lax.ppermute(dec_wo, ("seq", "heads"), regroup)
+    column_weight = lax.all_gather(piece, "seq", axis=0, tiled=False).reshape(
+        head_count, ratio, set_rows, block_cols
+    )
+    pieces, owners = heads_ring_gather(dec_context, "heads")
+    total = jnp.zeros((rows_dev, ratio, block_cols), jnp.float32)
+    for held, owner in zip(pieces, owners):
+        for offset in range(held.shape[0]):
+            weight_set = lax.dynamic_index_in_dim(
+                column_weight, owner * held.shape[0] + offset, 0, keepdims=False
+            )
+            term = jnp.einsum(
+                "rk,bkc->rbc", held[offset], weight_set, preferred_element_type=jnp.float32
+            )
+            total = total + term.astype(jnp.bfloat16).astype(jnp.float32)
+    summed = total.reshape(rows_dev, ratio * block_cols)
     col_share = model_width // head_count
     own_text = lax.dynamic_slice_in_dim(text, head_index * col_share, col_share, 1)
     dec_out = (own_text.astype(jnp.float32) + summed).astype(jnp.bfloat16)

time: 236 us -> 202 us (0.86)
  waiting for transfers between devices: 132 us -> 88.9 us
  matrix products: 34.1 us -> 39.1 us
  local copies, waits for them, and re-layouts: 9.01 us -> 13.9 us
    ppermute x0 -> x5, waiting for transfers between devices: none -> 53.5 us  [the longest x1 27.9 us: shards(): piece = lax.ppermute(dec_wo, ('seq', 'heads'), regroup)]
    reduce_scatter x1 -> x0, waiting for transfers between devices: 52.4 us -> none  [shards(): lax.psum_scatter(dec_term.astype(jnp.bfloat16), 'heads', scatter_dimensio...]
    all_gather x1, waiting for transfers between devices: 43.1 us -> 0.1 us  [shards(): lax.all_gather(piece, 'seq', axis=0, tiled=False)]
    dot_general x1 -> x8, matrix products: 10.1 us -> 14.5 us  [shards(): jnp.einsum('rk,bkc->rbc', held[offset], weight_set, preferred_element_typ...]
    ppermute x0 -> x5, starting transfers between devices: none -> 4.36 us  [the longest x1 3.56 us: shards(): piece = lax.ppermute(dec_wo, ('seq', 'heads'), regroup)]
    ppermute x3, starting transfers between devices: 5.01 us -> 0.79 us  [heads_gather(): other = lax.ppermute(gathered, axis, [(i, i ^ bit) for i in range(count)])]
    unnamed x27 -> x45, local copies, waits for them, and re-layouts: 7.23 us -> 9.71 us
    ppermute x3, waiting for transfers between devices: 8.28 us -> 10.7 us  [heads_gather(): other = lax.ppermute(gathered, axis, [(i, i ^ bit) for i in range(count)])]
  transfers between devices with their start and end apart: 12 -> 16, of which waited for: 7 -> 10; matrix products, arithmetic and copies ran while one was open for 20% -> 29% of each run, Pallas kernels for 0% -> 0%
where the time goes in v4:
time: 202 us; the launch traced here: 201 us
  waiting for transfers between devices  88.9 us (44%)
  matrix products  39.1 us (19%)
  starting transfers between devices  26.8 us (13%)
  other arithmetic  17.4 us (9%)
  between operations  14.6 us (7%)
  local copies, waits for them, and re-layouts  13.9 us (7%)
    ppermute x1, waiting for transfers between devices, shards(): piece = lax.ppermute(dec_wo, ('seq', 'heads'), regroup)  27.9 us
    ppermute x1, waiting for transfers between devices, heads_ring_gather(): near = lax.ppermute(own, axis, step)  15.4 us
    dot_general x8, matrix products, shards(): jnp.einsum('rk,bkc->rbc', held[offset], weight_set, preferred_element_typ...  14.5 us
    all_to_all x1, waiting for transfers between devices, shards(): context_share = lax.all_to_all(enc_context, 'heads', 0, 1, tiled=True)  12.4 us
    ppermute x3, waiting for transfers between devices, heads_gather(): other = lax.ppermute(gathered, axis, [(i, i ^ bit) for i in range(count)])  10.7 us
    dot_general x1, matrix products, shards(): jnp.dot(normed, lax.all_gather(dec_wq, 'seq', axis=0, tiled=True), prefer...  10.6 us
    unnamed x45, local copies, waits for them, and re-layouts  9.71 us
    ppermute x1, waiting for transfers between devices, heads_ring_gather(): far = lax.ppermute(near, axis, step)  8.48 us
  transfers between devices with their start and end apart: 16, of which 10 were waited for; matrix products, arithmetic and copies ran while one was open for 29% of the time, Pallas kernels for 0%

profile of v4, /device:TPU:96, one launch (start us, length us, event | category | flops | bytes accessed | tf_op | source)
XLA Modules:
  0.0 200.8 jit_solution(2329025166263068531)
XLA Ops:
  8.0 3.6 %collective-permute-start.8 = (bf16[512,512]{1,0:T(8,128)(2,1)}, bf16[512,512]{1,0:T(8,128)(2,1)S(1)}, u32[]{:S(2)}, u32[]{:S(2)}) collective-permute-start(bf16[512,512]{1,0:T(8,128)(2,1)} %param.37), channel_id=1, source_target_pairs={{0,0},{1,16},{2,32},{3,48},{4,64},{5,80},{6,96},{7,112},{8,8},{9,2... | collective-permute-start | bytes 1572872 | tf_op jit(solution)/shard_map/ppermute | solution.py:196
  11.6 27.9 %collective-permute-done.8 = bf16[512,512]{1,0:T(8,128)(2,1)S(1)} collective-permute-done((bf16[512,512]{1,0:T(8,128)(2,1)}, bf16[512,512]{1,0:T(8,128)(2,1)S(1)}, u32[]{:S(2)}, u32[]{:S(2)}) %collective-permute-start.8) | collective-permute-done | bytes 524320 | tf_op jit(solution)/shard_map/ppermute | solution.py:196
  41.7 1.4 fusion.36
  44.9 3.4 %collective-permute-start = (bf16[128,2,128]{2,0,1:T(8,128)(2,1)S(1)}, bf16[128,2,128]{2,0,1:T(8,128)(2,1)S(1)}, u32[]{:S(2)}, u32[]{:S(2)}) collective-permute-start(bf16[128,2,128]{2,0,1:T(8,128)(2,1)S(1)} %get-tuple-element.4), channel_id=1, source_target_pairs={{0,8},{8,16},{16,24},{24,32},{32,40},{40,48},{48,56},{56,64},{64,7... | collective-permute-start | bytes 196616 | tf_op jit(solution)/shard_map/ppermute | solution.py:15
  48.3 4.6 %collective-permute-start.1 = (bf16[128,2,128]{2,0,1:T(8,128)(2,1)S(1)}, bf16[128,2,128]{2,0,1:T(8,128)(2,1)}, u32[]{:S(2)}, u32[]{:S(2)}) collective-permute-start(bf16[128,2,128]{2,0,1:T(8,128)(2,1)S(1)} %get-tuple-element.5), channel_id=1, source_target_pairs={{8,0},{16,8},{24,16},{32,24},{40,32},{48,40},{56,48},{64,56},{72,6... | collective-permute-start | bytes 196616 | tf_op jit(solution)/shard_map/ppermute | solution.py:18
  54.3 5.8 %fusion.1 = f32[512]{0:T(512)S(1)} fusion(bf16[512,8192]{1,0:T(8,128)(2,1)} %param.33), kind=kLoop, calls=%fused_computation.3 | loop fusion | flops 12582400 | bytes 8390656 | tf_op jit(solution)/shard_map/reduce_sum | solution.py:70
  60.1 10.7 %collective-permute-done.3 = bf16[2,128,1280]{2,1,0:T(8,128)(2,1)} collective-permute-done((bf16[2,128,1280]{2,1,0:T(8,128)(2,1)S(1)}, bf16[2,128,1280]{2,1,0:T(8,128)(2,1)}, u32[]{:S(2)}, u32[]{:S(2)}) %collective-permute-start.3) | collective-permute-done | bytes 655392 | tf_op jit(solution)/shard_map/ppermute | solution.py:29
  70.8 1.5 maximum_select_fusion.10
  72.9 7.2 %copy.92 = bf16[160,8,8,256]{3,1,2,0:T(8,128)(2,1)} copy(bf16[160,8,8,256]{3,2,1,0:T(8,128)(2,1)} %bitcast.159) | data formatting | bytes 10485760
  84.0 2.8 %fusion.52 = bf16[256,2,64]{0,2,1:T(8,128)(2,1)S(1)} fusion(bf16[512,2,64]{0,2,1:T(8,128)(2,1)S(1)} %bitcast.172, f32[2,256]{1,0:T(2,128)S(1)} %fusion.97, f32[2,256,512]{2,1,0:T(8,128)} %copy-done.3, s32[256,512]{1,0:T(8,128)S(1)} %subtract_abs_fusion, s32[2]{0:T(128)S(1)} %copy-done.20, pred[512]{0:T(512)(128)(4,1)S(1)} %compare_and_fusion.3), kind=kOutput, calls=%fused_computation.68 | convolution fusion | flops 35947520 | bytes 1772040 | tf_op jit(solution)/shard_map/hqk,khd->qhd/dot_general | solution.py:133
  87.7 4.3 %all-to-all-start = ((bf16[8,32,128]{2,1,0:T(8,128)(2,1)}), bf16[8,32,128]{2,1,0:T(8,128)(2,1)S(1)}, u32[]{:S(2)}, u32[]{:S(2)}) async-start(bf16[8,32,128]{2,1,0:T(8,128)(2,1)} %all_to_all.24), calls=%async_computation | async-start | bytes 131072 | tf_op jit(solution)/shard_map/all_to_all | solution.py:139
  92.0 12.4 %all-to-all-done = bf16[8,32,128]{2,1,0:T(8,128)(2,1)S(1)} async-done(((bf16[8,32,128]{2,1,0:T(8,128)(2,1)}), bf16[8,32,128]{2,1,0:T(8,128)(2,1)S(1)}, u32[]{:S(2)}, u32[]{:S(2)}) %all-to-all-start) | async-done | bytes 65568 | tf_op jit(solution)/shard_map/all_to_all | solution.py:139
  104.4 2.5 %fusion.25 = bf16[32,1280]{1,0:T(8,128)(2,1)S(1)} fusion(bf16[4,128,1280]{2,1,0:T(8,128)(2,1)S(1)} %maximum_select_fusion.10, bf16[4,128,1280]{2,1,0:T(8,128)(2,1)} %collective-permute-done.4, pred[]{:T(512)S(6)} %ne.33, f32[1280]{0:T(1024)S(1)} %copy-done.18, bf16[256,1280]{1,0:T(8,128)(2,1)S(1)} %copy-done.2, s32[]{:T(128)S(6)} %select_n.102, ...), kind=kOutput, calls=%fused_computation.31 | convolution fusion | flops 87982080 | bytes 2855941 | tf_op jit(solution)/shard_map/dot_general | solution.py:140
  106.9 3.5 %fusion.24 = bf16[32,2048]{1,0:T(8,128)(2,1)S(1)} fusion(bf16[32,1280]{1,0:T(8,128)(2,1)S(1)} %fusion.25, bf16[1280,2048]{1,0:T(8,128)(2,1)} %bitcast.157, f32[2048]{0:T(1024)S(1)} %bitcast.181), kind=kOutput, calls=%fused_computation.30 | convolution fusion | flops 167903232 | bytes 5464064 | tf_op jit(solution)/shard_map/dot_general | solution.py:149
  111.1 3.4 %all-to-all-start.1 = ((bf16[32,8,256]{2,0,1:T(8,128)(2,1)}), bf16[32,8,256]{2,0,1:T(8,128)(2,1)S(1)}, u32[]{:S(2)}, u32[]{:S(2)}) async-start(bf16[32,8,256]{2,0,1:T(8,128)(2,1)} %bitcast.156), calls=%async_computation.1 | async-start | bytes 262144 | tf_op jit(solution)/shard_map/all_to_all | solution.py:156
  114.9 5.6 %all-to-all-done.1 = bf16[32,8,256]{2,0,1:T(8,128)(2,1)S(1)} async-done(((bf16[32,8,256]{2,0,1:T(8,128)(2,1)}), bf16[32,8,256]{2,0,1:T(8,128)(2,1)S(1)}, u32[]{:S(2)}, u32[]{:S(2)}) %all-to-all-start.1) | async-done | bytes 131104 | tf_op jit(solution)/shard_map/all_to_all | solution.py:156
  120.5 2.7 %collective-permute-start.6 = (bf16[256,1,256]{2,0,1:T(8,128)(2,1)S(1)}, bf16[256,1,256]{2,0,1:T(8,128)(2,1)S(1)}, u32[]{:S(2)}, u32[]{:S(2)}) collective-permute-start(bf16[256,1,256]{2,0,1:T(8,128)(2,1)S(1)} %bitcast.166), channel_id=1, source_target_pairs={{8,0},{16,8},{24,16},{32,24},{40,32},{48,40},{56,48},{64,56},{72,6... | collective-permute-start | bytes 393224 | tf_op jit(solution)/shard_map/ppermute | solution.py:18
  123.2 3.3 %collective-permute-start.5 = (bf16[256,1,256]{2,0,1:T(8,128)(2,1)S(1)}, bf16[256,1,256]{2,0,1:T(8,128)(2,1)S(1)}, u32[]{:S(2)}, u32[]{:S(2)}) collective-permute-start(bf16[256,1,256]{2,0,1:T(8,128)(2,1)S(1)} %bitcast.167), channel_id=1, source_target_pairs={{0,8},{8,16},{16,24},{24,32},{32,40},{40,48},{48,56},{56,64},{64,7... | collective-permute-start | bytes 393224 | tf_op jit(solution)/shard_map/ppermute | solution.py:15
  127.4 4.9 %collective-permute-done.5 = bf16[256,1,256]{2,0,1:T(8,128)(2,1)S(1)} collective-permute-done((bf16[256,1,256]{2,0,1:T(8,128)(2,1)S(1)}, bf16[256,1,256]{2,0,1:T(8,128)(2,1)S(1)}, u32[]{:S(2)}, u32[]{:S(2)}) %collective-permute-start.5) | collective-permute-done | bytes 131104 | tf_op jit(solution)/shard_map/ppermute | solution.py:15
  132.5 10.6 %fusion.46 = bf16[512,512]{0,1:T(8,128)(2,1)S(1)} fusion(bf16[8192,512]{1,0:T(8,128)(2,1)} %all-gather.4.cloned.1.call-done, bf16[512,8192]{1,0:T(8,128)(2,1)} %param.33, f32[8192]{0:T(1024)S(1)} %copy-done.17, f32[512]{0:T(512)S(1)} %add_rsqrt_fusion, f32[512]{0:T(512)S(1)} %copy-done.19), kind=kOutput, calls=%fused_computation.60 | convolution fusion | flops 4312268800 | bytes 17338368 | tf_op jit(solution)/shard_map/dot_general | solution.py:164
  145.6 2.1 %fusion.43 = bf16[128,512,4]{1,0,2:T(8,128)(2,1)S(1)} fusion(f32[512,4]{0,1:T(4,128)S(1)} %fusion.11, f32[512,4]{0,1:T(4,128)S(1)} %get-tuple-element.6, f32[768,512,4]{1,0,2:T(8,128)S(1)} %get-tuple-element.7, pred[512,768]{0,1:T(8,128)(4,1)S(1)} %compare_and_fusion, bf16[768,1,256]{2,0,1:T(8,128)(2,1)S(1)} %pad_maximum_fusion), kind=kOutput, calls=%fused_computation.59 | convolution fusion | flops 410779648 | bytes 7421952 | tf_op jit(solution)/shard_map/rgqk,kgd->rgqd/dot_general | solution.py:185
  148.2 1.7 collective-permute-done.7
  150.7 15.4 %collective-permute-done.9 = bf16[2,512,512]{2,1,0:T(8,128)(2,1)S(1)} collective-permute-done((bf16[2,512,512]{2,1,0:T(8,128)(2,1)S(1)}, bf16[2,512,512]{2,1,0:T(8,128)(2,1)S(1)}, u32[]{:S(2)}, u32[]{:S(2)}) %collective-permute-start.9) | collective-permute-done | bytes 1048608 | tf_op jit(solution)/shard_map/ppermute | solution.py:53
  166.2 2.1 %convolution_convert_fusion.6 = bf16[512,2,512]{0,2,1:T(8,128)(2,1)S(1)} fusion(bf16[8,2,512,512]{3,2,1,0:T(8,128)(2,1)} %bitcast.173, s32[]{:T(128)S(6)} %select_n.119, bf16[2,512,512]{2,1,0:T(8,128)(2,1)S(1)} %maximum_select_fusion.11), kind=kOutput, calls=%fused_computation.45 | convolution fusion | flops 537395200 | bytes 2621444 | tf_op jit(solution)/shard_map/rk,bkc->rbc/dot_general | solution.py:207
  168.4 2.5 %convolution_convert_fusion.7 = bf16[512,2,512]{0,2,1:T(8,128)(2,1)S(1)} fusion(bf16[8,2,512,512]{3,2,1,0:T(8,128)(2,1)} %bitcast.174, s32[]{:T(128)S(6)} %select_n.118, bf16[2,512,512]{2,1,0:T(8,128)(2,1)S(1)} %maximum_select_fusion.11), kind=kOutput, calls=%fused_computation.46 | convolution fusion | flops 537395200 | bytes 2621444 | tf_op jit(solution)/shard_map/rk,bkc->rbc/dot_general | solution.py:207
  171.0 2.0 convolution_convert_fusion.4
  173.7 8.5 %collective-permute-done.10 = bf16[2,512,512]{2,1,0:T(8,128)(2,1)} collective-permute-done((bf16[2,512,512]{2,1,0:T(8,128)(2,1)S(1)}, bf16[2,512,512]{2,1,0:T(8,128)(2,1)}, u32[]{:S(2)}, u32[]{:S(2)}) %collective-permute-start.10) | collective-permute-done | bytes 1048608 | tf_op jit(solution)/shard_map/ppermute | solution.py:54
  182.2 1.8 convolution_convert_fusion.2
  184.0 1.8 convolution_convert_fusion.3
  186.6 2.8 %convert_add_fusion = f32[512,2,512]{0,2,1:T(8,128)} fusion(bf16[512,2,512]{0,2,1:T(8,128)(2,1)S(1)} %convolution_convert_fusion.1, bf16[512,2,512]{0,2,1:T(8,128)(2,1)S(1)} %convolution_convert_fusion.2, bf16[512,2,512]{0,2,1:T(8,128)(2,1)S(1)} %convolution_convert_fusion.3, bf16[512,2,512]{0,2,1:T(8,128)(2,1)S(1)} %convolution_convert_fusion.4, ...), kind=kOutput, calls=%fused_computation.33 | convolution fusion | flops 545259520 | bytes 11010052 | tf_op jit(solution)/shard_map/rk,bkc->rbc/dot_general | solution.py:207
  189.4 2.0 copy.78
  191.4 2.6 %add_convert_fusion = bf16[512,1024]{1,0:T(8,128)(2,1)} fusion(f32[512,1024]{1,0:T(8,128)S(1)} %copy.78, bf16[512,8192]{1,0:T(8,128)(2,1)} %param.33, s32[]{:T(128)S(6)} %select_n.111), kind=kLoop, calls=%fused_computation.32 | loop fusion | flops 1572864 | bytes 4194308 | tf_op jit(solution)/shard_map/convert_element_type | solution.py:214
  (97 shorter events, 18.9 us)
Async XLA Ops:
  7.2 37.0 %copy-start = (bf16[1280,128]{1,0:T(8,128)(2,1)S(1)}, bf16[1280,128]{1,0:T(8,128)(2,1)}, u32[]{:S(2)}) copy-start(bf16[1280,128]{1,0:T(8,128)(2,1)} %param.25) | copy-start | bytes 983044
  7.2 36.0 %copy-start.2 = (bf16[256,1280]{1,0:T(8,128)(2,1)S(1)}, bf16[256,1280]{1,0:T(8,128)(2,1)}, u32[]{:S(2)}) copy-start(bf16[256,1280]{1,0:T(8,128)(2,1)} %param.20) | copy-start | bytes 1966084
  7.2 37.3 %copy-start.15 = (f32[128]{0:T(128)S(1)}, f32[128]{0:T(128)}, u32[]{:S(2)}) copy-start(f32[128]{0:T(128)} %param.27) | copy-start | bytes 1540
  7.2 37.3 %copy-start.5 = (bf16[1280,128]{1,0:T(8,128)(2,1)S(1)}, bf16[1280,128]{1,0:T(8,128)(2,1)}, u32[]{:S(2)}) copy-start(bf16[1280,128]{1,0:T(8,128)(2,1)} %param.26) | copy-start | bytes 983044
  7.2 125.2 %all-gather.4.cloned.1.call-start = ((), (), s32[]{:S(2)}) async-start(), calls=%async_computation.2 | async-start | bytes 8912896 | tf_op jit(solution)/shard_map/all_gather | solution.py:166
  7.9 158.3 %all-gather.6.cloned.1.call-start = ((), (), s32[]{:S(2)}) async-start(), calls=%async_computation.3 | async-start | bytes 8912896 | tf_op jit(solution)/shard_map/all_gather | solution.py:197
  8.0 31.5 %collective-permute-start.8 = (bf16[512,512]{1,0:T(8,128)(2,1)}, bf16[512,512]{1,0:T(8,128)(2,1)S(1)}, u32[]{:S(2)}, u32[]{:S(2)}) collective-permute-start(bf16[512,512]{1,0:T(8,128)(2,1)} %param.37), channel_id=1, source_target_pairs={{0,0},{1,16},{2,32},{3,48},{4,64},{5,80},{6,96},{7,112},{8,8},{9,2... | collective-permute-start | bytes 1572872 | tf_op jit(solution)/shard_map/ppermute | solution.py:196
  40.3 12.6 %copy-start.6 = (bf16[1280,128]{1,0:T(8,128)(2,1)S(1)}, bf16[1280,128]{1,0:T(8,128)(2,1)}, u32[]{:S(2)}) copy-start(bf16[1280,128]{1,0:T(8,128)(2,1)} %param.23) | copy-start | bytes 983044
  40.3 12.6 %copy-start.16 = (f32[128]{0:T(128)S(1)}, f32[128]{0:T(128)}, u32[]{:S(2)}) copy-start(f32[128]{0:T(128)} %param.24) | copy-start | bytes 1540
  40.3 13.6 %collective-permute-start.2 = (bf16[1,128,1280]{2,1,0:T(8,128)(2,1)}, bf16[1,128,1280]{2,1,0:T(8,128)(2,1)S(1)}, u32[]{:S(2)}, u32[]{:S(2)}) collective-permute-start(bf16[1,128,1280]{2,1,0:T(8,128)(2,1)} %bitcast.169), channel_id=1, source_target_pairs={{0,1},{1,0},{2,3},{3,2},{4,5},{5,4},{6,7},{7,6},{8,9},{9,8},{10,11... | collective-permute-start | bytes 983048 | tf_op jit(solution)/shard_map/ppermute | solution.py:29
  41.7 12.2 %copy-start.7 = (bf16[128,1280]{1,0:T(8,128)(2,1)S(1)}, bf16[128,1280]{1,0:T(8,128)(2,1)}, u32[]{:S(2)}) copy-start(bf16[128,1280]{1,0:T(8,128)(2,1)} %param.28) | copy-start | bytes 983044
  44.9 35.3 %collective-permute-start = (bf16[128,2,128]{2,0,1:T(8,128)(2,1)S(1)}, bf16[128,2,128]{2,0,1:T(8,128)(2,1)S(1)}, u32[]{:S(2)}, u32[]{:S(2)}) collective-permute-start(bf16[128,2,128]{2,0,1:T(8,128)(2,1)S(1)} %get-tuple-element.4), channel_id=1, source_target_pairs={{0,8},{8,16},{16,24},{24,32},{32,40},{40,48},{48,56},{56,64},{64,7... | collective-permute-start | bytes 196616 | tf_op jit(solution)/shard_map/ppermute | solution.py:15
  48.3 32.6 %collective-permute-start.1 = (bf16[128,2,128]{2,0,1:T(8,128)(2,1)S(1)}, bf16[128,2,128]{2,0,1:T(8,128)(2,1)}, u32[]{:S(2)}, u32[]{:S(2)}) collective-permute-start(bf16[128,2,128]{2,0,1:T(8,128)(2,1)S(1)} %get-tuple-element.5), channel_id=1, source_target_pairs={{8,0},{16,8},{24,16},{32,24},{40,32},{48,40},{56,48},{64,56},{72,6... | collective-permute-start | bytes 196616 | tf_op jit(solution)/shard_map/ppermute | solution.py:18
  54.0 16.8 %collective-permute-start.3 = (bf16[2,128,1280]{2,1,0:T(8,128)(2,1)S(1)}, bf16[2,128,1280]{2,1,0:T(8,128)(2,1)}, u32[]{:S(2)}, u32[]{:S(2)}) collective-permute-start(bf16[2,128,1280]{2,1,0:T(8,128)(2,1)S(1)} %maximum_select_fusion.12), channel_id=1, source_target_pairs={{0,2},{1,3},{2,0},{3,1},{4,6},{5,7},{6,4},{7,5},{8,10},{9,11},{10,... | collective-permute-start | bytes 1966088 | tf_op jit(solution)/shard_map/ppermute | solution.py:29
  60.1 12.8 %copy-start.13 = (f32[8,128]{1,0:T(8,128)S(1)}, f32[8,128]{1,0:T(8,128)}, u32[]{:S(2)}) copy-start(f32[8,128]{1,0:T(8,128)} %param.32) | copy-start | bytes 12292
  72.3 32.1 %collective-permute-start.4 = (bf16[4,128,1280]{2,1,0:T(8,128)(2,1)S(1)}, bf16[4,128,1280]{2,1,0:T(8,128)(2,1)}, u32[]{:S(2)}, u32[]{:S(2)}) collective-permute-start(bf16[4,128,1280]{2,1,0:T(8,128)(2,1)S(1)} %maximum_select_fusion.10), channel_id=1, source_target_pairs={{0,4},{1,5},{2,6},{3,7},{4,0},{5,1},{6,2},{7,3},{8,12},{9,13},{10,... | collective-permute-start | bytes 3932168 | tf_op jit(solution)/shard_map/ppermute | solution.py:29
  72.9 7.3 %copy-start.12 = (s32[512]{0:T(512)S(1)}, s32[512]{0:T(512)}, u32[]{:S(2)}) copy-start(s32[512]{0:T(512)} %param.38) | copy-start | bytes 6148
  72.9 7.2 %copy-start.14 = (s32[512]{0:T(512)S(1)}, s32[512]{0:T(512)}, u32[]{:S(2)}) copy-start(s32[512]{0:T(512)} %param.39) | copy-start | bytes 6148
  72.9 9.1 %copy-start.8 = (bf16[256,128]{0,1:T(8,128)(2,1)S(1)}, bf16[256,128]{0,1:T(8,128)(2,1)}, u32[]{:S(2)}) copy-start(bf16[256,128]{0,1:T(8,128)(2,1)} %fusion.50) | copy-start | bytes 196612
  84.0 20.4 %copy-start.18 = (f32[1280]{0:T(1024)S(1)}, f32[1280]{0:T(1024)}, u32[]{:S(2)}) copy-start(f32[1280]{0:T(1024)} %param.29) | copy-start | bytes 15364
  87.7 16.7 %all-to-all-start = ((bf16[8,32,128]{2,1,0:T(8,128)(2,1)}), bf16[8,32,128]{2,1,0:T(8,128)(2,1)S(1)}, u32[]{:S(2)}, u32[]{:S(2)}) async-start(bf16[8,32,128]{2,1,0:T(8,128)(2,1)} %all_to_all.24), calls=%async_computation | async-start | bytes 131072 | tf_op jit(solution)/shard_map/all_to_all | solution.py:139
  106.9 25.6 %copy-start.17 = (f32[8192]{0:T(1024)S(1)}, f32[8192]{0:T(1024)}, u32[]{:S(2)}) copy-start(f32[8192]{0:T(1024)} %param.34) | copy-start | bytes 98308
  106.9 25.6 %copy-start.19 = (f32[512]{0:T(512)S(1)}, f32[512]{0:T(512)}, u32[]{:S(2)}) copy-start(f32[512]{0:T(512)} %param.36) | copy-start | bytes 6148
  111.1 9.4 %all-to-all-start.1 = ((bf16[32,8,256]{2,0,1:T(8,128)(2,1)}), bf16[32,8,256]{2,0,1:T(8,128)(2,1)S(1)}, u32[]{:S(2)}, u32[]{:S(2)}) async-start(bf16[32,8,256]{2,0,1:T(8,128)(2,1)} %bitcast.156), calls=%async_computation.1 | async-start | bytes 262144 | tf_op jit(solution)/shard_map/all_to_all | solution.py:156
  120.5 6.9 %collective-permute-start.6 = (bf16[256,1,256]{2,0,1:T(8,128)(2,1)S(1)}, bf16[256,1,256]{2,0,1:T(8,128)(2,1)S(1)}, u32[]{:S(2)}, u32[]{:S(2)}) collective-permute-start(bf16[256,1,256]{2,0,1:T(8,128)(2,1)S(1)} %bitcast.166), channel_id=1, source_target_pairs={{8,0},{16,8},{24,16},{32,24},{40,32},{48,40},{56,48},{64,56},{72,6... | collective-permute-start | bytes 393224 | tf_op jit(solution)/shard_map/ppermute | solution.py:18
  123.2 9.2 %collective-permute-start.5 = (bf16[256,1,256]{2,0,1:T(8,128)(2,1)S(1)}, bf16[256,1,256]{2,0,1:T(8,128)(2,1)S(1)}, u32[]{:S(2)}, u32[]{:S(2)}) collective-permute-start(bf16[256,1,256]{2,0,1:T(8,128)(2,1)S(1)} %bitcast.167), channel_id=1, source_target_pairs={{0,8},{8,16},{16,24},{24,32},{32,40},{40,48},{48,56},{56,64},{64,7... | collective-permute-start | bytes 393224 | tf_op jit(solution)/shard_map/ppermute | solution.py:15
  147.9 2.0 collective-permute-start.7
  150.0 16.1 %collective-permute-start.9 = (bf16[2,512,512]{2,1,0:T(8,128)(2,1)S(1)}, bf16[2,512,512]{2,1,0:T(8,128)(2,1)S(1)}, u32[]{:S(2)}, u32[]{:S(2)}) collective-permute-start(bf16[2,512,512]{2,1,0:T(8,128)(2,1)S(1)} %maximum_select_fusion.11), channel_id=1, source_target_pairs={{0,2},{1,7},{2,4},{3,1},{4,6},{5,3},{6,0},{7,5},{8,10},{9,15},{10,... | collective-permute-start | bytes 3145736 | tf_op jit(solution)/shard_map/ppermute | solution.py:53
  166.1 16.1 %collective-permute-start.10 = (bf16[2,512,512]{2,1,0:T(8,128)(2,1)S(1)}, bf16[2,512,512]{2,1,0:T(8,128)(2,1)}, u32[]{:S(2)}, u32[]{:S(2)}) collective-permute-start(bf16[2,512,512]{2,1,0:T(8,128)(2,1)S(1)} %collective-permute-done.9), channel_id=1, source_target_pairs={{0,2},{1,7},{2,4},{3,1},{4,6},{5,3},{6,0},{7,5},{8,10},{9,15},{10,... | collective-permute-start | bytes 3145736 | tf_op jit(solution)/shard_map/ppermute | solution.py:54
  166.2 6.7 %copy-start.9 = (bf16[8192,512]{1,0:T(8,128)(2,1)S(1)}, bf16[8192,512]{1,0:T(8,128)(2,1)}, u32[]{:S(2)}) copy-start(bf16[8192,512]{1,0:T(8,128)(2,1)} %all-gather.6.cloned.1.call-done) | copy-start | bytes 25165828
  170.9 15.0 %collective-permute-start.11 = (bf16[2,512,512]{2,1,0:T(8,128)(2,1)S(1)}, bf16[2,512,512]{2,1,0:T(8,128)(2,1)S(1)}, u32[]{:S(2)}, u32[]{:S(2)}) collective-permute-start(bf16[2,512,512]{2,1,0:T(8,128)(2,1)S(1)} %collective-permute-done.9), channel_id=1, source_target_pairs={{0,1},{1,0},{2,3},{3,2},{4,5},{5,4},{6,7},{7,6},{8,9},{9,8},{10,11... | collective-permute-start | bytes 3145736 | tf_op jit(solution)/shard_map/ppermute | solution.py:55
  189.4 4.5 %copy-start.1 = (bf16[1280,128]{1,0:T(8,128)(2,1)S(1)}, bf16[1280,128]{1,0:T(8,128)(2,1)}, u32[]{:S(2)}) copy-start(bf16[1280,128]{1,0:T(8,128)(2,1)} %param.25) | copy-start | bytes 983044
  (5 other events, 9.2 us)
Sparse Core Ops, SparseCore 0:
  10.2 83.0 all-gather.3
  95.4 70.8 all-gather.5

commit v5 on v4

--- a/solution.py
+++ b/solution.py
@@ -135,9 +135,13 @@
     )
     enc_context = enc_context.astype(jnp.bfloat16).reshape(frames_dev, heads_dev * head_size)
     share = frames_dev // head_count
-    full_wo = heads_gather(enc_wo, "heads").reshape(head_count * enc_wo.shape[0], enc_width)
-    context_share = lax.all_to_all(enc_context, "heads", 0, 1, tiled=True)
-    mixed = jnp.dot(context_share, full_wo, preferred_element_type=jnp.float32)
+    enc_term = jnp.dot(enc_context, enc_wo, preferred_element_type=jnp.float32)
+    mixed = jnp.sum(
+        lax.all_to_all(
+            enc_term.reshape(head_count, share, enc_width), "heads", 0, 0, tiled=True
+        ),
+        axis=0,
+    )
     own_audio = lax.dynamic_slice_in_dim(audio, head_index * share, share, 0)
     enc_out = (own_audio.astype(jnp.float32) + mixed + enc_bo).astype(jnp.bfloat16)
     groups = dec_wkv.shape[1]

time: 202 us -> 198 us (0.980); the launches traced: 201 us -> 194 us
  local copies, waits for them, and re-layouts: 13.9 us -> 11.5 us
  waiting for transfers between devices: 88.9 us -> 86.7 us
    all_gather x1, waiting for transfers between devices: 0.1 us -> 16.5 us  [shards(): lax.all_gather(piece, 'seq', axis=0, tiled=False)]
    ppermute x3 -> x0, waiting for transfers between devices: 10.7 us -> none  [heads_gather(): other = lax.ppermute(gathered, axis, [(i, i ^ bit) for i in range(count)])]
    ppermute x1, waiting for transfers between devices: 8.48 us -> 0.01 us  [heads_ring_gather(): far = lax.ppermute(near, axis, step)]
    all_to_all x1, waiting for transfers between devices: 12.4 us -> 6.12 us  [shards(): lax.all_to_all(enc_term.reshape(head_count, share, enc_width), 'heads', 0...]
    ppermute x2, waiting for transfers between devices: 0.9 us -> 5.42 us  [with_halo(): lax.ppermute(lax.slice_in_dim(block, 0, width, axis=dim), axis, backward)]
    ppermute x2, starting transfers between devices: 7.25 us -> 11 us  [with_halo(): lax.ppermute(lax.slice_in_dim(block, 0, width, axis=dim), axis, backward)]
    ppermute x2, waiting for transfers between devices: 4.95 us -> 7.34 us  [with_halo(): lax.ppermute(lax.slice_in_dim(block, block.shape[dim] - width, None, axis...]
    unnamed x45 -> x31, local copies, waits for them, and re-layouts: 9.71 us -> 8.07 us
  transfers between devices with their start and end apart: 16 -> 13, of which waited for: 10 -> 9; matrix products, arithmetic and copies ran while one was open for 29% -> 29% of each run, Pallas kernels for 0% -> 0%
where the time goes in v5:
time: 198 us; the launch traced here: 194 us
  waiting for transfers between devices  86.7 us (44%)
  matrix products  37.7 us (19%)
  starting transfers between devices  28.1 us (14%)
  other arithmetic  15.7 us (8%)
  between operations  14.6 us (7%)
  local copies, waits for them, and re-layouts  11.5 us (6%)
    ppermute x1, waiting for transfers between devices, shards(): piece = lax.ppermute(dec_wo, ('seq', 'heads'), regroup)  27.9 us
    all_gather x1, waiting for transfers between devices, shards(): lax.all_gather(piece, 'seq', axis=0, tiled=False)  16.5 us
    ppermute x1, waiting for transfers between devices, heads_ring_gather(): near = lax.ppermute(own, axis, step)  15.4 us
    dot_general x8, matrix products, shards(): jnp.einsum('rk,bkc->rbc', held[offset], weight_set, preferred_element_typ...  14.6 us
    ppermute x2, starting transfers between devices, with_halo(): lax.ppermute(lax.slice_in_dim(block, 0, width, axis=dim), axis, backward)  11 us
    dot_general x1, matrix products, shards(): jnp.dot(normed, lax.all_gather(dec_wq, 'seq', axis=0, tiled=True), prefer...  10.4 us
    unnamed x31, local copies, waits for them, and re-layouts  8.07 us
    ppermute x2, waiting for transfers between devices, with_halo(): lax.ppermute(lax.slice_in_dim(block, block.shape[dim] - width, None, axis...  7.34 us
  transfers between devices with their start and end apart: 13, of which 9 were waited for; matrix products, arithmetic and copies ran while one was open for 29% of the time, Pallas kernels for 0%

profile of v5, /device:TPU:96, one launch (start us, length us, event | category | flops | bytes accessed | tf_op | source)
XLA Modules:
  0.0 194.3 jit_solution(17260053496969563046)
XLA Ops:
  8.0 3.6 %collective-permute-start.5 = (bf16[512,512]{1,0:T(8,128)(2,1)}, bf16[512,512]{1,0:T(8,128)(2,1)S(1)}, u32[]{:S(2)}, u32[]{:S(2)}) collective-permute-start(bf16[512,512]{1,0:T(8,128)(2,1)} %param.37), channel_id=1, source_target_pairs={{0,0},{1,16},{2,32},{3,48},{4,64},{5,80},{6,96},{7,112},{8,8},{9,2... | collective-permute-start | bytes 1572872 | tf_op jit(solution)/shard_map/ppermute | solution.py:200
  11.6 27.9 %collective-permute-done.5 = bf16[512,512]{1,0:T(8,128)(2,1)S(1)} collective-permute-done((bf16[512,512]{1,0:T(8,128)(2,1)}, bf16[512,512]{1,0:T(8,128)(2,1)S(1)}, u32[]{:S(2)}, u32[]{:S(2)}) %collective-permute-start.5) | collective-permute-done | bytes 524320 | tf_op jit(solution)/shard_map/ppermute | solution.py:200
  41.5 1.4 fusion.25
  42.9 1.4 fusion.28
  47.0 3.4 %collective-permute-start = (bf16[128,2,128]{2,0,1:T(8,128)(2,1)S(1)}, bf16[128,2,128]{2,0,1:T(8,128)(2,1)S(1)}, u32[]{:S(2)}, u32[]{:S(2)}) collective-permute-start(bf16[128,2,128]{2,0,1:T(8,128)(2,1)S(1)} %get-tuple-element.4), channel_id=1, source_target_pairs={{0,8},{8,16},{16,24},{24,32},{32,40},{40,48},{48,56},{56,64},{64,7... | collective-permute-start | bytes 196616 | tf_op jit(solution)/shard_map/ppermute | solution.py:15
  50.4 4.6 %collective-permute-start.1 = (bf16[128,2,128]{2,0,1:T(8,128)(2,1)S(1)}, bf16[128,2,128]{2,0,1:T(8,128)(2,1)S(1)}, u32[]{:S(2)}, u32[]{:S(2)}) collective-permute-start(bf16[128,2,128]{2,0,1:T(8,128)(2,1)S(1)} %get-tuple-element.5), channel_id=1, source_target_pairs={{8,0},{16,8},{24,16},{32,24},{40,32},{48,40},{56,48},{64,56},{72,6... | collective-permute-start | bytes 196616 | tf_op jit(solution)/shard_map/ppermute | solution.py:18
  55.6 2.3 %collective-permute-done.1 = bf16[128,2,128]{2,0,1:T(8,128)(2,1)S(1)} collective-permute-done((bf16[128,2,128]{2,0,1:T(8,128)(2,1)S(1)}, bf16[128,2,128]{2,0,1:T(8,128)(2,1)S(1)}, u32[]{:S(2)}, u32[]{:S(2)}) %collective-permute-start.1) | collective-permute-done | bytes 65568 | tf_op jit(solution)/shard_map/ppermute | solution.py:18
  60.7 1.4 fusion.63
  62.1 3.7 %all-to-all-start = ((f32[8,32,1280]{2,1,0:T(8,128)}), f32[8,32,1280]{2,1,0:T(8,128)S(1)}, u32[]{:S(2)}, u32[]{:S(2)}) async-start(f32[8,32,1280]{2,1,0:T(8,128)} %fusion.63), calls=%async_computation | async-start | bytes 2621440 | tf_op jit(solution)/shard_map/all_to_all | solution.py:140
  65.8 7.2 %copy.92 = bf16[160,8,8,256]{3,1,2,0:T(8,128)(2,1)} copy(bf16[160,8,8,256]{3,2,1,0:T(8,128)(2,1)} %bitcast.151) | data formatting | bytes 10485760
  73.1 5.3 %fusion.1 = f32[512]{0:T(512)S(1)} fusion(bf16[512,8192]{1,0:T(8,128)(2,1)} %param.33), kind=kLoop, calls=%fused_computation.3 | loop fusion | flops 12582400 | bytes 8390656 | tf_op jit(solution)/shard_map/reduce_sum | solution.py:70
  78.4 6.1 %all-to-all-done = f32[8,32,1280]{2,1,0:T(8,128)S(1)} async-done(((f32[8,32,1280]{2,1,0:T(8,128)}), f32[8,32,1280]{2,1,0:T(8,128)S(1)}, u32[]{:S(2)}, u32[]{:S(2)}) %all-to-all-start) | async-done | bytes 1310752 | tf_op jit(solution)/shard_map/all_to_all | solution.py:140
  85.5 3.5 %fusion.14 = bf16[32,2048]{1,0:T(8,128)(2,1)S(1)} fusion(bf16[32,1280]{1,0:T(8,128)(2,1)S(1)} %add_convert_fusion.1, bf16[1280,2048]{1,0:T(8,128)(2,1)} %bitcast.149, f32[2048]{0:T(1024)S(1)} %bitcast.171), kind=kOutput, calls=%fused_computation.19 | convolution fusion | flops 167903232 | bytes 5464064 | tf_op jit(solution)/shard_map/dot_general | solution.py:153
  89.7 3.4 %all-to-all-start.1 = ((bf16[32,8,256]{2,0,1:T(8,128)(2,1)}), bf16[32,8,256]{2,0,1:T(8,128)(2,1)S(1)}, u32[]{:S(2)}, u32[]{:S(2)}) async-start(bf16[32,8,256]{2,0,1:T(8,128)(2,1)} %bitcast.148), calls=%async_computation.1 | async-start | bytes 262144 | tf_op jit(solution)/shard_map/all_to_all | solution.py:160
  93.4 5.6 %all-to-all-done.1 = bf16[32,8,256]{2,0,1:T(8,128)(2,1)S(1)} async-done(((bf16[32,8,256]{2,0,1:T(8,128)(2,1)}), bf16[32,8,256]{2,0,1:T(8,128)(2,1)S(1)}, u32[]{:S(2)}, u32[]{:S(2)}) %all-to-all-start.1) | async-done | bytes 131104 | tf_op jit(solution)/shard_map/all_to_all | solution.py:160
  99.1 6.5 %collective-permute-start.3 = (bf16[256,1,256]{2,0,1:T(8,128)(2,1)S(1)}, bf16[256,1,256]{2,0,1:T(8,128)(2,1)S(1)}, u32[]{:S(2)}, u32[]{:S(2)}) collective-permute-start(bf16[256,1,256]{2,0,1:T(8,128)(2,1)S(1)} %bitcast.158), channel_id=1, source_target_pairs={{8,0},{16,8},{24,16},{32,24},{40,32},{48,40},{56,48},{64,56},{72,6... | collective-permute-start | bytes 393224 | tf_op jit(solution)/shard_map/ppermute | solution.py:18
  105.6 2.1 %collective-permute-start.2 = (bf16[256,1,256]{2,0,1:T(8,128)(2,1)S(1)}, bf16[256,1,256]{2,0,1:T(8,128)(2,1)S(1)}, u32[]{:S(2)}, u32[]{:S(2)}) collective-permute-start(bf16[256,1,256]{2,0,1:T(8,128)(2,1)S(1)} %bitcast.159), channel_id=1, source_target_pairs={{0,8},{8,16},{16,24},{24,32},{32,40},{40,48},{48,56},{56,64},{64,7... | collective-permute-start | bytes 393224 | tf_op jit(solution)/shard_map/ppermute | solution.py:15
  107.7 3.1 %collective-permute-done.3 = bf16[256,1,256]{2,0,1:T(8,128)(2,1)S(1)} collective-permute-done((bf16[256,1,256]{2,0,1:T(8,128)(2,1)S(1)}, bf16[256,1,256]{2,0,1:T(8,128)(2,1)S(1)}, u32[]{:S(2)}, u32[]{:S(2)}) %collective-permute-start.3) | collective-permute-done | bytes 131104 | tf_op jit(solution)/shard_map/ppermute | solution.py:18
  110.8 7.3 %collective-permute-done.2 = bf16[256,1,256]{2,0,1:T(8,128)(2,1)S(1)} collective-permute-done((bf16[256,1,256]{2,0,1:T(8,128)(2,1)S(1)}, bf16[256,1,256]{2,0,1:T(8,128)(2,1)S(1)}, u32[]{:S(2)}, u32[]{:S(2)}) %collective-permute-start.2) | collective-permute-done | bytes 131104 | tf_op jit(solution)/shard_map/ppermute | solution.py:15
  118.2 10.4 %fusion.35 = bf16[512,512]{0,1:T(8,128)(2,1)S(1)} fusion(bf16[8192,512]{1,0:T(8,128)(2,1)} %all-gather.4.cloned.1.call-done, bf16[512,8192]{1,0:T(8,128)(2,1)} %param.33, f32[8192]{0:T(1024)S(1)} %copy-done.11, f32[512]{0:T(512)S(1)} %add_rsqrt_fusion, f32[512]{0:T(512)S(1)} %copy-done.12), kind=kOutput, calls=%fused_computation.47 | convolution fusion | flops 4312268800 | bytes 17338368 | tf_op jit(solution)/shard_map/dot_general | solution.py:168
  131.2 2.1 %fusion.32 = bf16[128,512,4]{1,0,2:T(8,128)(2,1)S(1)} fusion(f32[512,4]{0,1:T(4,128)S(1)} %fusion.11, f32[512,4]{0,1:T(4,128)S(1)} %get-tuple-element.6, f32[768,512,4]{1,0,2:T(8,128)S(1)} %get-tuple-element.7, pred[512,768]{0,1:T(8,128)(4,1)S(1)} %compare_and_fusion, bf16[768,1,256]{2,0,1:T(8,128)(2,1)S(1)} %pad_maximum_fusion), kind=kOutput, calls=%fused_computation.46 | convolution fusion | flops 410779648 | bytes 7421952 | tf_op jit(solution)/shard_map/rgqk,kgd->rgqd/dot_general | solution.py:189
  133.8 1.7 collective-permute-done.4
  136.4 15.4 %collective-permute-done.6 = bf16[2,512,512]{2,1,0:T(8,128)(2,1)S(1)} collective-permute-done((bf16[2,512,512]{2,1,0:T(8,128)(2,1)S(1)}, bf16[2,512,512]{2,1,0:T(8,128)(2,1)S(1)}, u32[]{:S(2)}, u32[]{:S(2)}) %collective-permute-start.6) | collective-permute-done | bytes 1048608 | tf_op jit(solution)/shard_map/ppermute | solution.py:53
  151.7 16.5 %all-gather.6.cloned.1.call-done = bf16[8192,512]{1,0:T(8,128)(2,1)} async-done(((bf16[512,512]{1,0:T(8,128)(2,1)}), bf16[8192,512]{1,0:T(8,128)(2,1)}) %all-gather.6.cloned.1.call-update) | async-done | bytes 8388624 | tf_op jit(solution)/shard_map/all_gather | solution.py:201
  168.3 2.1 %convolution_convert_fusion.6 = bf16[512,2,512]{0,2,1:T(8,128)(2,1)S(1)} fusion(bf16[8,2,512,512]{3,2,1,0:T(8,128)(2,1)} %bitcast.163, s32[]{:T(128)S(6)} %select_n.89, bf16[2,512,512]{2,1,0:T(8,128)(2,1)S(1)} %maximum_select_fusion), kind=kOutput, calls=%fused_computation.33 | convolution fusion | flops 537395200 | bytes 2621444 | tf_op jit(solution)/shard_map/rk,bkc->rbc/dot_general | solution.py:211
  170.4 2.5 %convolution_convert_fusion.7 = bf16[512,2,512]{0,2,1:T(8,128)(2,1)S(1)} fusion(bf16[8,2,512,512]{3,2,1,0:T(8,128)(2,1)} %bitcast.164, s32[]{:T(128)S(6)} %select_n.88, bf16[2,512,512]{2,1,0:T(8,128)(2,1)S(1)} %maximum_select_fusion), kind=kOutput, calls=%fused_computation.34 | convolution fusion | flops 537395200 | bytes 2621444 | tf_op jit(solution)/shard_map/rk,bkc->rbc/dot_general | solution.py:211
  173.0 2.0 %convolution_convert_fusion.4 = bf16[512,2,512]{0,2,1:T(8,128)(2,1)S(1)} fusion(bf16[8,2,512,512]{3,2,1,0:T(8,128)(2,1)} %bitcast.165, s32[]{:T(128)S(6)} %select_n.92, bf16[2,512,512]{2,1,0:T(8,128)(2,1)S(1)} %collective-permute-done.6), kind=kOutput, calls=%fused_computation.31 | convolution fusion | flops 537395200 | bytes 2621444 | tf_op jit(solution)/shard_map/rk,bkc->rbc/dot_general | solution.py:211
  175.8 1.8 convolution_convert_fusion.2
  177.6 1.8 convolution_convert_fusion.3
  180.2 2.8 %convert_add_fusion = f32[512,2,512]{0,2,1:T(8,128)} fusion(bf16[512,2,512]{0,2,1:T(8,128)(2,1)S(1)} %convolution_convert_fusion.1, bf16[512,2,512]{0,2,1:T(8,128)(2,1)S(1)} %convolution_convert_fusion.2, bf16[512,2,512]{0,2,1:T(8,128)(2,1)S(1)} %convolution_convert_fusion.3, bf16[512,2,512]{0,2,1:T(8,128)(2,1)S(1)} %convolution_convert_fusion.4, ...), kind=kOutput, calls=%fused_computation.21 | convolution fusion | flops 545259520 | bytes 11010052 | tf_op jit(solution)/shard_map/rk,bkc->rbc/dot_general | solution.py:211
  183.0 1.9 copy.78
  184.9 2.6 %add_convert_fusion = bf16[512,1024]{1,0:T(8,128)(2,1)} fusion(f32[512,1024]{1,0:T(8,128)S(1)} %copy.78, bf16[512,8192]{1,0:T(8,128)(2,1)} %param.33, s32[]{:T(128)S(6)} %select_n.81), kind=kLoop, calls=%fused_computation.20 | loop fusion | flops 1572864 | bytes 4194308 | tf_op jit(solution)/shard_map/convert_element_type | solution.py:218
  (77 shorter events, 16.4 us)
Async XLA Ops:
  7.2 53.5 %copy-start = (bf16[128,1280]{1,0:T(8,128)(2,1)S(1)}, bf16[128,1280]{1,0:T(8,128)(2,1)}, u32[]{:S(2)}) copy-start(bf16[128,1280]{1,0:T(8,128)(2,1)} %param.28) | copy-start | bytes 983044
  7.2 47.9 %copy-start.10 = (f32[128]{0:T(128)S(1)}, f32[128]{0:T(128)}, u32[]{:S(2)}) copy-start(f32[128]{0:T(128)} %param.24) | copy-start | bytes 1540
  7.2 47.9 %copy-start.3 = (bf16[1280,128]{1,0:T(8,128)(2,1)S(1)}, bf16[1280,128]{1,0:T(8,128)(2,1)}, u32[]{:S(2)}) copy-start(bf16[1280,128]{1,0:T(8,128)(2,1)} %param.23) | copy-start | bytes 983044
  7.2 51.3 %copy-start.13 = (s32[2]{0:T(128)S(1)}, s32[2]{0:T(128)}, u32[]{:S(2)}) copy-start(s32[2]{0:T(128)} %param.30) | copy-start | bytes 28
  7.2 111.0 %all-gather.4.cloned.1.call-start = ((), (), s32[]{:S(2)}) async-start(), calls=%async_computation.2 | async-start | bytes 8912896 | tf_op jit(solution)/shard_map/all_gather | solution.py:170
  7.9 160.3 %all-gather.6.cloned.1.call-start = ((), (), s32[]{:S(2)}) async-start(), calls=%async_computation.3 | async-start | bytes 8912896 | tf_op jit(solution)/shard_map/all_gather | solution.py:201
  8.0 31.5 %collective-permute-start.5 = (bf16[512,512]{1,0:T(8,128)(2,1)}, bf16[512,512]{1,0:T(8,128)(2,1)S(1)}, u32[]{:S(2)}, u32[]{:S(2)}) collective-permute-start(bf16[512,512]{1,0:T(8,128)(2,1)} %param.37), channel_id=1, source_target_pairs={{0,0},{1,16},{2,32},{3,48},{4,64},{5,80},{6,96},{7,112},{8,8},{9,2... | collective-permute-start | bytes 1572872 | tf_op jit(solution)/shard_map/ppermute | solution.py:200
  39.5 0.8 copy-start.2
  47.0 8.6 %collective-permute-start = (bf16[128,2,128]{2,0,1:T(8,128)(2,1)S(1)}, bf16[128,2,128]{2,0,1:T(8,128)(2,1)S(1)}, u32[]{:S(2)}, u32[]{:S(2)}) collective-permute-start(bf16[128,2,128]{2,0,1:T(8,128)(2,1)S(1)} %get-tuple-element.4), channel_id=1, source_target_pairs={{0,8},{8,16},{16,24},{24,32},{32,40},{40,48},{48,56},{56,64},{64,7... | collective-permute-start | bytes 196616 | tf_op jit(solution)/shard_map/ppermute | solution.py:15
  50.4 7.5 %collective-permute-start.1 = (bf16[128,2,128]{2,0,1:T(8,128)(2,1)S(1)}, bf16[128,2,128]{2,0,1:T(8,128)(2,1)S(1)}, u32[]{:S(2)}, u32[]{:S(2)}) collective-permute-start(bf16[128,2,128]{2,0,1:T(8,128)(2,1)S(1)} %get-tuple-element.5), channel_id=1, source_target_pairs={{8,0},{16,8},{24,16},{32,24},{40,32},{48,40},{56,48},{64,56},{72,6... | collective-permute-start | bytes 196616 | tf_op jit(solution)/shard_map/ppermute | solution.py:18
  58.5 7.3 %copy-start.8 = (f32[8,128]{1,0:T(8,128)S(1)}, f32[8,128]{1,0:T(8,128)}, u32[]{:S(2)}) copy-start(f32[8,128]{1,0:T(8,128)} %param.32) | copy-start | bytes 12292
  62.1 11.0 %copy-start.6 = (s32[512]{0:T(512)S(1)}, s32[512]{0:T(512)}, u32[]{:S(2)}) copy-start(s32[512]{0:T(512)} %param.38) | copy-start | bytes 6148
  62.1 11.0 %copy-start.9 = (s32[512]{0:T(512)S(1)}, s32[512]{0:T(512)}, u32[]{:S(2)}) copy-start(s32[512]{0:T(512)} %param.39) | copy-start | bytes 6148
  62.1 22.4 %all-to-all-start = ((f32[8,32,1280]{2,1,0:T(8,128)}), f32[8,32,1280]{2,1,0:T(8,128)S(1)}, u32[]{:S(2)}, u32[]{:S(2)}) async-start(f32[8,32,1280]{2,1,0:T(8,128)} %fusion.63), calls=%async_computation | async-start | bytes 2621440 | tf_op jit(solution)/shard_map/all_to_all | solution.py:140
  73.0 11.5 %copy-start.7 = (f32[1280]{0:T(1024)S(1)}, f32[1280]{0:T(1024)}, u32[]{:S(2)}) copy-start(f32[1280]{0:T(1024)} %param.29) | copy-start | bytes 15364
  78.3 39.9 %copy-start.11 = (f32[8192]{0:T(1024)S(1)}, f32[8192]{0:T(1024)}, u32[]{:S(2)}) copy-start(f32[8192]{0:T(1024)} %param.34) | copy-start | bytes 98308
  78.3 39.9 %copy-start.12 = (f32[512]{0:T(512)S(1)}, f32[512]{0:T(512)}, u32[]{:S(2)}) copy-start(f32[512]{0:T(512)} %param.36) | copy-start | bytes 6148
  85.5 43.2 %copy-start.4 = (bf16[32,1280]{1,0:T(8,128)(2,1)}, bf16[32,1280]{1,0:T(8,128)(2,1)S(1)}, u32[]{:S(2)}) copy-start(bf16[32,1280]{1,0:T(8,128)(2,1)S(1)} %add_convert_fusion.1) | copy-start | bytes 245764
  89.7 9.4 %all-to-all-start.1 = ((bf16[32,8,256]{2,0,1:T(8,128)(2,1)}), bf16[32,8,256]{2,0,1:T(8,128)(2,1)S(1)}, u32[]{:S(2)}, u32[]{:S(2)}) async-start(bf16[32,8,256]{2,0,1:T(8,128)(2,1)} %bitcast.148), calls=%async_computation.1 | async-start | bytes 262144 | tf_op jit(solution)/shard_map/all_to_all | solution.py:160
  99.1 11.7 %collective-permute-start.3 = (bf16[256,1,256]{2,0,1:T(8,128)(2,1)S(1)}, bf16[256,1,256]{2,0,1:T(8,128)(2,1)S(1)}, u32[]{:S(2)}, u32[]{:S(2)}) collective-permute-start(bf16[256,1,256]{2,0,1:T(8,128)(2,1)S(1)} %bitcast.158), channel_id=1, source_target_pairs={{8,0},{16,8},{24,16},{32,24},{40,32},{48,40},{56,48},{64,56},{72,6... | collective-permute-start | bytes 393224 | tf_op jit(solution)/shard_map/ppermute | solution.py:18
  105.6 12.5 %collective-permute-start.2 = (bf16[256,1,256]{2,0,1:T(8,128)(2,1)S(1)}, bf16[256,1,256]{2,0,1:T(8,128)(2,1)S(1)}, u32[]{:S(2)}, u32[]{:S(2)}) collective-permute-start(bf16[256,1,256]{2,0,1:T(8,128)(2,1)S(1)} %bitcast.159), channel_id=1, source_target_pairs={{0,8},{8,16},{16,24},{24,32},{32,40},{40,48},{48,56},{56,64},{64,7... | collective-permute-start | bytes 393224 | tf_op jit(solution)/shard_map/ppermute | solution.py:15
  133.5 2.0 %collective-permute-start.4 = (bf16[512,512]{1,0:T(8,128)(2,1)S(1)}, bf16[512,512]{1,0:T(8,128)(2,1)S(1)}, u32[]{:S(2)}, u32[]{:S(2)}) collective-permute-start(bf16[512,512]{1,0:T(8,128)(2,1)S(1)} %copy.67), channel_id=1, source_target_pairs={{0,1},{1,0},{2,3},{3,2},{4,5},{5,4},{6,7},{7,6},{8,9},{9,8},{10,11... | collective-permute-start | bytes 1572872 | tf_op jit(solution)/shard_map/ppermute | solution.py:47
  135.7 16.1 %collective-permute-start.6 = (bf16[2,512,512]{2,1,0:T(8,128)(2,1)S(1)}, bf16[2,512,512]{2,1,0:T(8,128)(2,1)S(1)}, u32[]{:S(2)}, u32[]{:S(2)}) collective-permute-start(bf16[2,512,512]{2,1,0:T(8,128)(2,1)S(1)} %maximum_select_fusion), channel_id=1, source_target_pairs={{0,2},{1,7},{2,4},{3,1},{4,6},{5,3},{6,0},{7,5},{8,10},{9,15},{10,... | collective-permute-start | bytes 3145736 | tf_op jit(solution)/shard_map/ppermute | solution.py:53
  151.7 24.1 %collective-permute-start.7 = (bf16[2,512,512]{2,1,0:T(8,128)(2,1)S(1)}, bf16[2,512,512]{2,1,0:T(8,128)(2,1)}, u32[]{:S(2)}, u32[]{:S(2)}) collective-permute-start(bf16[2,512,512]{2,1,0:T(8,128)(2,1)S(1)} %collective-permute-done.6), channel_id=1, source_target_pairs={{0,2},{1,7},{2,4},{3,1},{4,6},{5,3},{6,0},{7,5},{8,10},{9,15},{10,... | collective-permute-start | bytes 3145736 | tf_op jit(solution)/shard_map/ppermute | solution.py:54
  168.3 6.7 %copy-start.5 = (bf16[8192,512]{1,0:T(8,128)(2,1)S(1)}, bf16[8192,512]{1,0:T(8,128)(2,1)}, u32[]{:S(2)}) copy-start(bf16[8192,512]{1,0:T(8,128)(2,1)} %all-gather.6.cloned.1.call-done) | copy-start | bytes 25165828
  172.9 6.5 %collective-permute-start.8 = (bf16[2,512,512]{2,1,0:T(8,128)(2,1)S(1)}, bf16[2,512,512]{2,1,0:T(8,128)(2,1)S(1)}, u32[]{:S(2)}, u32[]{:S(2)}) collective-permute-start(bf16[2,512,512]{2,1,0:T(8,128)(2,1)S(1)} %collective-permute-done.6), channel_id=1, source_target_pairs={{0,1},{1,0},{2,3},{3,2},{4,5},{5,4},{6,7},{7,6},{8,9},{9,8},{10,11... | collective-permute-start | bytes 3145736 | tf_op jit(solution)/shard_map/ppermute | solution.py:55
  180.2 7.3 %copy-start.1 = (bf16[128,1280]{1,0:T(8,128)(2,1)S(1)}, bf16[128,1280]{1,0:T(8,128)(2,1)}, u32[]{:S(2)}) copy-start(bf16[128,1280]{1,0:T(8,128)(2,1)} %param.28) | copy-start | bytes 983044
Sparse Core Ops, SparseCore 0:
  10.2 83.0 all-gather.3
  96.0 72.2 all-gather.5

commit v6 on v5

--- a/solution.py
+++ b/solution.py
@@ -198,21 +198,18 @@
         (c * head_count + j, (ratio * j + c % ratio) * head_count + c // ratio) for c, j in flat
     ]
     piece = lax.ppermute(dec_wo, ("seq", "heads"), regroup)
-    column_weight = lax.all_gather(piece, "seq", axis=0, tiled=False).reshape(
-        head_count, ratio, set_rows, block_cols
-    )
     pieces, owners = heads_ring_gather(dec_context, "heads")
-    total = jnp.zeros((rows_dev, ratio, block_cols), jnp.float32)
+    set_cols = ratio * block_cols
+    column_weight = lax.all_gather(piece, "seq", axis=1, tiled=True)
+    total = jnp.zeros((rows_dev, set_cols), jnp.float32)
     for held, owner in zip(pieces, owners):
         for offset in range(held.shape[0]):
-            weight_set = lax.dynamic_index_in_dim(
-                column_weight, owner * held.shape[0] + offset, 0, keepdims=False
+            weight_set = lax.dynamic_slice_in_dim(
+                column_weight, (owner * held.shape[0] + offset) * set_cols, set_cols, 1
             )
-            term = jnp.einsum(
-                "rk,bkc->rbc", held[offset], weight_set, preferred_element_type=jnp.float32
-            )
+            term = jnp.dot(held[offset], weight_set, preferred_element_type=jnp.float32)
             total = total + term.astype(jnp.bfloat16).astype(jnp.float32)
-    summed = total.reshape(rows_dev, ratio * block_cols)
+    summed = total
     col_share = model_width // head_count
     own_text = lax.dynamic_slice_in_dim(text, head_index * col_share, col_share, 1)
     dec_out = (own_text.astype(jnp.float32) + summed).astype(jnp.bfloat16)

time: 198 us -> 198 us (level)
  waiting for transfers between devices: 86.7 us -> 92.6 us
  other arithmetic: 15.7 us -> 13.2 us
  matrix products: 37.7 us -> 35.3 us
  local copies, waits for them, and re-layouts: 11.5 us -> 9.19 us
    all_gather x1, waiting for transfers between devices: 16.5 us -> 25.4 us  [shards(): column_weight = lax.all_gather(piece, 'seq', axis=1, tiled=True)]
    ppermute x2, waiting for transfers between devices: 7.34 us -> 4.68 us  [with_halo(): lax.ppermute(lax.slice_in_dim(block, block.shape[dim] - width, None, axis...]
    convert_element_type x1 -> x0, other arithmetic: 2.56 us -> none  [shards(): dec_out = (own_text.astype(jnp.float32) + summed).astype(jnp.bfloat16)]
    dot_general x8, matrix products: 14.6 us -> 12.1 us  [shards(): term = jnp.dot(held[offset], weight_set, preferred_element_type=jnp.float32)]
    reshape x2 -> x0, local copies, waits for them, and re-layouts: 2.13 us -> none  [the longest x1 1.92 us: shards(): summed = total.reshape(rows_dev, ratio * block_cols)]
  transfers between devices with their start and end apart: 13 -> 13, of which waited for: 9 -> 9; matrix products, arithmetic and copies ran while one was open for 29% -> 27% of each run, Pallas kernels for 0% -> 0%
where the time goes in v6:
time: 198 us; the launch traced here: 194 us
  waiting for transfers between devices  92.6 us (47%)
  matrix products  35.3 us (18%)
  starting transfers between devices  29.1 us (15%)
  between operations  14.6 us (7%)
  other arithmetic  13.2 us (7%)
  local copies, waits for them, and re-layouts  9.19 us (5%)
    ppermute x1, waiting for transfers between devices, shards(): piece = lax.ppermute(dec_wo, ('seq', 'heads'), regroup)  27.9 us
    all_gather x1, waiting for transfers between devices, shards(): column_weight = lax.all_gather(piece, 'seq', axis=1, tiled=True)  25.4 us
    ppermute x1, waiting for transfers between devices, heads_ring_gather(): near = lax.ppermute(own, axis, step)  14.8 us
    dot_general x8, matrix products, shards(): term = jnp.dot(held[offset], weight_set, preferred_element_type=jnp.float32)  12.1 us
    ppermute x2, starting transfers between devices, with_halo(): lax.ppermute(lax.slice_in_dim(block, 0, width, axis=dim), axis, backward)  11 us
    dot_general x1, matrix products, shards(): jnp.dot(normed, lax.all_gather(dec_wq, 'seq', axis=0, tiled=True), prefer...  10.6 us
    unnamed x31, local copies, waits for them, and re-layouts  8.06 us
    all_to_all x1, waiting for transfers between devices, shards(): lax.all_to_all(enc_term.reshape(head_count, share, enc_width), 'heads', 0...  6.12 us
  transfers between devices with their start and end apart: 13, of which 9 were waited for; matrix products, arithmetic and copies ran while one was open for 27% of the time, Pallas kernels for 0%

profile of v6, /device:TPU:96, one launch (start us, length us, event | category | flops | bytes accessed | tf_op | source)
XLA Modules:
  0.0 194.0 jit_solution(16843577729594235310)
XLA Ops:
  8.0 3.6 %collective-permute-start.5 = (bf16[512,512]{1,0:T(8,128)(2,1)}, bf16[512,512]{1,0:T(8,128)(2,1)S(1)}, u32[]{:S(2)}, u32[]{:S(2)}) collective-permute-start(bf16[512,512]{1,0:T(8,128)(2,1)} %param.37), channel_id=1, source_target_pairs={{0,0},{1,16},{2,32},{3,48},{4,64},{5,80},{6,96},{7,112},{8,8},{9,2... | collective-permute-start | bytes 1572872 | tf_op jit(solution)/shard_map/ppermute | solution.py:200
  11.6 27.9 %collective-permute-done.5 = bf16[512,512]{1,0:T(8,128)(2,1)S(1)} collective-permute-done((bf16[512,512]{1,0:T(8,128)(2,1)}, bf16[512,512]{1,0:T(8,128)(2,1)S(1)}, u32[]{:S(2)}, u32[]{:S(2)}) %collective-permute-start.5) | collective-permute-done | bytes 524320 | tf_op jit(solution)/shard_map/ppermute | solution.py:200
  40.3 1.3 convert_reduce_fusion
  41.5 1.4 fusion.25
  42.9 1.4 fusion.28
  44.4 1.3 fusion.40
  45.7 1.3 fusion.42
  47.0 3.4 %collective-permute-start = (bf16[128,2,128]{2,0,1:T(8,128)(2,1)S(1)}, bf16[128,2,128]{2,0,1:T(8,128)(2,1)S(1)}, u32[]{:S(2)}, u32[]{:S(2)}) collective-permute-start(bf16[128,2,128]{2,0,1:T(8,128)(2,1)S(1)} %get-tuple-element.4), channel_id=1, source_target_pairs={{0,8},{8,16},{16,24},{24,32},{32,40},{40,48},{48,56},{56,64},{64,7... | collective-permute-start | bytes 196616 | tf_op jit(solution)/shard_map/ppermute | solution.py:15
  50.4 4.5 %collective-permute-start.1 = (bf16[128,2,128]{2,0,1:T(8,128)(2,1)S(1)}, bf16[128,2,128]{2,0,1:T(8,128)(2,1)S(1)}, u32[]{:S(2)}, u32[]{:S(2)}) collective-permute-start(bf16[128,2,128]{2,0,1:T(8,128)(2,1)S(1)} %get-tuple-element.5), channel_id=1, source_target_pairs={{8,0},{16,8},{24,16},{32,24},{40,32},{48,40},{56,48},{64,56},{72,6... | collective-permute-start | bytes 196616 | tf_op jit(solution)/shard_map/ppermute | solution.py:18
  55.6 2.3 %collective-permute-done.1 = bf16[128,2,128]{2,0,1:T(8,128)(2,1)S(1)} collective-permute-done((bf16[128,2,128]{2,0,1:T(8,128)(2,1)S(1)}, bf16[128,2,128]{2,0,1:T(8,128)(2,1)S(1)}, u32[]{:S(2)}, u32[]{:S(2)}) %collective-permute-start.1) | collective-permute-done | bytes 65568 | tf_op jit(solution)/shard_map/ppermute | solution.py:18
  60.7 1.4 fusion.55
  62.1 3.7 %all-to-all-start = ((f32[8,32,1280]{2,1,0:T(8,128)}), f32[8,32,1280]{2,1,0:T(8,128)S(1)}, u32[]{:S(2)}, u32[]{:S(2)}) async-start(f32[8,32,1280]{2,1,0:T(8,128)} %fusion.55), calls=%async_computation | async-start | bytes 2621440 | tf_op jit(solution)/shard_map/all_to_all | solution.py:140
  65.9 7.2 %copy.48 = bf16[160,8,8,256]{3,1,2,0:T(8,128)(2,1)} copy(bf16[160,8,8,256]{3,2,1,0:T(8,128)(2,1)} %bitcast.108) | data formatting | bytes 10485760
  73.1 5.3 %fusion.1 = f32[512]{0:T(512)S(1)} fusion(bf16[512,8192]{1,0:T(8,128)(2,1)} %param.33), kind=kLoop, calls=%fused_computation.3 | loop fusion | flops 12582400 | bytes 8390656 | tf_op jit(solution)/shard_map/reduce_sum | solution.py:70
  78.4 6.1 %all-to-all-done = f32[8,32,1280]{2,1,0:T(8,128)S(1)} async-done(((f32[8,32,1280]{2,1,0:T(8,128)}), f32[8,32,1280]{2,1,0:T(8,128)S(1)}, u32[]{:S(2)}, u32[]{:S(2)}) %all-to-all-start) | async-done | bytes 1310752 | tf_op jit(solution)/shard_map/all_to_all | solution.py:140
  85.5 3.5 %fusion.14 = bf16[32,2048]{1,0:T(8,128)(2,1)S(1)} fusion(bf16[32,1280]{1,0:T(8,128)(2,1)S(1)} %add_convert_fusion.1, bf16[1280,2048]{1,0:T(8,128)(2,1)} %bitcast.107, f32[2048]{0:T(1024)S(1)} %bitcast.120), kind=kOutput, calls=%fused_computation.19 | convolution fusion | flops 167903232 | bytes 5464064 | tf_op jit(solution)/shard_map/dot_general | solution.py:153
  89.7 3.4 %all-to-all-start.1 = ((bf16[32,8,256]{2,0,1:T(8,128)(2,1)}), bf16[32,8,256]{2,0,1:T(8,128)(2,1)S(1)}, u32[]{:S(2)}, u32[]{:S(2)}) async-start(bf16[32,8,256]{2,0,1:T(8,128)(2,1)} %bitcast.106), calls=%async_computation.1 | async-start | bytes 262144 | tf_op jit(solution)/shard_map/all_to_all | solution.py:160
  93.5 5.6 %all-to-all-done.1 = bf16[32,8,256]{2,0,1:T(8,128)(2,1)S(1)} async-done(((bf16[32,8,256]{2,0,1:T(8,128)(2,1)}), bf16[32,8,256]{2,0,1:T(8,128)(2,1)S(1)}, u32[]{:S(2)}, u32[]{:S(2)}) %all-to-all-start.1) | async-done | bytes 131104 | tf_op jit(solution)/shard_map/all_to_all | solution.py:160
  99.1 6.5 %collective-permute-start.3 = (bf16[256,1,256]{2,0,1:T(8,128)(2,1)S(1)}, bf16[256,1,256]{2,0,1:T(8,128)(2,1)S(1)}, u32[]{:S(2)}, u32[]{:S(2)}) collective-permute-start(bf16[256,1,256]{2,0,1:T(8,128)(2,1)S(1)} %bitcast.115), channel_id=1, source_target_pairs={{8,0},{16,8},{24,16},{32,24},{40,32},{48,40},{56,48},{64,56},{72,6... | collective-permute-start | bytes 393224 | tf_op jit(solution)/shard_map/ppermute | solution.py:18
  105.6 2.1 %collective-permute-start.2 = (bf16[256,1,256]{2,0,1:T(8,128)(2,1)S(1)}, bf16[256,1,256]{2,0,1:T(8,128)(2,1)S(1)}, u32[]{:S(2)}, u32[]{:S(2)}) collective-permute-start(bf16[256,1,256]{2,0,1:T(8,128)(2,1)S(1)} %bitcast.116), channel_id=1, source_target_pairs={{0,8},{8,16},{16,24},{24,32},{32,40},{40,48},{48,56},{56,64},{64,7... | collective-permute-start | bytes 393224 | tf_op jit(solution)/shard_map/ppermute | solution.py:15
  107.8 3.2 %collective-permute-done.3 = bf16[256,1,256]{2,0,1:T(8,128)(2,1)S(1)} collective-permute-done((bf16[256,1,256]{2,0,1:T(8,128)(2,1)S(1)}, bf16[256,1,256]{2,0,1:T(8,128)(2,1)S(1)}, u32[]{:S(2)}, u32[]{:S(2)}) %collective-permute-start.3) | collective-permute-done | bytes 131104 | tf_op jit(solution)/shard_map/ppermute | solution.py:18
  110.9 4.7 %collective-permute-done.2 = bf16[256,1,256]{2,0,1:T(8,128)(2,1)S(1)} collective-permute-done((bf16[256,1,256]{2,0,1:T(8,128)(2,1)S(1)}, bf16[256,1,256]{2,0,1:T(8,128)(2,1)S(1)}, u32[]{:S(2)}, u32[]{:S(2)}) %collective-permute-start.2) | collective-permute-done | bytes 131104 | tf_op jit(solution)/shard_map/ppermute | solution.py:15
  115.7 10.6 %fusion.35 = bf16[512,512]{0,1:T(8,128)(2,1)S(1)} fusion(bf16[8192,512]{1,0:T(8,128)(2,1)} %all-gather.3.cloned.1.call-done, bf16[512,8192]{1,0:T(8,128)(2,1)} %param.33, f32[8192]{0:T(1024)S(1)} %copy-done.11, f32[512]{0:T(512)S(1)} %add_rsqrt_fusion, f32[512]{0:T(512)S(1)} %copy-done.12), kind=kOutput, calls=%fused_computation.46 | convolution fusion | flops 4312268800 | bytes 17338368 | tf_op jit(solution)/shard_map/dot_general | solution.py:168
  127.4 1.4 fusion.11
  128.8 2.1 %fusion.32 = bf16[128,512,4]{1,0,2:T(8,128)(2,1)S(1)} fusion(f32[512,4]{0,1:T(4,128)S(1)} %fusion.11, f32[512,4]{0,1:T(4,128)S(1)} %get-tuple-element.6, f32[768,512,4]{1,0,2:T(8,128)S(1)} %get-tuple-element.7, pred[512,768]{0,1:T(8,128)(4,1)S(1)} %compare_and_fusion, bf16[768,1,256]{2,0,1:T(8,128)(2,1)S(1)} %pad_maximum_fusion), kind=kOutput, calls=%fused_computation.45 | convolution fusion | flops 410779648 | bytes 7421952 | tf_op jit(solution)/shard_map/rgqk,kgd->rgqd/dot_general | solution.py:189
  131.0 1.9 collective-permute-done.4
  133.0 1.5 collective-permute-start.6
  134.5 14.8 %collective-permute-done.6 = bf16[2,512,512]{1,2,0:T(8,128)(2,1)S(1)} collective-permute-done((bf16[2,512,512]{1,2,0:T(8,128)(2,1)S(1)}, bf16[2,512,512]{1,2,0:T(8,128)(2,1)S(1)}, u32[]{:S(2)}, u32[]{:S(2)}) %collective-permute-start.6) | collective-permute-done | bytes 1048608 | tf_op jit(solution)/shard_map/ppermute | solution.py:53
  149.3 25.4 %all-gather.5.cloned.1.call-done = bf16[512,8192]{1,0:T(8,128)(2,1)} async-done(((bf16[512,512]{1,0:T(8,128)(2,1)}), bf16[512,8192]{1,0:T(8,128)(2,1)}) %all-gather.5.cloned.1.call-update) | async-done | bytes 8388624 | tf_op jit(solution)/shard_map/all_gather | solution.py:203
  174.7 2.1 %convolution_convert_fusion.6 = bf16[512,1024]{1,0:T(8,128)(2,1)S(1)} fusion(bf16[512,8192]{1,0:T(8,128)(2,1)} %all-gather.5.cloned.1.call-done, s32[]{:T(128)S(6)} %select_n.88, bf16[2,512,512]{1,2,0:T(8,128)(2,1)S(1)} %maximum_select_fusion), kind=kOutput, calls=%fused_computation.32 | convolution fusion | flops 537395200 | bytes 2621444 | tf_op jit(solution)/shard_map/dot_general | solution.py:210
  176.8 2.5 %convolution_convert_fusion.7 = bf16[512,1024]{1,0:T(8,128)(2,1)S(1)} fusion(bf16[512,8192]{1,0:T(8,128)(2,1)} %all-gather.5.cloned.1.call-done, s32[]{:T(128)S(6)} %select_n.87, bf16[2,512,512]{1,2,0:T(8,128)(2,1)S(1)} %maximum_select_fusion), kind=kOutput, calls=%fused_computation.33 | convolution fusion | flops 537395200 | bytes 2621444 | tf_op jit(solution)/shard_map/dot_general | solution.py:210
  183.4 3.8 %add_convert_fusion = bf16[512,1024]{1,0:T(8,128)(2,1)} fusion(bf16[512,1024]{1,0:T(8,128)(2,1)S(1)} %convolution_convert_fusion.1, bf16[512,1024]{1,0:T(8,128)(2,1)S(1)} %convolution_convert_fusion.2, bf16[512,1024]{1,0:T(8,128)(2,1)S(1)} %convolution_convert_fusion.3, bf16[512,1024]{1,0:T(8,128)(2,1)S(1)} %convolution_convert_fusion.4, ...), kind=kOutput, calls=%fused_computation.20 | convolution fusion | flops 546832384 | bytes 11010056 | tf_op jit(solution)/shard_map/dot_general | solution.py:210
  (73 shorter events, 12.5 us)
Async XLA Ops:
  7.2 53.5 %copy-start = (bf16[128,1280]{1,0:T(8,128)(2,1)S(1)}, bf16[128,1280]{1,0:T(8,128)(2,1)}, u32[]{:S(2)}) copy-start(bf16[128,1280]{1,0:T(8,128)(2,1)} %param.28) | copy-start | bytes 983044
  7.2 48.0 %copy-start.9 = (f32[128]{0:T(128)S(1)}, f32[128]{0:T(128)}, u32[]{:S(2)}) copy-start(f32[128]{0:T(128)} %param.24) | copy-start | bytes 1540
  7.2 48.0 %copy-start.3 = (bf16[1280,128]{1,0:T(8,128)(2,1)S(1)}, bf16[1280,128]{1,0:T(8,128)(2,1)}, u32[]{:S(2)}) copy-start(bf16[1280,128]{1,0:T(8,128)(2,1)} %param.23) | copy-start | bytes 983044
  7.2 51.3 %copy-start.13 = (s32[2]{0:T(128)S(1)}, s32[2]{0:T(128)}, u32[]{:S(2)}) copy-start(s32[2]{0:T(128)} %param.30) | copy-start | bytes 28
  7.2 108.4 %all-gather.3.cloned.1.call-start = ((), (), s32[]{:S(2)}) async-start(), calls=%async_computation.2 | async-start | bytes 8912896 | tf_op jit(solution)/shard_map/all_gather | solution.py:170
  7.9 166.7 %all-gather.5.cloned.1.call-start = ((), (), s32[]{:S(2)}) async-start(), calls=%async_computation.3 | async-start | bytes 8912896 | tf_op jit(solution)/shard_map/all_gather | solution.py:203
  8.0 31.5 %collective-permute-start.5 = (bf16[512,512]{1,0:T(8,128)(2,1)}, bf16[512,512]{1,0:T(8,128)(2,1)S(1)}, u32[]{:S(2)}, u32[]{:S(2)}) collective-permute-start(bf16[512,512]{1,0:T(8,128)(2,1)} %param.37), channel_id=1, source_target_pairs={{0,0},{1,16},{2,32},{3,48},{4,64},{5,80},{6,96},{7,112},{8,8},{9,2... | collective-permute-start | bytes 1572872 | tf_op jit(solution)/shard_map/ppermute | solution.py:200
  39.5 0.8 copy-start.2
  47.0 8.6 %collective-permute-start = (bf16[128,2,128]{2,0,1:T(8,128)(2,1)S(1)}, bf16[128,2,128]{2,0,1:T(8,128)(2,1)S(1)}, u32[]{:S(2)}, u32[]{:S(2)}) collective-permute-start(bf16[128,2,128]{2,0,1:T(8,128)(2,1)S(1)} %get-tuple-element.4), channel_id=1, source_target_pairs={{0,8},{8,16},{16,24},{24,32},{32,40},{40,48},{48,56},{56,64},{64,7... | collective-permute-start | bytes 196616 | tf_op jit(solution)/shard_map/ppermute | solution.py:15
  50.4 7.5 %collective-permute-start.1 = (bf16[128,2,128]{2,0,1:T(8,128)(2,1)S(1)}, bf16[128,2,128]{2,0,1:T(8,128)(2,1)S(1)}, u32[]{:S(2)}, u32[]{:S(2)}) collective-permute-start(bf16[128,2,128]{2,0,1:T(8,128)(2,1)S(1)} %get-tuple-element.5), channel_id=1, source_target_pairs={{8,0},{16,8},{24,16},{32,24},{40,32},{48,40},{56,48},{64,56},{72,6... | collective-permute-start | bytes 196616 | tf_op jit(solution)/shard_map/ppermute | solution.py:18
  58.5 7.3 %copy-start.7 = (f32[8,128]{1,0:T(8,128)S(1)}, f32[8,128]{1,0:T(8,128)}, u32[]{:S(2)}) copy-start(f32[8,128]{1,0:T(8,128)} %param.32) | copy-start | bytes 12292
  62.1 11.0 %copy-start.5 = (s32[512]{0:T(512)S(1)}, s32[512]{0:T(512)}, u32[]{:S(2)}) copy-start(s32[512]{0:T(512)} %param.38) | copy-start | bytes 6148
  62.1 11.0 %copy-start.8 = (s32[512]{0:T(512)S(1)}, s32[512]{0:T(512)}, u32[]{:S(2)}) copy-start(s32[512]{0:T(512)} %param.39) | copy-start | bytes 6148
  62.1 22.4 %all-to-all-start = ((f32[8,32,1280]{2,1,0:T(8,128)}), f32[8,32,1280]{2,1,0:T(8,128)S(1)}, u32[]{:S(2)}, u32[]{:S(2)}) async-start(f32[8,32,1280]{2,1,0:T(8,128)} %fusion.55), calls=%async_computation | async-start | bytes 2621440 | tf_op jit(solution)/shard_map/all_to_all | solution.py:140
  73.1 11.5 %copy-start.6 = (f32[1280]{0:T(1024)S(1)}, f32[1280]{0:T(1024)}, u32[]{:S(2)}) copy-start(f32[1280]{0:T(1024)} %param.29) | copy-start | bytes 15364
  78.4 37.3 %copy-start.11 = (f32[8192]{0:T(1024)S(1)}, f32[8192]{0:T(1024)}, u32[]{:S(2)}) copy-start(f32[8192]{0:T(1024)} %param.34) | copy-start | bytes 98308
  78.4 37.3 %copy-start.12 = (f32[512]{0:T(512)S(1)}, f32[512]{0:T(512)}, u32[]{:S(2)}) copy-start(f32[512]{0:T(512)} %param.36) | copy-start | bytes 6148
  85.5 40.7 %copy-start.4 = (bf16[32,1280]{1,0:T(8,128)(2,1)}, bf16[32,1280]{1,0:T(8,128)(2,1)S(1)}, u32[]{:S(2)}) copy-start(bf16[32,1280]{1,0:T(8,128)(2,1)S(1)} %add_convert_fusion.1) | copy-start | bytes 245764
  89.7 9.4 %all-to-all-start.1 = ((bf16[32,8,256]{2,0,1:T(8,128)(2,1)}), bf16[32,8,256]{2,0,1:T(8,128)(2,1)S(1)}, u32[]{:S(2)}, u32[]{:S(2)}) async-start(bf16[32,8,256]{2,0,1:T(8,128)(2,1)} %bitcast.106), calls=%async_computation.1 | async-start | bytes 262144 | tf_op jit(solution)/shard_map/all_to_all | solution.py:160
  99.1 11.8 %collective-permute-start.3 = (bf16[256,1,256]{2,0,1:T(8,128)(2,1)S(1)}, bf16[256,1,256]{2,0,1:T(8,128)(2,1)S(1)}, u32[]{:S(2)}, u32[]{:S(2)}) collective-permute-start(bf16[256,1,256]{2,0,1:T(8,128)(2,1)S(1)} %bitcast.115), channel_id=1, source_target_pairs={{8,0},{16,8},{24,16},{32,24},{40,32},{48,40},{56,48},{64,56},{72,6... | collective-permute-start | bytes 393224 | tf_op jit(solution)/shard_map/ppermute | solution.py:18
  105.6 10.0 %collective-permute-start.2 = (bf16[256,1,256]{2,0,1:T(8,128)(2,1)S(1)}, bf16[256,1,256]{2,0,1:T(8,128)(2,1)S(1)}, u32[]{:S(2)}, u32[]{:S(2)}) collective-permute-start(bf16[256,1,256]{2,0,1:T(8,128)(2,1)S(1)} %bitcast.116), channel_id=1, source_target_pairs={{0,8},{8,16},{16,24},{24,32},{32,40},{40,48},{48,56},{56,64},{64,7... | collective-permute-start | bytes 393224 | tf_op jit(solution)/shard_map/ppermute | solution.py:15
  130.9 2.0 %collective-permute-start.4 = (bf16[512,512]{0,1:T(8,128)(2,1)S(1)}, bf16[512,512]{0,1:T(8,128)(2,1)S(1)}, u32[]{:S(2)}, u32[]{:S(2)}) collective-permute-start(bf16[512,512]{0,1:T(8,128)(2,1)S(1)} %bitcast.109), channel_id=1, source_target_pairs={{0,1},{1,0},{2,3},{3,2},{4,5},{5,4},{6,7},{7,6},{8,9},{9,8},{10,11... | collective-permute-start | bytes 1572872 | tf_op jit(solution)/shard_map/ppermute | solution.py:47
  133.0 16.3 %collective-permute-start.6 = (bf16[2,512,512]{1,2,0:T(8,128)(2,1)S(1)}, bf16[2,512,512]{1,2,0:T(8,128)(2,1)S(1)}, u32[]{:S(2)}, u32[]{:S(2)}) collective-permute-start(bf16[2,512,512]{1,2,0:T(8,128)(2,1)S(1)} %maximum_select_fusion), channel_id=1, source_target_pairs={{0,2},{1,7},{2,4},{3,1},{4,6},{5,3},{6,0},{7,5},{8,10},{9,15},{10,... | collective-permute-start | bytes 3145736 | tf_op jit(solution)/shard_map/ppermute | solution.py:53
  149.3 31.8 %collective-permute-start.7 = (bf16[2,512,512]{1,2,0:T(8,128)(2,1)S(1)}, bf16[2,512,512]{1,2,0:T(8,128)(2,1)S(1)}, u32[]{:S(2)}, u32[]{:S(2)}) collective-permute-start(bf16[2,512,512]{1,2,0:T(8,128)(2,1)S(1)} %collective-permute-done.6), channel_id=1, source_target_pairs={{0,2},{1,7},{2,4},{3,1},{4,6},{5,3},{6,0},{7,5},{8,10},{9,15},{10,... | collective-permute-start | bytes 3145736 | tf_op jit(solution)/shard_map/ppermute | solution.py:54
  174.6 4.9 %copy-start.10 = (bf16[512,8192]{1,0:T(8,128)(2,1)S(1)}, bf16[512,8192]{1,0:T(8,128)(2,1)}, u32[]{:S(2)}) copy-start(bf16[512,8192]{1,0:T(8,128)(2,1)} %all-gather.5.cloned.1.call-done) | copy-start | bytes 25165828
  179.2 3.4 %collective-permute-start.8 = (bf16[2,512,512]{1,2,0:T(8,128)(2,1)S(1)}, bf16[2,512,512]{1,2,0:T(8,128)(2,1)S(1)}, u32[]{:S(2)}, u32[]{:S(2)}) collective-permute-start(bf16[2,512,512]{1,2,0:T(8,128)(2,1)S(1)} %collective-permute-done.6), channel_id=1, source_target_pairs={{0,1},{1,0},{2,3},{3,2},{4,5},{5,4},{6,7},{7,6},{8,9},{9,8},{10,11... | collective-permute-start | bytes 3145736 | tf_op jit(solution)/shard_map/ppermute | solution.py:55
  182.6 4.5 %copy-start.1 = (bf16[128,1280]{1,0:T(8,128)(2,1)S(1)}, bf16[128,1280]{1,0:T(8,128)(2,1)}, u32[]{:S(2)}) copy-start(bf16[128,1280]{1,0:T(8,128)(2,1)} %param.28) | copy-start | bytes 983044
Sparse Core Ops, SparseCore 0:
  10.2 83.0 all-gather.2
  95.9 78.6 all-gather.4

commit v7 on v6

--- a/solution.py
+++ b/solution.py
@@ -138,8 +138,12 @@
     enc_term = jnp.dot(enc_context, enc_wo, preferred_element_type=jnp.float32)
     mixed = jnp.sum(
         lax.all_to_all(
-            enc_term.reshape(head_count, share, enc_width), "heads", 0, 0, tiled=True
-        ),
+            enc_term.astype(jnp.bfloat16).reshape(head_count, share, enc_width),
+            "heads",
+            0,
+            0,
+            tiled=True,
+        ).astype(jnp.float32),
         axis=0,
     )
     own_audio = lax.dynamic_slice_in_dim(audio, head_index * share, share, 0)

time: 198 us -> 195 us (0.985)
  starting transfers between devices: 29.1 us -> 25.3 us
    ppermute x2, waiting for transfers between devices: 5.47 us -> 0.89 us  [with_halo(): lax.ppermute(lax.slice_in_dim(block, 0, width, axis=dim), axis, backward)]
    ppermute x2, starting transfers between devices: 11 us -> 6.46 us  [with_halo(): lax.ppermute(lax.slice_in_dim(block, 0, width, axis=dim), axis, backward)]
    all_gather x1, waiting for transfers between devices: 25.4 us -> 29.7 us  [shards(): column_weight = lax.all_gather(piece, 'seq', axis=1, tiled=True)]
    ppermute x2, starting transfers between devices: 5.51 us -> 7.5 us  [with_halo(): lax.ppermute(lax.slice_in_dim(block, block.shape[dim] - width, None, axis...]
    unnamed x31 -> x27, local copies, waits for them, and re-layouts: 8.06 us -> 9.16 us
  transfers between devices with their start and end apart: 13 -> 13, of which waited for: 9 -> 8; matrix products, arithmetic and copies ran while one was open for 27% -> 28% of each run, Pallas kernels for 0% -> 0%
where the time goes in v7:
time: 195 us; the launch traced here: 191 us
  waiting for transfers between devices  92.9 us (48%)
  matrix products  35.2 us (18%)
  starting transfers between devices  25.3 us (13%)
  between operations  14.5 us (7%)
  other arithmetic  13.2 us (7%)
  local copies, waits for them, and re-layouts  10.1 us (5%)
    all_gather x1, waiting for transfers between devices, shards(): column_weight = lax.all_gather(piece, 'seq', axis=1, tiled=True)  29.7 us
    ppermute x1, waiting for transfers between devices, shards(): piece = lax.ppermute(dec_wo, ('seq', 'heads'), regroup)  27.9 us
    ppermute x1, waiting for transfers between devices, heads_ring_gather(): near = lax.ppermute(own, axis, step)  15.6 us
    dot_general x8, matrix products, shards(): term = jnp.dot(held[offset], weight_set, preferred_element_type=jnp.float32)  12.1 us
    dot_general x1, matrix products, shards(): jnp.dot(normed, lax.all_gather(dec_wq, 'seq', axis=0, tiled=True), prefer...  10.6 us
    unnamed x27, local copies, waits for them, and re-layouts  9.16 us
    ppermute x2, starting transfers between devices, with_halo(): lax.ppermute(lax.slice_in_dim(block, block.shape[dim] - width, None, axis...  7.5 us
    ppermute x2, starting transfers between devices, with_halo(): lax.ppermute(lax.slice_in_dim(block, 0, width, axis=dim), axis, backward)  6.46 us
  transfers between devices with their start and end apart: 13, of which 8 were waited for; matrix products, arithmetic and copies ran while one was open for 28% of the time, Pallas kernels for 0%

profile of v7, /device:TPU:96, one launch (start us, length us, event | category | flops | bytes accessed | tf_op | source)
XLA Modules:
  0.0 191.2 jit_solution(3535932592329753961)
XLA Ops:
  8.0 3.6 %collective-permute-start.5 = (bf16[512,512]{1,0:T(8,128)(2,1)}, bf16[512,512]{1,0:T(8,128)(2,1)S(1)}, u32[]{:S(2)}, u32[]{:S(2)}) collective-permute-start(bf16[512,512]{1,0:T(8,128)(2,1)} %param.37), channel_id=1, source_target_pairs={{0,0},{1,16},{2,32},{3,48},{4,64},{5,80},{6,96},{7,112},{8,8},{9,2... | collective-permute-start | bytes 1572872 | tf_op jit(solution)/shard_map/ppermute | solution.py:204
  11.5 27.9 %collective-permute-done.5 = bf16[512,512]{1,0:T(8,128)(2,1)S(1)} collective-permute-done((bf16[512,512]{1,0:T(8,128)(2,1)}, bf16[512,512]{1,0:T(8,128)(2,1)S(1)}, u32[]{:S(2)}, u32[]{:S(2)}) %collective-permute-start.5) | collective-permute-done | bytes 524320 | tf_op jit(solution)/shard_map/ppermute | solution.py:204
  40.3 1.3 convert_reduce_fusion
  41.5 1.4 fusion.25
  42.9 1.4 fusion.28
  44.4 1.3 fusion.40
  45.7 1.3 fusion.41
  47.1 3.4 %collective-permute-start = (bf16[128,2,128]{2,0,1:T(8,128)(2,1)S(1)}, bf16[128,2,128]{2,0,1:T(8,128)(2,1)S(1)}, u32[]{:S(2)}, u32[]{:S(2)}) collective-permute-start(bf16[128,2,128]{2,0,1:T(8,128)(2,1)S(1)} %get-tuple-element.4), channel_id=1, source_target_pairs={{0,8},{8,16},{16,24},{24,32},{32,40},{40,48},{48,56},{56,64},{64,7... | collective-permute-start | bytes 196616 | tf_op jit(solution)/shard_map/ppermute | solution.py:15
  50.5 4.6 %collective-permute-start.1 = (bf16[128,2,128]{2,0,1:T(8,128)(2,1)S(1)}, bf16[128,2,128]{2,0,1:T(8,128)(2,1)S(1)}, u32[]{:S(2)}, u32[]{:S(2)}) collective-permute-start(bf16[128,2,128]{2,0,1:T(8,128)(2,1)S(1)} %get-tuple-element.5), channel_id=1, source_target_pairs={{8,0},{16,8},{24,16},{32,24},{40,32},{48,40},{56,48},{64,56},{72,6... | collective-permute-start | bytes 196616 | tf_op jit(solution)/shard_map/ppermute | solution.py:18
  55.8 7.6 %copy.45 = bf16[160,8,8,256]{3,1,2,0:T(8,128)(2,1)} copy(bf16[160,8,8,256]{3,2,1,0:T(8,128)(2,1)} %bitcast.108) | data formatting | bytes 10485760
  65.3 1.2 convolution_convert_fusion.9
  66.6 1.2 convolution_convert_fusion
  67.8 3.5 %all-to-all-start = ((bf16[8,32,1280]{2,1,0:T(8,128)(2,1)}), bf16[8,32,1280]{2,1,0:T(8,128)(2,1)S(1)}, u32[]{:S(2)}, u32[]{:S(2)}) async-start(bf16[8,32,1280]{2,1,0:T(8,128)(2,1)} %bitcast.7), calls=%async_computation | async-start | bytes 1310720 | tf_op jit(solution)/shard_map/all_to_all | solution.py:140
  71.3 5.3 %fusion.1 = f32[512]{0:T(512)S(1)} fusion(bf16[512,8192]{1,0:T(8,128)(2,1)} %param.33), kind=kLoop, calls=%fused_computation.3 | loop fusion | flops 12582400 | bytes 8390656 | tf_op jit(solution)/shard_map/reduce_sum | solution.py:70
  76.6 6.3 %all-to-all-done = bf16[8,32,1280]{2,1,0:T(8,128)(2,1)S(1)} async-done(((bf16[8,32,1280]{2,1,0:T(8,128)(2,1)}), bf16[8,32,1280]{2,1,0:T(8,128)(2,1)S(1)}, u32[]{:S(2)}, u32[]{:S(2)}) %all-to-all-start) | async-done | bytes 655392 | tf_op jit(solution)/shard_map/all_to_all | solution.py:140
  83.1 0.9 add_convert_fusion.1
  84.0 3.5 %fusion.14 = bf16[32,2048]{1,0:T(8,128)(2,1)S(1)} fusion(bf16[32,1280]{1,0:T(8,128)(2,1)S(1)} %add_convert_fusion.1, bf16[1280,2048]{1,0:T(8,128)(2,1)} %bitcast.107, f32[2048]{0:T(1024)S(1)} %bitcast.121), kind=kOutput, calls=%fused_computation.20 | convolution fusion | flops 167903232 | bytes 5464064 | tf_op jit(solution)/shard_map/dot_general | solution.py:157
  88.2 3.4 %all-to-all-start.1 = ((bf16[32,8,256]{2,0,1:T(8,128)(2,1)}), bf16[32,8,256]{2,0,1:T(8,128)(2,1)S(1)}, u32[]{:S(2)}, u32[]{:S(2)}) async-start(bf16[32,8,256]{2,0,1:T(8,128)(2,1)} %bitcast.106), calls=%async_computation.1 | async-start | bytes 262144 | tf_op jit(solution)/shard_map/all_to_all | solution.py:164
  92.0 5.6 %all-to-all-done.1 = bf16[32,8,256]{2,0,1:T(8,128)(2,1)S(1)} async-done(((bf16[32,8,256]{2,0,1:T(8,128)(2,1)}), bf16[32,8,256]{2,0,1:T(8,128)(2,1)S(1)}, u32[]{:S(2)}, u32[]{:S(2)}) %all-to-all-start.1) | async-done | bytes 131104 | tf_op jit(solution)/shard_map/all_to_all | solution.py:164
  97.6 1.9 collective-permute-start.3
  99.5 4.1 %collective-permute-start.2 = (bf16[256,1,256]{2,0,1:T(8,128)(2,1)S(1)}, bf16[256,1,256]{2,0,1:T(8,128)(2,1)S(1)}, u32[]{:S(2)}, u32[]{:S(2)}) collective-permute-start(bf16[256,1,256]{2,0,1:T(8,128)(2,1)S(1)} %bitcast.116), channel_id=1, source_target_pairs={{0,8},{8,16},{16,24},{24,32},{32,40},{40,48},{48,56},{56,64},{64,7... | collective-permute-start | bytes 393224 | tf_op jit(solution)/shard_map/ppermute | solution.py:15
  104.6 4.1 %collective-permute-done.2 = bf16[256,1,256]{2,0,1:T(8,128)(2,1)S(1)} collective-permute-done((bf16[256,1,256]{2,0,1:T(8,128)(2,1)S(1)}, bf16[256,1,256]{2,0,1:T(8,128)(2,1)S(1)}, u32[]{:S(2)}, u32[]{:S(2)}) %collective-permute-start.2) | collective-permute-done | bytes 131104 | tf_op jit(solution)/shard_map/ppermute | solution.py:15
  108.8 10.6 %fusion.35 = bf16[512,512]{0,1:T(8,128)(2,1)S(1)} fusion(bf16[8192,512]{1,0:T(8,128)(2,1)} %all-gather.3.cloned.1.call-done, bf16[512,8192]{1,0:T(8,128)(2,1)} %param.33, f32[8192]{0:T(1024)S(1)} %copy-done.9, f32[512]{0:T(512)S(1)} %add_rsqrt_fusion, f32[512]{0:T(512)S(1)} %copy-done.10), kind=kOutput, calls=%fused_computation.48 | convolution fusion | flops 4312268800 | bytes 17338368 | tf_op jit(solution)/shard_map/dot_general | solution.py:172
  119.4 1.2 fusion.8
  120.5 1.4 fusion.11
  121.9 2.1 %fusion.32 = bf16[128,512,4]{1,0,2:T(8,128)(2,1)S(1)} fusion(f32[512,4]{0,1:T(4,128)S(1)} %fusion.11, f32[512,4]{0,1:T(4,128)S(1)} %get-tuple-element.6, f32[768,512,4]{1,0,2:T(8,128)S(1)} %get-tuple-element.7, pred[512,768]{0,1:T(8,128)(4,1)S(1)} %compare_and_fusion, bf16[768,1,256]{2,0,1:T(8,128)(2,1)S(1)} %pad_maximum_fusion), kind=kOutput, calls=%fused_computation.47 | convolution fusion | flops 410779648 | bytes 7421952 | tf_op jit(solution)/shard_map/rgqk,kgd->rgqd/dot_general | solution.py:193
  124.1 1.9 collective-permute-done.4
  126.6 15.6 %collective-permute-done.6 = bf16[2,512,512]{1,2,0:T(8,128)(2,1)S(1)} collective-permute-done((bf16[2,512,512]{1,2,0:T(8,128)(2,1)S(1)}, bf16[2,512,512]{1,2,0:T(8,128)(2,1)S(1)}, u32[]{:S(2)}, u32[]{:S(2)}) %collective-permute-start.6) | collective-permute-done | bytes 1048608 | tf_op jit(solution)/shard_map/ppermute | solution.py:53
  142.2 29.7 %all-gather.5.cloned.1.call-done = bf16[512,8192]{1,0:T(8,128)(2,1)} async-done(((bf16[512,512]{1,0:T(8,128)(2,1)}), bf16[512,8192]{1,0:T(8,128)(2,1)}) %all-gather.5.cloned.1.call-update) | async-done | bytes 8388624 | tf_op jit(solution)/shard_map/all_gather | solution.py:207
  172.0 2.1 %convolution_convert_fusion.7 = bf16[512,1024]{1,0:T(8,128)(2,1)S(1)} fusion(bf16[512,8192]{1,0:T(8,128)(2,1)} %all-gather.5.cloned.1.call-done, s32[]{:T(128)S(6)} %select_n.88, bf16[2,512,512]{1,2,0:T(8,128)(2,1)S(1)} %maximum_select_fusion), kind=kOutput, calls=%fused_computation.33 | convolution fusion | flops 537395200 | bytes 2621444 | tf_op jit(solution)/shard_map/dot_general | solution.py:214
  174.1 2.5 %convolution_convert_fusion.8 = bf16[512,1024]{1,0:T(8,128)(2,1)S(1)} fusion(bf16[512,8192]{1,0:T(8,128)(2,1)} %all-gather.5.cloned.1.call-done, s32[]{:T(128)S(6)} %select_n.87, bf16[2,512,512]{1,2,0:T(8,128)(2,1)S(1)} %maximum_select_fusion), kind=kOutput, calls=%fused_computation.34 | convolution fusion | flops 537395200 | bytes 2621444 | tf_op jit(solution)/shard_map/dot_general | solution.py:214
  180.6 3.8 %add_convert_fusion = bf16[512,1024]{1,0:T(8,128)(2,1)} fusion(bf16[512,1024]{1,0:T(8,128)(2,1)S(1)} %convolution_convert_fusion.2, bf16[512,1024]{1,0:T(8,128)(2,1)S(1)} %convolution_convert_fusion.3, bf16[512,1024]{1,0:T(8,128)(2,1)S(1)} %convolution_convert_fusion.4, bf16[512,1024]{1,0:T(8,128)(2,1)S(1)} %convolution_convert_fusion.5, ...), kind=kOutput, calls=%fused_computation.21 | convolution fusion | flops 546832384 | bytes 11010056 | tf_op jit(solution)/shard_map/dot_general | solution.py:214
  (67 shorter events, 11.0 us)
Async XLA Ops:
  7.2 59.4 %copy-start = (bf16[128,1280]{1,0:T(8,128)(2,1)S(1)}, bf16[128,1280]{1,0:T(8,128)(2,1)}, u32[]{:S(2)}) copy-start(bf16[128,1280]{1,0:T(8,128)(2,1)} %param.28) | copy-start | bytes 983044
  7.2 101.6 %all-gather.3.cloned.1.call-start = ((), (), s32[]{:S(2)}) async-start(), calls=%async_computation.2 | async-start | bytes 8912896 | tf_op jit(solution)/shard_map/all_gather | solution.py:174
  7.9 164.0 %all-gather.5.cloned.1.call-start = ((), (), s32[]{:S(2)}) async-start(), calls=%async_computation.3 | async-start | bytes 8912896 | tf_op jit(solution)/shard_map/all_gather | solution.py:207
  8.0 31.5 %collective-permute-start.5 = (bf16[512,512]{1,0:T(8,128)(2,1)}, bf16[512,512]{1,0:T(8,128)(2,1)S(1)}, u32[]{:S(2)}, u32[]{:S(2)}) collective-permute-start(bf16[512,512]{1,0:T(8,128)(2,1)} %param.37), channel_id=1, source_target_pairs={{0,0},{1,16},{2,32},{3,48},{4,64},{5,80},{6,96},{7,112},{8,8},{9,2... | collective-permute-start | bytes 1572872 | tf_op jit(solution)/shard_map/ppermute | solution.py:204
  39.4 0.8 copy-start.1
  44.4 19.0 %copy-start.4 = (s32[512]{0:T(512)S(1)}, s32[512]{0:T(512)}, u32[]{:S(2)}) copy-start(s32[512]{0:T(512)} %param.38) | copy-start | bytes 6148
  44.4 19.0 %copy-start.6 = (s32[512]{0:T(512)S(1)}, s32[512]{0:T(512)}, u32[]{:S(2)}) copy-start(s32[512]{0:T(512)} %param.39) | copy-start | bytes 6148
  45.7 17.9 %copy-start.2 = (bf16[1280,128]{1,0:T(8,128)(2,1)S(1)}, bf16[1280,128]{1,0:T(8,128)(2,1)}, u32[]{:S(2)}) copy-start(bf16[1280,128]{1,0:T(8,128)(2,1)} %param.23) | copy-start | bytes 983044
  45.7 17.9 %copy-start.7 = (f32[128]{0:T(128)S(1)}, f32[128]{0:T(128)}, u32[]{:S(2)}) copy-start(f32[128]{0:T(128)} %param.24) | copy-start | bytes 1540
  47.1 16.9 %collective-permute-start = (bf16[128,2,128]{2,0,1:T(8,128)(2,1)S(1)}, bf16[128,2,128]{2,0,1:T(8,128)(2,1)S(1)}, u32[]{:S(2)}, u32[]{:S(2)}) collective-permute-start(bf16[128,2,128]{2,0,1:T(8,128)(2,1)S(1)} %get-tuple-element.4), channel_id=1, source_target_pairs={{0,8},{8,16},{16,24},{24,32},{32,40},{40,48},{48,56},{56,64},{64,7... | collective-permute-start | bytes 196616 | tf_op jit(solution)/shard_map/ppermute | solution.py:15
  50.5 13.5 %collective-permute-start.1 = (bf16[128,2,128]{2,0,1:T(8,128)(2,1)S(1)}, bf16[128,2,128]{2,0,1:T(8,128)(2,1)S(1)}, u32[]{:S(2)}, u32[]{:S(2)}) collective-permute-start(bf16[128,2,128]{2,0,1:T(8,128)(2,1)S(1)} %get-tuple-element.5), channel_id=1, source_target_pairs={{8,0},{16,8},{24,16},{32,24},{40,32},{48,40},{56,48},{64,56},{72,6... | collective-permute-start | bytes 196616 | tf_op jit(solution)/shard_map/ppermute | solution.py:18
  55.8 8.9 %copy-start.11 = (s32[2]{0:T(128)S(1)}, s32[2]{0:T(128)}, u32[]{:S(2)}) copy-start(s32[2]{0:T(128)} %param.30) | copy-start | bytes 28
  66.5 16.5 %copy-start.5 = (f32[1280]{0:T(1024)S(1)}, f32[1280]{0:T(1024)}, u32[]{:S(2)}) copy-start(f32[1280]{0:T(1024)} %param.29) | copy-start | bytes 15364
  67.8 15.2 %all-to-all-start = ((bf16[8,32,1280]{2,1,0:T(8,128)(2,1)}), bf16[8,32,1280]{2,1,0:T(8,128)(2,1)S(1)}, u32[]{:S(2)}, u32[]{:S(2)}) async-start(bf16[8,32,1280]{2,1,0:T(8,128)(2,1)} %bitcast.7), calls=%async_computation | async-start | bytes 1310720 | tf_op jit(solution)/shard_map/all_to_all | solution.py:140
  71.3 37.4 %copy-start.9 = (f32[8192]{0:T(1024)S(1)}, f32[8192]{0:T(1024)}, u32[]{:S(2)}) copy-start(f32[8192]{0:T(1024)} %param.34) | copy-start | bytes 98308
  71.3 37.4 %copy-start.10 = (f32[512]{0:T(512)S(1)}, f32[512]{0:T(512)}, u32[]{:S(2)}) copy-start(f32[512]{0:T(512)} %param.36) | copy-start | bytes 6148
  84.0 35.4 %copy-start.3 = (bf16[32,1280]{1,0:T(8,128)(2,1)}, bf16[32,1280]{1,0:T(8,128)(2,1)S(1)}, u32[]{:S(2)}) copy-start(bf16[32,1280]{1,0:T(8,128)(2,1)S(1)} %add_convert_fusion.1) | copy-start | bytes 245764
  88.2 9.4 %all-to-all-start.1 = ((bf16[32,8,256]{2,0,1:T(8,128)(2,1)}), bf16[32,8,256]{2,0,1:T(8,128)(2,1)S(1)}, u32[]{:S(2)}, u32[]{:S(2)}) async-start(bf16[32,8,256]{2,0,1:T(8,128)(2,1)} %bitcast.106), calls=%async_computation.1 | async-start | bytes 262144 | tf_op jit(solution)/shard_map/all_to_all | solution.py:164
  97.6 6.9 %collective-permute-start.3 = (bf16[256,1,256]{2,0,1:T(8,128)(2,1)S(1)}, bf16[256,1,256]{2,0,1:T(8,128)(2,1)S(1)}, u32[]{:S(2)}, u32[]{:S(2)}) collective-permute-start(bf16[256,1,256]{2,0,1:T(8,128)(2,1)S(1)} %bitcast.115), channel_id=1, source_target_pairs={{8,0},{16,8},{24,16},{32,24},{40,32},{48,40},{56,48},{64,56},{72,6... | collective-permute-start | bytes 393224 | tf_op jit(solution)/shard_map/ppermute | solution.py:18
  99.5 9.1 %collective-permute-start.2 = (bf16[256,1,256]{2,0,1:T(8,128)(2,1)S(1)}, bf16[256,1,256]{2,0,1:T(8,128)(2,1)S(1)}, u32[]{:S(2)}, u32[]{:S(2)}) collective-permute-start(bf16[256,1,256]{2,0,1:T(8,128)(2,1)S(1)} %bitcast.116), channel_id=1, source_target_pairs={{0,8},{8,16},{16,24},{24,32},{32,40},{40,48},{48,56},{56,64},{64,7... | collective-permute-start | bytes 393224 | tf_op jit(solution)/shard_map/ppermute | solution.py:15
  124.0 2.0 %collective-permute-start.4 = (bf16[512,512]{0,1:T(8,128)(2,1)S(1)}, bf16[512,512]{0,1:T(8,128)(2,1)S(1)}, u32[]{:S(2)}, u32[]{:S(2)}) collective-permute-start(bf16[512,512]{0,1:T(8,128)(2,1)S(1)} %bitcast.109), channel_id=1, source_target_pairs={{0,1},{1,0},{2,3},{3,2},{4,5},{5,4},{6,7},{7,6},{8,9},{9,8},{10,11... | collective-permute-start | bytes 1572872 | tf_op jit(solution)/shard_map/ppermute | solution.py:47
  126.1 16.1 %collective-permute-start.6 = (bf16[2,512,512]{1,2,0:T(8,128)(2,1)S(1)}, bf16[2,512,512]{1,2,0:T(8,128)(2,1)S(1)}, u32[]{:S(2)}, u32[]{:S(2)}) collective-permute-start(bf16[2,512,512]{1,2,0:T(8,128)(2,1)S(1)} %maximum_select_fusion), channel_id=1, source_target_pairs={{0,2},{1,7},{2,4},{3,1},{4,6},{5,3},{6,0},{7,5},{8,10},{9,15},{10,... | collective-permute-start | bytes 3145736 | tf_op jit(solution)/shard_map/ppermute | solution.py:53
  142.2 36.2 %collective-permute-start.7 = (bf16[2,512,512]{1,2,0:T(8,128)(2,1)S(1)}, bf16[2,512,512]{1,2,0:T(8,128)(2,1)S(1)}, u32[]{:S(2)}, u32[]{:S(2)}) collective-permute-start(bf16[2,512,512]{1,2,0:T(8,128)(2,1)S(1)} %collective-permute-done.6), channel_id=1, source_target_pairs={{0,2},{1,7},{2,4},{3,1},{4,6},{5,3},{6,0},{7,5},{8,10},{9,15},{10,... | collective-permute-start | bytes 3145736 | tf_op jit(solution)/shard_map/ppermute | solution.py:54
  172.0 4.9 %copy-start.8 = (bf16[512,8192]{1,0:T(8,128)(2,1)S(1)}, bf16[512,8192]{1,0:T(8,128)(2,1)}, u32[]{:S(2)}) copy-start(bf16[512,8192]{1,0:T(8,128)(2,1)} %all-gather.5.cloned.1.call-done) | copy-start | bytes 25165828
  176.5 3.4 %collective-permute-start.8 = (bf16[2,512,512]{1,2,0:T(8,128)(2,1)S(1)}, bf16[2,512,512]{1,2,0:T(8,128)(2,1)S(1)}, u32[]{:S(2)}, u32[]{:S(2)}) collective-permute-start(bf16[2,512,512]{1,2,0:T(8,128)(2,1)S(1)} %collective-permute-done.6), channel_id=1, source_target_pairs={{0,1},{1,0},{2,3},{3,2},{4,5},{5,4},{6,7},{7,6},{8,9},{9,8},{10,11... | collective-permute-start | bytes 3145736 | tf_op jit(solution)/shard_map/ppermute | solution.py:55
Sparse Core Ops, SparseCore 0:
  10.1 83.0 all-gather.2
  95.3 76.6 all-gather.4

commit v8 on v7

--- a/solution.py
+++ b/solution.py
@@ -201,7 +201,8 @@
     regroup = [
         (c * head_count + j, (ratio * j + c % ratio) * head_count + c // ratio) for c, j in flat
     ]
-    piece = lax.ppermute(dec_wo, ("seq", "heads"), regroup)
+    held_wo, _ = lax.optimization_barrier((dec_wo, enc_out))
+    piece = lax.ppermute(held_wo, ("seq", "heads"), regroup)
     pieces, owners = heads_ring_gather(dec_context, "heads")
     set_cols = ratio * block_cols
     column_weight = lax.all_gather(piece, "seq", axis=1, tiled=True)

time: 195 us -> 207 us (1.062)
  waiting for transfers between devices: 92.9 us -> 106 us
    all_gather x1, waiting for transfers between devices: 29.7 us -> 37.1 us  [shards(): column_weight = lax.all_gather(piece, 'seq', axis=1, tiled=True)]
    all_to_all x1, waiting for transfers between devices: 6.35 us -> 11.6 us  [shards(): lax.all_to_all(enc_term.astype(jnp.bfloat16).reshape(head_count, share, e...]
    ppermute x2, starting transfers between devices: 6.46 us -> 10.7 us  [with_halo(): lax.ppermute(lax.slice_in_dim(block, 0, width, axis=dim), axis, backward)]
    ppermute x2, waiting for transfers between devices: 4.14 us -> 0.89 us  [with_halo(): lax.ppermute(lax.slice_in_dim(block, block.shape[dim] - width, None, axis...]
    dot_general x1, matrix products: 3.54 us -> 1.02 us  [shards(): jnp.dot(enc_out, dec_wkv.reshape(enc_width, groups * pair_width), preferr...]
    ppermute x2, waiting for transfers between devices: 0.89 us -> 3.1 us  [with_halo(): lax.ppermute(lax.slice_in_dim(block, 0, width, axis=dim), axis, backward)]
    ppermute x2, starting transfers between devices: 7.5 us -> 5.41 us  [with_halo(): lax.ppermute(lax.slice_in_dim(block, block.shape[dim] - width, None, axis...]
    unnamed x27 -> x29, local copies, waits for them, and re-layouts: 9.16 us -> 7.97 us
  transfers between devices with their start and end apart: 13 -> 13, of which waited for: 8 -> 9; matrix products, arithmetic and copies ran while one was open for 28% -> 25% of each run, Pallas kernels for 0% -> 0%
where the time goes in v8:
time: 207 us; the launch traced here: 203 us
  waiting for transfers between devices  106 us (51%)
  matrix products  33.9 us (16%)
  starting transfers between devices  26.9 us (13%)
  between operations  14.5 us (7%)
  other arithmetic  13.2 us (6%)
  local copies, waits for them, and re-layouts  8.89 us (4%)
    all_gather x1, waiting for transfers between devices, shards(): column_weight = lax.all_gather(piece, 'seq', axis=1, tiled=True)  37.1 us
    ppermute x1, waiting for transfers between devices, shards(): piece = lax.ppermute(held_wo, ('seq', 'heads'), regroup)  29.2 us
    ppermute x1, waiting for transfers between devices, heads_ring_gather(): near = lax.ppermute(own, axis, step)  15.5 us
    dot_general x8, matrix products, shards(): term = jnp.dot(held[offset], weight_set, preferred_element_type=jnp.float32)  12.1 us
    all_to_all x1, waiting for transfers between devices, shards(): lax.all_to_all(enc_term.astype(jnp.bfloat16).reshape(head_count, share, e...  11.6 us
    dot_general x1, matrix products, shards(): jnp.dot(normed, lax.all_gather(dec_wq, 'seq', axis=0, tiled=True), prefer...  10.9 us
    ppermute x2, starting transfers between devices, with_halo(): lax.ppermute(lax.slice_in_dim(block, 0, width, axis=dim), axis, backward)  10.7 us
    unnamed x29, local copies, waits for them, and re-layouts  7.97 us
  transfers between devices with their start and end apart: 13, of which 9 were waited for; matrix products, arithmetic and copies ran while one was open for 25% of the time, Pallas kernels for 0%

profile of v8, /device:TPU:96, one launch (start us, length us, event | category | flops | bytes accessed | tf_op | source)
XLA Modules:
  0.0 203.1 jit_solution(11348163624634616580)
XLA Ops:
  7.9 1.3 convert_reduce_fusion
  9.2 1.4 fusion.25
  10.6 1.4 fusion.28
  12.0 1.3 fusion.40
  13.3 1.3 fusion.41
  14.6 3.4 %collective-permute-start = (bf16[128,2,128]{2,0,1:T(8,128)(2,1)S(1)}, bf16[128,2,128]{2,0,1:T(8,128)(2,1)S(1)}, u32[]{:S(2)}, u32[]{:S(2)}) collective-permute-start(bf16[128,2,128]{2,0,1:T(8,128)(2,1)S(1)} %get-tuple-element.6), channel_id=1, source_target_pairs={{0,8},{8,16},{16,24},{24,32},{32,40},{40,48},{48,56},{56,64},{64,7... | collective-permute-start | bytes 196616 | tf_op jit(solution)/shard_map/ppermute | solution.py:15
  18.1 4.6 %collective-permute-start.1 = (bf16[128,2,128]{2,0,1:T(8,128)(2,1)S(1)}, bf16[128,2,128]{2,0,1:T(8,128)(2,1)S(1)}, u32[]{:S(2)}, u32[]{:S(2)}) collective-permute-start(bf16[128,2,128]{2,0,1:T(8,128)(2,1)S(1)} %get-tuple-element.7), channel_id=1, source_target_pairs={{8,0},{16,8},{24,16},{32,24},{40,32},{48,40},{56,48},{64,56},{72,6... | collective-permute-start | bytes 196616 | tf_op jit(solution)/shard_map/ppermute | solution.py:18
  22.8 1.4 fusion.39
  24.2 1.7 collective-permute-done.1
  27.2 1.2 convolution_convert_fusion.9
  28.4 1.2 convolution_convert_fusion
  29.6 4.6 %all-to-all-start = ((bf16[8,32,1280]{2,1,0:T(8,128)(2,1)}), bf16[8,32,1280]{2,1,0:T(8,128)(2,1)S(1)}, u32[]{:S(2)}, u32[]{:S(2)}) async-start(bf16[8,32,1280]{2,1,0:T(8,128)(2,1)} %bitcast.7), calls=%async_computation | async-start | bytes 1310720 | tf_op jit(solution)/shard_map/all_to_all | solution.py:140
  34.2 11.6 %all-to-all-done = bf16[8,32,1280]{2,1,0:T(8,128)(2,1)S(1)} async-done(((bf16[8,32,1280]{2,1,0:T(8,128)(2,1)}), bf16[8,32,1280]{2,1,0:T(8,128)(2,1)S(1)}, u32[]{:S(2)}, u32[]{:S(2)}) %all-to-all-start) | async-done | bytes 655392 | tf_op jit(solution)/shard_map/all_to_all | solution.py:140
  46.9 1.9 collective-permute-start.5
  48.8 29.2 %collective-permute-done.5 = bf16[512,512]{1,0:T(8,128)(2,1)S(1)} collective-permute-done((bf16[512,512]{1,0:T(8,128)(2,1)S(1)}, bf16[512,512]{1,0:T(8,128)(2,1)S(1)}, u32[]{:S(2)}, u32[]{:S(2)}) %collective-permute-start.5) | collective-permute-done | bytes 524320 | tf_op jit(solution)/shard_map/ppermute | solution.py:205
  78.9 7.1 %copy.45 = bf16[160,8,8,256]{3,1,2,0:T(8,128)(2,1)} copy(bf16[160,8,8,256]{3,2,1,0:T(8,128)(2,1)} %bitcast.108) | data formatting | bytes 10485760
  86.1 5.3 %fusion.1 = f32[512]{0:T(512)S(1)} fusion(bf16[512,8192]{1,0:T(8,128)(2,1)} %param.33), kind=kLoop, calls=%fused_computation.3 | loop fusion | flops 12582400 | bytes 8390656 | tf_op jit(solution)/shard_map/reduce_sum | solution.py:70
  93.0 3.4 %all-to-all-start.1 = ((bf16[32,8,256]{2,0,1:T(8,128)(2,1)}), bf16[32,8,256]{2,0,1:T(8,128)(2,1)S(1)}, u32[]{:S(2)}, u32[]{:S(2)}) async-start(bf16[32,8,256]{2,0,1:T(8,128)(2,1)} %bitcast.106), calls=%async_computation.1 | async-start | bytes 262144 | tf_op jit(solution)/shard_map/all_to_all | solution.py:164
  96.8 5.6 %all-to-all-done.1 = bf16[32,8,256]{2,0,1:T(8,128)(2,1)S(1)} async-done(((bf16[32,8,256]{2,0,1:T(8,128)(2,1)}), bf16[32,8,256]{2,0,1:T(8,128)(2,1)S(1)}, u32[]{:S(2)}, u32[]{:S(2)}) %all-to-all-start.1) | async-done | bytes 131104 | tf_op jit(solution)/shard_map/all_to_all | solution.py:164
  102.4 2.0 collective-permute-start.2
  104.5 6.1 %collective-permute-start.3 = (bf16[256,1,256]{2,0,1:T(8,128)(2,1)S(1)}, bf16[256,1,256]{2,0,1:T(8,128)(2,1)S(1)}, u32[]{:S(2)}, u32[]{:S(2)}) collective-permute-start(bf16[256,1,256]{2,0,1:T(8,128)(2,1)S(1)} %bitcast.116), channel_id=1, source_target_pairs={{8,0},{16,8},{24,16},{32,24},{40,32},{48,40},{56,48},{64,56},{72,6... | collective-permute-start | bytes 393224 | tf_op jit(solution)/shard_map/ppermute | solution.py:18
  111.5 1.4 collective-permute-done.3
  113.0 10.9 %fusion.35 = bf16[512,512]{0,1:T(8,128)(2,1)S(1)} fusion(bf16[8192,512]{1,0:T(8,128)(2,1)} %all-gather.3.cloned.1.call-done, bf16[512,8192]{1,0:T(8,128)(2,1)} %param.33, f32[8192]{0:T(1024)S(1)} %copy-done.10, f32[512]{0:T(512)S(1)} %add_rsqrt_fusion, f32[512]{0:T(512)S(1)} %copy-done.11), kind=kOutput, calls=%fused_computation.48 | convolution fusion | flops 4312268800 | bytes 17338368 | tf_op jit(solution)/shard_map/dot_general | solution.py:172
  123.9 1.2 fusion.8
  125.0 1.4 fusion.11
  126.4 2.1 %fusion.32 = bf16[128,512,4]{1,0,2:T(8,128)(2,1)S(1)} fusion(f32[512,4]{0,1:T(4,128)S(1)} %fusion.11, f32[512,4]{0,1:T(4,128)S(1)} %get-tuple-element.8, f32[768,512,4]{1,0,2:T(8,128)S(1)} %get-tuple-element.9, pred[512,768]{0,1:T(8,128)(4,1)S(1)} %compare_and_fusion, bf16[768,1,256]{2,0,1:T(8,128)(2,1)S(1)} %pad_maximum_fusion), kind=kOutput, calls=%fused_computation.47 | convolution fusion | flops 410779648 | bytes 7421952 | tf_op jit(solution)/shard_map/rgqk,kgd->rgqd/dot_general | solution.py:193
  128.6 1.9 collective-permute-done.4
  131.2 15.5 %collective-permute-done.6 = bf16[2,512,512]{1,2,0:T(8,128)(2,1)S(1)} collective-permute-done((bf16[2,512,512]{1,2,0:T(8,128)(2,1)S(1)}, bf16[2,512,512]{1,2,0:T(8,128)(2,1)S(1)}, u32[]{:S(2)}, u32[]{:S(2)}) %collective-permute-start.6) | collective-permute-done | bytes 1048608 | tf_op jit(solution)/shard_map/ppermute | solution.py:53
  146.8 37.1 %all-gather.5.cloned.1.call-done = bf16[512,8192]{1,0:T(8,128)(2,1)} async-done(((bf16[512,512]{1,0:T(8,128)(2,1)}), bf16[512,8192]{1,0:T(8,128)(2,1)}) %all-gather.5.cloned.1.call-update) | async-done | bytes 8388624 | tf_op jit(solution)/shard_map/all_gather | solution.py:208
  183.8 2.1 %convolution_convert_fusion.7 = bf16[512,1024]{1,0:T(8,128)(2,1)S(1)} fusion(bf16[512,8192]{1,0:T(8,128)(2,1)} %all-gather.5.cloned.1.call-done, s32[]{:T(128)S(6)} %select_n.88, bf16[2,512,512]{1,2,0:T(8,128)(2,1)S(1)} %maximum_select_fusion), kind=kOutput, calls=%fused_computation.33 | convolution fusion | flops 537395200 | bytes 2621444 | tf_op jit(solution)/shard_map/dot_general | solution.py:215
  185.9 2.5 %convolution_convert_fusion.8 = bf16[512,1024]{1,0:T(8,128)(2,1)S(1)} fusion(bf16[512,8192]{1,0:T(8,128)(2,1)} %all-gather.5.cloned.1.call-done, s32[]{:T(128)S(6)} %select_n.87, bf16[2,512,512]{1,2,0:T(8,128)(2,1)S(1)} %maximum_select_fusion), kind=kOutput, calls=%fused_computation.34 | convolution fusion | flops 537395200 | bytes 2621444 | tf_op jit(solution)/shard_map/dot_general | solution.py:215
  192.5 3.8 %add_convert_fusion = bf16[512,1024]{1,0:T(8,128)(2,1)} fusion(bf16[512,1024]{1,0:T(8,128)(2,1)S(1)} %convolution_convert_fusion.2, bf16[512,1024]{1,0:T(8,128)(2,1)S(1)} %convolution_convert_fusion.3, bf16[512,1024]{1,0:T(8,128)(2,1)S(1)} %convolution_convert_fusion.4, bf16[512,1024]{1,0:T(8,128)(2,1)S(1)} %convolution_convert_fusion.5, ...), kind=kOutput, calls=%fused_computation.21 | convolution fusion | flops 546832384 | bytes 11010056 | tf_op jit(solution)/shard_map/dot_general | solution.py:215
  (69 shorter events, 11.9 us)
Async XLA Ops:
  7.2 21.2 %copy-start = (bf16[128,1280]{1,0:T(8,128)(2,1)S(1)}, bf16[128,1280]{1,0:T(8,128)(2,1)}, u32[]{:S(2)}) copy-start(bf16[128,1280]{1,0:T(8,128)(2,1)} %param.28) | copy-start | bytes 983044
  7.2 19.3 %copy-start.12 = (s32[2]{0:T(128)S(1)}, s32[2]{0:T(128)}, u32[]{:S(2)}) copy-start(s32[2]{0:T(128)} %param.30) | copy-start | bytes 28
  7.2 105.8 %all-gather.3.cloned.1.call-start = ((), (), s32[]{:S(2)}) async-start(), calls=%async_computation.2 | async-start | bytes 8912896 | tf_op jit(solution)/shard_map/all_gather | solution.py:174
  14.6 9.5 %collective-permute-start = (bf16[128,2,128]{2,0,1:T(8,128)(2,1)S(1)}, bf16[128,2,128]{2,0,1:T(8,128)(2,1)S(1)}, u32[]{:S(2)}, u32[]{:S(2)}) collective-permute-start(bf16[128,2,128]{2,0,1:T(8,128)(2,1)S(1)} %get-tuple-element.6), channel_id=1, source_target_pairs={{0,8},{8,16},{16,24},{24,32},{32,40},{40,48},{48,56},{56,64},{64,7... | collective-permute-start | bytes 196616 | tf_op jit(solution)/shard_map/ppermute | solution.py:15
  18.1 7.8 %collective-permute-start.1 = (bf16[128,2,128]{2,0,1:T(8,128)(2,1)S(1)}, bf16[128,2,128]{2,0,1:T(8,128)(2,1)S(1)}, u32[]{:S(2)}, u32[]{:S(2)}) collective-permute-start(bf16[128,2,128]{2,0,1:T(8,128)(2,1)S(1)} %get-tuple-element.7), channel_id=1, source_target_pairs={{8,0},{16,8},{24,16},{32,24},{40,32},{48,40},{56,48},{64,56},{72,6... | collective-permute-start | bytes 196616 | tf_op jit(solution)/shard_map/ppermute | solution.py:18
  26.1 19.8 %copy-start.5 = (f32[1280]{0:T(1024)S(1)}, f32[1280]{0:T(1024)}, u32[]{:S(2)}) copy-start(f32[1280]{0:T(1024)} %param.29) | copy-start | bytes 15364
  26.2 20.7 %copy-start.9 = (bf16[512,512]{1,0:T(8,128)(2,1)S(1)}, bf16[512,512]{1,0:T(8,128)(2,1)}, u32[]{:S(2)}) copy-start(bf16[512,512]{1,0:T(8,128)(2,1)} %param.37) | copy-start | bytes 1572868
  29.6 16.3 %all-to-all-start = ((bf16[8,32,1280]{2,1,0:T(8,128)(2,1)}), bf16[8,32,1280]{2,1,0:T(8,128)(2,1)S(1)}, u32[]{:S(2)}, u32[]{:S(2)}) async-start(bf16[8,32,1280]{2,1,0:T(8,128)(2,1)} %bitcast.7), calls=%async_computation | async-start | bytes 1310720 | tf_op jit(solution)/shard_map/all_to_all | solution.py:140
  34.1 51.8 %copy-start.6 = (f32[8,128]{1,0:T(8,128)S(1)}, f32[8,128]{1,0:T(8,128)}, u32[]{:S(2)}) copy-start(f32[8,128]{1,0:T(8,128)} %param.32) | copy-start | bytes 12292
  34.1 51.9 %copy-start.4 = (s32[512]{0:T(512)S(1)}, s32[512]{0:T(512)}, u32[]{:S(2)}) copy-start(s32[512]{0:T(512)} %param.38) | copy-start | bytes 6148
  34.2 51.9 %copy-start.7 = (s32[512]{0:T(512)S(1)}, s32[512]{0:T(512)}, u32[]{:S(2)}) copy-start(s32[512]{0:T(512)} %param.39) | copy-start | bytes 6148
  34.2 149.6 %all-gather.5.cloned.1.call-start = ((), (), s32[]{:S(2)}) async-start(), calls=%async_computation.3 | async-start | bytes 8912896 | tf_op jit(solution)/shard_map/all_gather | solution.py:208
  46.9 77.0 %copy-start.3 = (bf16[32,1280]{1,0:T(8,128)(2,1)}, bf16[32,1280]{1,0:T(8,128)(2,1)S(1)}, u32[]{:S(2)}) copy-start(bf16[32,1280]{1,0:T(8,128)(2,1)S(1)} %add_convert_fusion.1) | copy-start | bytes 245764
  46.9 31.2 %collective-permute-start.5 = (bf16[512,512]{1,0:T(8,128)(2,1)S(1)}, bf16[512,512]{1,0:T(8,128)(2,1)S(1)}, u32[]{:S(2)}, u32[]{:S(2)}) collective-permute-start(bf16[512,512]{1,0:T(8,128)(2,1)S(1)} %copy-done.9), channel_id=1, source_target_pairs={{0,0},{1,16},{2,32},{3,48},{4,64},{5,80},{6,96},{7,112},{8,8},{9,2... | collective-permute-start | bytes 1572872 | tf_op jit(solution)/shard_map/ppermute | solution.py:205
  78.1 0.8 copy-start.2
  86.0 5.3 %copy-start.1 = (bf16[160,8,8,256]{3,1,2,0:T(8,128)(2,1)S(1)}, bf16[160,8,8,256]{3,1,2,0:T(8,128)(2,1)}, u32[]{:S(2)}) copy-start(bf16[160,8,8,256]{3,1,2,0:T(8,128)(2,1)} %copy.45) | copy-start | bytes 15728644
  86.1 26.9 %copy-start.10 = (f32[8192]{0:T(1024)S(1)}, f32[8192]{0:T(1024)}, u32[]{:S(2)}) copy-start(f32[8192]{0:T(1024)} %param.34) | copy-start | bytes 98308
  86.1 26.9 %copy-start.11 = (f32[512]{0:T(512)S(1)}, f32[512]{0:T(512)}, u32[]{:S(2)}) copy-start(f32[512]{0:T(512)} %param.36) | copy-start | bytes 6148
  93.0 9.4 %all-to-all-start.1 = ((bf16[32,8,256]{2,0,1:T(8,128)(2,1)}), bf16[32,8,256]{2,0,1:T(8,128)(2,1)S(1)}, u32[]{:S(2)}, u32[]{:S(2)}) async-start(bf16[32,8,256]{2,0,1:T(8,128)(2,1)} %bitcast.106), calls=%async_computation.1 | async-start | bytes 262144 | tf_op jit(solution)/shard_map/all_to_all | solution.py:164
  102.4 9.0 %collective-permute-start.2 = (bf16[256,1,256]{2,0,1:T(8,128)(2,1)S(1)}, bf16[256,1,256]{2,0,1:T(8,128)(2,1)S(1)}, u32[]{:S(2)}, u32[]{:S(2)}) collective-permute-start(bf16[256,1,256]{2,0,1:T(8,128)(2,1)S(1)} %bitcast.115), channel_id=1, source_target_pairs={{0,8},{8,16},{16,24},{24,32},{32,40},{40,48},{48,56},{56,64},{64,7... | collective-permute-start | bytes 393224 | tf_op jit(solution)/shard_map/ppermute | solution.py:15
  104.5 8.4 %collective-permute-start.3 = (bf16[256,1,256]{2,0,1:T(8,128)(2,1)S(1)}, bf16[256,1,256]{2,0,1:T(8,128)(2,1)S(1)}, u32[]{:S(2)}, u32[]{:S(2)}) collective-permute-start(bf16[256,1,256]{2,0,1:T(8,128)(2,1)S(1)} %bitcast.116), channel_id=1, source_target_pairs={{8,0},{16,8},{24,16},{32,24},{40,32},{48,40},{56,48},{64,56},{72,6... | collective-permute-start | bytes 393224 | tf_op jit(solution)/shard_map/ppermute | solution.py:18
  128.5 2.0 collective-permute-start.4
  130.7 16.1 %collective-permute-start.6 = (bf16[2,512,512]{1,2,0:T(8,128)(2,1)S(1)}, bf16[2,512,512]{1,2,0:T(8,128)(2,1)S(1)}, u32[]{:S(2)}, u32[]{:S(2)}) collective-permute-start(bf16[2,512,512]{1,2,0:T(8,128)(2,1)S(1)} %maximum_select_fusion), channel_id=1, source_target_pairs={{0,2},{1,7},{2,4},{3,1},{4,6},{5,3},{6,0},{7,5},{8,10},{9,15},{10,... | collective-permute-start | bytes 3145736 | tf_op jit(solution)/shard_map/ppermute | solution.py:53
  146.7 43.5 %collective-permute-start.7 = (bf16[2,512,512]{1,2,0:T(8,128)(2,1)S(1)}, bf16[2,512,512]{1,2,0:T(8,128)(2,1)S(1)}, u32[]{:S(2)}, u32[]{:S(2)}) collective-permute-start(bf16[2,512,512]{1,2,0:T(8,128)(2,1)S(1)} %collective-permute-done.6), channel_id=1, source_target_pairs={{0,2},{1,7},{2,4},{3,1},{4,6},{5,3},{6,0},{7,5},{8,10},{9,15},{10,... | collective-permute-start | bytes 3145736 | tf_op jit(solution)/shard_map/ppermute | solution.py:54
  183.8 4.9 %copy-start.8 = (bf16[512,8192]{1,0:T(8,128)(2,1)S(1)}, bf16[512,8192]{1,0:T(8,128)(2,1)}, u32[]{:S(2)}) copy-start(bf16[512,8192]{1,0:T(8,128)(2,1)} %all-gather.5.cloned.1.call-done) | copy-start | bytes 25165828
  188.4 3.4 %collective-permute-start.8 = (bf16[2,512,512]{1,2,0:T(8,128)(2,1)S(1)}, bf16[2,512,512]{1,2,0:T(8,128)(2,1)S(1)}, u32[]{:S(2)}, u32[]{:S(2)}) collective-permute-start(bf16[2,512,512]{1,2,0:T(8,128)(2,1)S(1)} %collective-permute-done.6), channel_id=1, source_target_pairs={{0,1},{1,0},{2,3},{3,2},{4,5},{5,4},{6,7},{7,6},{8,9},{9,8},{10,11... | collective-permute-start | bytes 3145736 | tf_op jit(solution)/shard_map/ppermute | solution.py:55
Sparse Core Ops, SparseCore 0:
  10.1 80.7 all-gather.2
  93.6 90.1 all-gather.4

commit v9 on v7

--- a/solution.py
+++ b/solution.py
@@ -18,23 +18,6 @@
         high = lax.ppermute(lax.slice_in_dim(block, 0, width, axis=dim), axis, backward)
         block = jnp.concatenate([low, block, high], axis=dim)
     return block
-
-
-def heads_gather(block, axis):
-    count = lax.axis_size(axis)
-    index = lax.axis_index(axis)
-    gathered = block[None]
-    bit = 1
-    while bit < count:
-        other = lax.ppermute(gathered, axis, [(i, i ^ bit) for i in range(count)])
-        upper = (index & bit) != 0
-        gathered = jnp.where(
-            upper,
-            jnp.concatenate([other, gathered], axis=0),
-            jnp.concatenate([gathered, other], axis=0),
-        )
-        bit *= 2
-    return gathered
 
 
 def heads_ring_gather(block, axis):
@@ -76,7 +59,7 @@
     return (raised / jnp.sum(raised, axis=-1, keepdims=True)).astype(jnp.bfloat16)
 
 
-def shards(
+def layer_body(
     audio,
     ln_gain,
     ln_shift,
@@ -198,22 +181,37 @@
     set_rows = dec_wo.shape[0]
     block_cols = dec_wo.shape[1]
     flat = [(c, j) for c in range(seq_count) for j in range(head_count)]
-    regroup = [
+    half_k = set_rows // ratio
+    regroup_same = [
         (c * head_count + j, (ratio * j + c % ratio) * head_count + c // ratio) for c, j in flat
     ]
-    piece = lax.ppermute(dec_wo, ("seq", "heads"), regroup)
+    regroup_other = [
+        (c * head_count + j, (ratio * j + 1 - c % ratio) * head_count + c // ratio)
+        for c, j in flat
+    ]
+    own_parity = lax.axis_index("seq") % ratio
+    block_parity = lax.axis_index("seq") % ratio
+    same_rows = lax.dynamic_slice_in_dim(dec_wo, block_parity * half_k, half_k, 0)
+    other_rows = lax.dynamic_slice_in_dim(dec_wo, (1 - block_parity) * half_k, half_k, 0)
+    same_piece = lax.ppermute(same_rows, ("seq", "heads"), regroup_same)
+    other_piece = lax.ppermute(other_rows, ("seq", "heads"), regroup_other)
+    first_piece = jnp.where(own_parity == 0, same_piece, other_piece)
+    second_piece = jnp.where(own_parity == 0, other_piece, same_piece)
+    first_weight = lax.all_gather(first_piece, "seq", axis=0, tiled=True)
+    second_weight = lax.all_gather(second_piece, "seq", axis=0, tiled=True)
     pieces, owners = heads_ring_gather(dec_context, "heads")
-    set_cols = ratio * block_cols
-    column_weight = lax.all_gather(piece, "seq", axis=1, tiled=True)
-    total = jnp.zeros((rows_dev, set_cols), jnp.float32)
-    for held, owner in zip(pieces, owners):
-        for offset in range(held.shape[0]):
-            weight_set = lax.dynamic_slice_in_dim(
-                column_weight, (owner * held.shape[0] + offset) * set_cols, set_cols, 1
-            )
-            term = jnp.dot(held[offset], weight_set, preferred_element_type=jnp.float32)
-            total = total + term.astype(jnp.bfloat16).astype(jnp.float32)
-    summed = total
+    outputs = []
+    for column_weight in (first_weight, second_weight):
+        total = jnp.zeros((rows_dev, block_cols), jnp.float32)
+        for held, owner in zip(pieces, owners):
+            for offset in range(held.shape[0]):
+                weight_set = lax.dynamic_slice_in_dim(
+                    column_weight, (owner * held.shape[0] + offset) * set_rows, set_rows, 0
+                )
+                term = jnp.dot(held[offset], weight_set, preferred_element_type=jnp.float32)
+                total = total + term.astype(jnp.bfloat16).astype(jnp.float32)
+        outputs.append(total)
+    summed = jnp.concatenate(outputs, axis=1)
     col_share = model_width // head_count
     own_text = lax.dynamic_slice_in_dim(text, head_index * col_share, col_share, 1)
     dec_out = (own_text.astype(jnp.float32) + summed).astype(jnp.bfloat16)
@@ -222,7 +220,7 @@
 
 def solution(mesh):
     return jax.shard_map(
-        shards,
+        layer_body,
         mesh=mesh,
         in_specs=(
             P("seq", None),

time: 195 us -> 234 us (1.20)
  waiting for transfers between devices: 92.9 us -> 122 us
  starting transfers between devices: 25.3 us -> 34.1 us
  local copies, waits for them, and re-layouts: 10.1 us -> 15 us
    all_gather x2 -> x3, waiting for transfers between devices: 29.8 us -> 74.1 us  [the longest x1 51.7 us: layer_body(): second_weight = lax.all_gather(second_piece, 'seq', axis=0, tiled=True)]
    ppermute x1, waiting for transfers between devices: 15.6 us -> 0.01 us  [heads_ring_gather(): near = lax.ppermute(own, axis, step)]
    ppermute x1, waiting for transfers between devices: 0.01 us -> 8.26 us  [heads_ring_gather(): far = lax.ppermute(near, axis, step)]
    ppermute x1 -> x2, waiting for transfers between devices: 27.9 us -> 23.1 us  [the longest x1 23.1 us: layer_body(): same_piece = lax.ppermute(same_rows, ('seq', 'heads'), regroup_same)]
    ppermute x1 -> x2, starting transfers between devices: 3.56 us -> 8.26 us  [the longest x1 4.7 us: layer_body(): other_piece = lax.ppermute(other_rows, ('seq', 'heads'), regroup_other)]
    ppermute x2, starting transfers between devices: 6.46 us -> 10.8 us  [with_halo(): lax.ppermute(lax.slice_in_dim(block, 0, width, axis=dim), axis, backward)]
    ppermute x2, waiting for transfers between devices: 4.14 us -> 0.95 us  [with_halo(): lax.ppermute(lax.slice_in_dim(block, block.shape[dim] - width, None, axis...]
    unnamed x27 -> x47, local copies, waits for them, and re-layouts: 9.16 us -> 11.7 us
  transfers between devices with their start and end apart: 13 -> 15, of which waited for: 8 -> 9; matrix products, arithmetic and copies ran while one was open for 28% -> 23% of each run, Pallas kernels for 0% -> 0%
where the time goes in v9:
time: 234 us; the launch traced here: 232 us
  waiting for transfers between devices  122 us (52%)
  starting transfers between devices  34.1 us (15%)
  matrix products  33.6 us (14%)
  local copies, waits for them, and re-layouts  15 us (6%)
  between operations  14.5 us (6%)
  other arithmetic  12.4 us (5%)
    all_gather x1, waiting for transfers between devices, layer_body(): second_weight = lax.all_gather(second_piece, 'seq', axis=0, tiled=True)  51.7 us
    ppermute x1, waiting for transfers between devices, layer_body(): same_piece = lax.ppermute(same_rows, ('seq', 'heads'), regroup_same)  23.1 us
    all_gather x1, waiting for transfers between devices, layer_body(): first_weight = lax.all_gather(first_piece, 'seq', axis=0, tiled=True)  22.4 us
    dot_general x16, matrix products, layer_body(): term = jnp.dot(held[offset], weight_set, preferred_element_type=jnp.float32)  12.3 us
    unnamed x47, local copies, waits for them, and re-layouts  11.7 us
    ppermute x2, starting transfers between devices, with_halo(): lax.ppermute(lax.slice_in_dim(block, 0, width, axis=dim), axis, backward)  10.8 us
    dot_general x1, matrix products, layer_body(): jnp.dot(normed, lax.all_gather(dec_wq, 'seq', axis=0, tiled=True), prefer...  10.7 us
    ppermute x1, waiting for transfers between devices, heads_ring_gather(): far = lax.ppermute(near, axis, step)  8.26 us
  transfers between devices with their start and end apart: 15, of which 9 were waited for; matrix products, arithmetic and copies ran while one was open for 23% of the time, Pallas kernels for 0%

profile of v9, /device:TPU:96, one launch (start us, length us, event | category | flops | bytes accessed | tf_op | source)
XLA Modules:
  0.0 232.0 jit_solution(1533821247629731193)
XLA Ops:
  9.1 3.6 %collective-permute-start.5 = (bf16[256,512]{1,0:T(8,128)(2,1)S(1)}, bf16[256,512]{1,0:T(8,128)(2,1)S(1)}, u32[]{:S(2)}, u32[]{:S(2)}) collective-permute-start(bf16[256,512]{1,0:T(8,128)(2,1)S(1)} %get-tuple-element.10), channel_id=1, source_target_pairs={{0,0},{1,16},{2,32},{3,48},{4,64},{5,80},{6,96},{7,112},{8,8},{9,2... | collective-permute-start | bytes 786440 | tf_op jit(solution)/shard_map/ppermute | solution.py:196
  12.7 4.7 %collective-permute-start.6 = (bf16[256,512]{1,0:T(8,128)(2,1)S(1)}, bf16[256,512]{1,0:T(8,128)(2,1)S(1)}, u32[]{:S(2)}, u32[]{:S(2)}) collective-permute-start(bf16[256,512]{1,0:T(8,128)(2,1)S(1)} %get-tuple-element.11), channel_id=1, source_target_pairs={{0,8},{1,24},{2,40},{3,56},{4,72},{5,88},{6,104},{7,120},{8,0},{9,... | collective-permute-start | bytes 786440 | tf_op jit(solution)/shard_map/ppermute | solution.py:197
  17.4 23.1 %collective-permute-done.5 = bf16[256,512]{1,0:T(8,128)(2,1)S(1)} collective-permute-done((bf16[256,512]{1,0:T(8,128)(2,1)S(1)}, bf16[256,512]{1,0:T(8,128)(2,1)S(1)}, u32[]{:S(2)}, u32[]{:S(2)}) %collective-permute-start.5) | collective-permute-done | bytes 262176 | tf_op jit(solution)/shard_map/ppermute | solution.py:196
  41.4 1.3 convert_reduce_fusion
  42.6 1.4 fusion.26
  45.1 3.4 %collective-permute-start = (bf16[128,2,128]{2,0,1:T(8,128)(2,1)S(1)}, bf16[128,2,128]{2,0,1:T(8,128)(2,1)S(1)}, u32[]{:S(2)}, u32[]{:S(2)}) collective-permute-start(bf16[128,2,128]{2,0,1:T(8,128)(2,1)S(1)} %get-tuple-element.14), channel_id=1, source_target_pairs={{0,8},{8,16},{16,24},{24,32},{32,40},{40,48},{48,56},{56,64},{64,7... | collective-permute-start | bytes 196616 | tf_op jit(solution)/shard_map/ppermute | solution.py:15
  48.5 4.6 %collective-permute-start.1 = (bf16[128,2,128]{2,0,1:T(8,128)(2,1)S(1)}, bf16[128,2,128]{2,0,1:T(8,128)(2,1)S(1)}, u32[]{:S(2)}, u32[]{:S(2)}) collective-permute-start(bf16[128,2,128]{2,0,1:T(8,128)(2,1)S(1)} %get-tuple-element.15), channel_id=1, source_target_pairs={{8,0},{16,8},{24,16},{32,24},{40,32},{48,40},{56,48},{64,56},{72,6... | collective-permute-start | bytes 196616 | tf_op jit(solution)/shard_map/ppermute | solution.py:18
  53.2 7.2 %copy.52 = bf16[160,8,8,256]{3,1,2,0:T(8,128)(2,1)} copy(bf16[160,8,8,256]{3,2,1,0:T(8,128)(2,1)} %bitcast.116) | data formatting | bytes 10485760
  64.8 3.5 %all-to-all-start = ((bf16[8,32,1280]{2,1,0:T(8,128)(2,1)}), bf16[8,32,1280]{2,1,0:T(8,128)(2,1)S(1)}, u32[]{:S(2)}, u32[]{:S(2)}) async-start(bf16[8,32,1280]{2,1,0:T(8,128)(2,1)} %bitcast.7), calls=%async_computation | async-start | bytes 1310720 | tf_op jit(solution)/shard_map/all_to_all | solution.py:123
  68.3 5.3 %fusion.1 = f32[512]{0:T(512)S(1)} fusion(bf16[512,8192]{1,0:T(8,128)(2,1)} %param.33), kind=kLoop, calls=%fused_computation.3 | loop fusion | flops 12582400 | bytes 8390656 | tf_op jit(solution)/shard_map/reduce_sum | solution.py:53
  73.6 6.3 %all-to-all-done = bf16[8,32,1280]{2,1,0:T(8,128)(2,1)S(1)} async-done(((bf16[8,32,1280]{2,1,0:T(8,128)(2,1)}), bf16[8,32,1280]{2,1,0:T(8,128)(2,1)S(1)}, u32[]{:S(2)}, u32[]{:S(2)}) %all-to-all-start) | async-done | bytes 655392 | tf_op jit(solution)/shard_map/all_to_all | solution.py:123
  80.1 3.7 %fusion.14 = bf16[32,2048]{1,0:T(8,128)(2,1)S(1)} fusion(bf16[32,1280]{1,0:T(8,128)(2,1)S(1)} %add_convert_fusion, bf16[1280,2048]{1,0:T(8,128)(2,1)} %bitcast.115, f32[2048]{0:T(1024)S(1)} %bitcast.129), kind=kOutput, calls=%fused_computation.20 | convolution fusion | flops 167903232 | bytes 5464064 | tf_op jit(solution)/shard_map/dot_general | solution.py:140
  84.5 3.4 %all-to-all-start.1 = ((bf16[32,8,256]{2,0,1:T(8,128)(2,1)}), bf16[32,8,256]{2,0,1:T(8,128)(2,1)S(1)}, u32[]{:S(2)}, u32[]{:S(2)}) async-start(bf16[32,8,256]{2,0,1:T(8,128)(2,1)} %bitcast.114), calls=%async_computation.1 | async-start | bytes 262144 | tf_op jit(solution)/shard_map/all_to_all | solution.py:147
  88.2 5.6 %all-to-all-done.1 = bf16[32,8,256]{2,0,1:T(8,128)(2,1)S(1)} async-done(((bf16[32,8,256]{2,0,1:T(8,128)(2,1)}), bf16[32,8,256]{2,0,1:T(8,128)(2,1)S(1)}, u32[]{:S(2)}, u32[]{:S(2)}) %all-to-all-start.1) | async-done | bytes 131104 | tf_op jit(solution)/shard_map/all_to_all | solution.py:147
  93.9 1.9 collective-permute-start.2
  95.8 6.2 %collective-permute-start.3 = (bf16[256,1,256]{2,0,1:T(8,128)(2,1)S(1)}, bf16[256,1,256]{2,0,1:T(8,128)(2,1)S(1)}, u32[]{:S(2)}, u32[]{:S(2)}) collective-permute-start(bf16[256,1,256]{2,0,1:T(8,128)(2,1)S(1)} %bitcast.124), channel_id=1, source_target_pairs={{8,0},{16,8},{24,16},{32,24},{40,32},{48,40},{56,48},{64,56},{72,6... | collective-permute-start | bytes 393224 | tf_op jit(solution)/shard_map/ppermute | solution.py:18
  103.0 1.4 collective-permute-done.3
  104.4 10.7 %fusion.66 = bf16[512,512]{0,1:T(8,128)(2,1)S(1)} fusion(bf16[8192,512]{1,0:T(8,128)(2,1)} %all-gather.4.cloned.1.call-done, bf16[512,8192]{1,0:T(8,128)(2,1)} %param.33, f32[8192]{0:T(1024)S(1)} %copy-done.18, f32[512]{0:T(512)S(1)} %add_rsqrt_fusion, f32[512]{0:T(512)S(1)} %copy-done.19), kind=kOutput, calls=%fused_computation.87 | convolution fusion | flops 4312268800 | bytes 17338368 | tf_op jit(solution)/shard_map/dot_general | solution.py:155
  116.3 1.4 fusion.11
  117.6 2.1 fusion.33
  119.8 1.9 collective-permute-done.4
  122.7 1.3 constant_dynamic-slice_fusion.2
  124.0 1.3 copy.50
  125.3 22.4 %all-gather.6.cloned.1.call-done = bf16[4096,512]{1,0:T(8,128)(2,1)} async-done(((bf16[256,512]{1,0:T(8,128)(2,1)}), bf16[4096,512]{1,0:T(8,128)(2,1)}) %all-gather.6.cloned.1.call-update) | async-done | bytes 4194320 | tf_op jit(solution)/shard_map/all_gather | solution.py:200
  147.7 1.5 fusion.40
  149.2 51.7 %all-gather.8.cloned.1.call-done = bf16[4096,512]{1,0:T(8,128)(2,1)} async-done(((bf16[256,512]{1,0:T(8,128)(2,1)}), bf16[4096,512]{1,0:T(8,128)(2,1)}) %all-gather.8.cloned.1.call-update) | async-done | bytes 4194320 | tf_op jit(solution)/shard_map/all_gather | solution.py:201
  201.0 1.7 fusion.55
  202.7 1.8 collective-permute-start.8
  204.5 1.5 fusion.41
  206.0 1.5 fusion.56
  210.8 8.3 %collective-permute-done.8 = bf16[2,512,512]{1,2,0:T(8,128)(2,1)S(1)} collective-permute-done((bf16[2,512,512]{1,2,0:T(8,128)(2,1)S(1)}, bf16[2,512,512]{1,2,0:T(8,128)(2,1)S(1)}, u32[]{:S(2)}, u32[]{:S(2)}) %collective-permute-start.8) | collective-permute-done | bytes 1048608 | tf_op jit(solution)/shard_map/ppermute | solution.py:37
  224.2 1.3 copy.45
  (104 shorter events, 20.7 us)
Async XLA Ops:
  7.2 56.4 %copy-start = (bf16[128,1280]{1,0:T(8,128)(2,1)S(1)}, bf16[128,1280]{1,0:T(8,128)(2,1)}, u32[]{:S(2)}) copy-start(bf16[128,1280]{1,0:T(8,128)(2,1)} %param.28) | copy-start | bytes 983044
  7.2 36.9 %copy-start.2 = (bf16[256,1280]{1,0:T(8,128)(2,1)S(1)}, bf16[256,1280]{1,0:T(8,128)(2,1)}, u32[]{:S(2)}) copy-start(bf16[256,1280]{1,0:T(8,128)(2,1)} %param.20) | copy-start | bytes 1966084
  7.2 36.9 %copy-start.13 = (f32[1280]{0:T(1024)S(1)}, f32[1280]{0:T(1024)}, u32[]{:S(2)}) copy-start(f32[1280]{0:T(1024)} %param.21) | copy-start | bytes 15364
  7.2 36.9 %copy-start.12 = (f32[1280]{0:T(1024)S(1)}, f32[1280]{0:T(1024)}, u32[]{:S(2)}) copy-start(f32[1280]{0:T(1024)} %param.22) | copy-start | bytes 15364
  7.2 37.2 %copy-start.6 = (bf16[1280,128]{1,0:T(8,128)(2,1)S(1)}, bf16[1280,128]{1,0:T(8,128)(2,1)}, u32[]{:S(2)}) copy-start(bf16[1280,128]{1,0:T(8,128)(2,1)} %param.25) | copy-start | bytes 983044
  7.2 37.5 %copy-start.7 = (bf16[1280,128]{1,0:T(8,128)(2,1)S(1)}, bf16[1280,128]{1,0:T(8,128)(2,1)}, u32[]{:S(2)}) copy-start(bf16[1280,128]{1,0:T(8,128)(2,1)} %param.26) | copy-start | bytes 983044
  7.2 37.5 %copy-start.16 = (f32[128]{0:T(128)S(1)}, f32[128]{0:T(128)}, u32[]{:S(2)}) copy-start(f32[128]{0:T(128)} %param.27) | copy-start | bytes 1540
  7.2 97.1 %all-gather.4.cloned.1.call-start = ((), (), s32[]{:S(2)}) async-start(), calls=%async_computation.2 | async-start | bytes 8912896 | tf_op jit(solution)/shard_map/all_gather | solution.py:157
  8.0 139.7 %all-gather.6.cloned.1.call-start = ((), (), s32[]{:S(2)}) async-start(), calls=%async_computation.3 | async-start | bytes 4456448 | tf_op jit(solution)/shard_map/all_gather | solution.py:200
  9.1 31.3 %collective-permute-start.5 = (bf16[256,512]{1,0:T(8,128)(2,1)S(1)}, bf16[256,512]{1,0:T(8,128)(2,1)S(1)}, u32[]{:S(2)}, u32[]{:S(2)}) collective-permute-start(bf16[256,512]{1,0:T(8,128)(2,1)S(1)} %get-tuple-element.10), channel_id=1, source_target_pairs={{0,0},{1,16},{2,32},{3,48},{4,64},{5,80},{6,96},{7,112},{8,8},{9,2... | collective-permute-start | bytes 786440 | tf_op jit(solution)/shard_map/ppermute | solution.py:196
  12.7 27.8 %collective-permute-start.6 = (bf16[256,512]{1,0:T(8,128)(2,1)S(1)}, bf16[256,512]{1,0:T(8,128)(2,1)S(1)}, u32[]{:S(2)}, u32[]{:S(2)}) collective-permute-start(bf16[256,512]{1,0:T(8,128)(2,1)S(1)} %get-tuple-element.11), channel_id=1, source_target_pairs={{0,8},{1,24},{2,40},{3,56},{4,72},{5,88},{6,104},{7,120},{8,0},{9,... | collective-permute-start | bytes 786440 | tf_op jit(solution)/shard_map/ppermute | solution.py:197
  41.3 159.6 %all-gather.8.cloned.1.call-start = ((), (), s32[]{:S(2)}) async-start(), calls=%async_computation.4 | async-start | bytes 4456448 | tf_op jit(solution)/shard_map/all_gather | solution.py:201
  45.1 15.9 %collective-permute-start = (bf16[128,2,128]{2,0,1:T(8,128)(2,1)S(1)}, bf16[128,2,128]{2,0,1:T(8,128)(2,1)S(1)}, u32[]{:S(2)}, u32[]{:S(2)}) collective-permute-start(bf16[128,2,128]{2,0,1:T(8,128)(2,1)S(1)} %get-tuple-element.14), channel_id=1, source_target_pairs={{0,8},{8,16},{16,24},{24,32},{32,40},{40,48},{48,56},{56,64},{64,7... | collective-permute-start | bytes 196616 | tf_op jit(solution)/shard_map/ppermute | solution.py:15
  48.5 12.5 %collective-permute-start.1 = (bf16[128,2,128]{2,0,1:T(8,128)(2,1)S(1)}, bf16[128,2,128]{2,0,1:T(8,128)(2,1)S(1)}, u32[]{:S(2)}, u32[]{:S(2)}) collective-permute-start(bf16[128,2,128]{2,0,1:T(8,128)(2,1)S(1)} %get-tuple-element.15), channel_id=1, source_target_pairs={{8,0},{16,8},{24,16},{32,24},{40,32},{48,40},{56,48},{64,56},{72,6... | collective-permute-start | bytes 196616 | tf_op jit(solution)/shard_map/ppermute | solution.py:18
  53.1 7.3 %copy-start.14 = (f32[8,128]{1,0:T(8,128)S(1)}, f32[8,128]{1,0:T(8,128)}, u32[]{:S(2)}) copy-start(f32[8,128]{1,0:T(8,128)} %param.32) | copy-start | bytes 12292
  53.1 7.3 %copy-start.10 = (s32[512]{0:T(512)S(1)}, s32[512]{0:T(512)}, u32[]{:S(2)}) copy-start(s32[512]{0:T(512)} %param.38) | copy-start | bytes 6148
  53.1 7.3 %copy-start.15 = (s32[512]{0:T(512)S(1)}, s32[512]{0:T(512)}, u32[]{:S(2)}) copy-start(s32[512]{0:T(512)} %param.39) | copy-start | bytes 6148
  53.1 7.5 %copy-start.8 = (bf16[1280,128]{1,0:T(8,128)(2,1)S(1)}, bf16[1280,128]{1,0:T(8,128)(2,1)}, u32[]{:S(2)}) copy-start(bf16[1280,128]{1,0:T(8,128)(2,1)} %param.23) | copy-start | bytes 983044
  53.1 7.5 %copy-start.17 = (f32[128]{0:T(128)S(1)}, f32[128]{0:T(128)}, u32[]{:S(2)}) copy-start(f32[128]{0:T(128)} %param.24) | copy-start | bytes 1540
  64.8 15.2 %all-to-all-start = ((bf16[8,32,1280]{2,1,0:T(8,128)(2,1)}), bf16[8,32,1280]{2,1,0:T(8,128)(2,1)S(1)}, u32[]{:S(2)}, u32[]{:S(2)}) async-start(bf16[8,32,1280]{2,1,0:T(8,128)(2,1)} %bitcast.7), calls=%async_computation | async-start | bytes 1310720 | tf_op jit(solution)/shard_map/all_to_all | solution.py:123
  68.3 11.7 %copy-start.11 = (f32[1280]{0:T(1024)S(1)}, f32[1280]{0:T(1024)}, u32[]{:S(2)}) copy-start(f32[1280]{0:T(1024)} %param.29) | copy-start | bytes 15364
  73.6 30.8 %copy-start.18 = (f32[8192]{0:T(1024)S(1)}, f32[8192]{0:T(1024)}, u32[]{:S(2)}) copy-start(f32[8192]{0:T(1024)} %param.34) | copy-start | bytes 98308
  73.6 30.8 %copy-start.19 = (f32[512]{0:T(512)S(1)}, f32[512]{0:T(512)}, u32[]{:S(2)}) copy-start(f32[512]{0:T(512)} %param.36) | copy-start | bytes 6148
  80.1 35.0 %copy-start.9 = (bf16[32,1280]{1,0:T(8,128)(2,1)}, bf16[32,1280]{1,0:T(8,128)(2,1)S(1)}, u32[]{:S(2)}) copy-start(bf16[32,1280]{1,0:T(8,128)(2,1)S(1)} %add_convert_fusion) | copy-start | bytes 245764
  84.5 9.4 %all-to-all-start.1 = ((bf16[32,8,256]{2,0,1:T(8,128)(2,1)}), bf16[32,8,256]{2,0,1:T(8,128)(2,1)S(1)}, u32[]{:S(2)}, u32[]{:S(2)}) async-start(bf16[32,8,256]{2,0,1:T(8,128)(2,1)} %bitcast.114), calls=%async_computation.1 | async-start | bytes 262144 | tf_op jit(solution)/shard_map/all_to_all | solution.py:147
  93.9 9.1 %collective-permute-start.2 = (bf16[256,1,256]{2,0,1:T(8,128)(2,1)S(1)}, bf16[256,1,256]{2,0,1:T(8,128)(2,1)S(1)}, u32[]{:S(2)}, u32[]{:S(2)}) collective-permute-start(bf16[256,1,256]{2,0,1:T(8,128)(2,1)S(1)} %bitcast.123), channel_id=1, source_target_pairs={{0,8},{8,16},{16,24},{24,32},{32,40},{40,48},{48,56},{56,64},{64,7... | collective-permute-start | bytes 393224 | tf_op jit(solution)/shard_map/ppermute | solution.py:15
  95.8 8.5 %collective-permute-start.3 = (bf16[256,1,256]{2,0,1:T(8,128)(2,1)S(1)}, bf16[256,1,256]{2,0,1:T(8,128)(2,1)S(1)}, u32[]{:S(2)}, u32[]{:S(2)}) collective-permute-start(bf16[256,1,256]{2,0,1:T(8,128)(2,1)S(1)} %bitcast.124), channel_id=1, source_target_pairs={{8,0},{16,8},{24,16},{32,24},{40,32},{48,40},{56,48},{64,56},{72,6... | collective-permute-start | bytes 393224 | tf_op jit(solution)/shard_map/ppermute | solution.py:18
  119.7 2.0 collective-permute-start.4
  121.9 80.7 %collective-permute-start.7 = (bf16[2,512,512]{1,2,0:T(8,128)(2,1)S(1)}, bf16[2,512,512]{1,2,0:T(8,128)(2,1)S(1)}, u32[]{:S(2)}, u32[]{:S(2)}) collective-permute-start(bf16[2,512,512]{1,2,0:T(8,128)(2,1)S(1)} %maximum_select_fusion), channel_id=1, source_target_pairs={{0,2},{1,7},{2,4},{3,1},{4,6},{5,3},{6,0},{7,5},{8,10},{9,15},{10,... | collective-permute-start | bytes 3145736 | tf_op jit(solution)/shard_map/ppermute | solution.py:36
  201.0 6.6 %copy-start.3 = (bf16[4096,512]{1,0:T(8,128)(2,1)S(1)}, bf16[4096,512]{1,0:T(8,128)(2,1)}, u32[]{:S(2)}) copy-start(bf16[4096,512]{1,0:T(8,128)(2,1)} %all-gather.6.cloned.1.call-done) | copy-start | bytes 12582916
  202.6 17.4 %collective-permute-start.9 = (bf16[2,512,512]{1,2,0:T(8,128)(2,1)S(1)}, bf16[2,512,512]{1,2,0:T(8,128)(2,1)S(1)}, u32[]{:S(2)}, u32[]{:S(2)}) collective-permute-start(bf16[2,512,512]{1,2,0:T(8,128)(2,1)S(1)} %collective-permute-done.7), channel_id=1, source_target_pairs={{0,1},{1,0},{2,3},{3,2},{4,5},{5,4},{6,7},{7,6},{8,9},{9,8},{10,11... | collective-permute-start | bytes 3145736 | tf_op jit(solution)/shard_map/ppermute | solution.py:38
  202.7 16.3 %collective-permute-start.8 = (bf16[2,512,512]{1,2,0:T(8,128)(2,1)S(1)}, bf16[2,512,512]{1,2,0:T(8,128)(2,1)S(1)}, u32[]{:S(2)}, u32[]{:S(2)}) collective-permute-start(bf16[2,512,512]{1,2,0:T(8,128)(2,1)S(1)} %collective-permute-done.7), channel_id=1, source_target_pairs={{0,2},{1,7},{2,4},{3,1},{4,6},{5,3},{6,0},{7,5},{8,10},{9,15},{10,... | collective-permute-start | bytes 3145736 | tf_op jit(solution)/shard_map/ppermute | solution.py:37
  (4 other events, 7.7 us)
Sparse Core Ops, SparseCore 0:
  10.2 83.9 all-gather.3
  96.3 51.3 all-gather.5
  149.9 51.0 all-gather.7
